TPU v7x, 512 devices: a whole 4x8x8 slice. The times are simulated.
512 devices in a mesh: seq: 64 (over z_hi, y, core), tp: 8 (over x, z_lo).
Axes of the slice: x: 4, y: 8, z: 8 (z_hi: 4, z_lo: 2; z = z_hi * 2 + z_lo), core: 2. Of those that a mesh axis runs over, the one named last changes fastest.
Arguments:
- query_proj: bfloat16 [16384, 3072], P('seq', 'tp'), may hold values from -8 to 8
- key_proj: bfloat16 [16384, 3072], P('seq', 'tp'), may hold values from -8 to 8
- value_proj: bfloat16 [16384, 3072], P('seq', 'tp'), may hold values from -6 to 6
- hidden: bfloat16 [16384, 3072], P('seq', 'tp'), may hold values from -2 to 2
- out_weight: bfloat16 [3072, 3072], P('tp'), may hold values from -0.109375 to 0.109375
- norm_gain: bfloat16 [3072], P('tp'), may hold values from 0.099609375 to 1.8984375
- segment_ids: int32 [16384], P('seq'), may hold values from 0 to 31, never falling along the last dimension, each value on 1 to 8192 neighbouring positions
- pad_mask: int32 [16384], P('seq'), may hold values 0 or 1
- page_table: int32 [128], P('seq'), may hold values from 0 to 1, as said below
Outputs:
- hidden_out: bfloat16 [16384, 3072], P('seq', 'tp')
- normed: bfloat16 [16384, 3072], P('seq', 'tp')
- kv_pages: bfloat16 [128, 2, 128, 3072], P('seq', None, None, 'tp')
Inputs may be any that keep to these rules, and one draw needn't show every extreme that they name: `segment_ids`: never falling along the tokens; each of the 32 prompts has 1 to 8192 tokens, one exactly 8192. `page_table`: the 2 pages of each aligned block of 2 pages name each slot once.
All inputs are finite; a program needn't handle non-finite values. No bound on the sum of `pad_mask` on one device may be relied on, other than what follows from the above.
Results may differ from a plain program's by a relative error of at most 0.014.
Values may be sent and summed in bfloat16 or wider, within the bound.
No kernel may reach another device: no remote copies, remote signals or barrier semaphores. Data moves between devices by JAX's collectives and lax.ppermute only.
A program may use at most 128 MiB of HBM per device.

v0:
```python
import math

import jax
import jax.numpy as jnp
from jax import lax
from jax.sharding import PartitionSpec as P

D = 3072
HEAD_DIM = 96
PAGE = 128


far_index = 1073741824
masked_score = -1e30
norm_epsilon = 1e-05


def passed_along(block, axis, distance):
    devices = range(lax.axis_size(axis))
    route = [(i - distance, i) for i in devices if i - distance in devices]
    return lax.ppermute(block, axis, route)


def rotate(values_in, position, head_count, head_dim):
    count_rows = values_in.shape[0]
    half_dim = head_dim // 2
    frequency = jnp.exp(
        jnp.arange(half_dim, dtype=jnp.float32) * (-2.0 * math.log(10000.0) / head_dim)
    )
    angles = position.astype(jnp.float32)[:, None] * frequency[None, :]
    cosine = jnp.cos(angles)[:, None, :]
    sine_part = jnp.sin(angles)[:, None, :]
    as_float = values_in.astype(jnp.float32).reshape(count_rows, head_count, head_dim)
    lower_half = as_float[..., :half_dim]
    upper_half = as_float[..., half_dim:]
    rotated = jnp.concatenate(
        [
            lower_half * cosine - upper_half * sine_part,
            upper_half * cosine + lower_half * sine_part,
        ],
        axis=-1,
    )
    return rotated.reshape(count_rows, head_count * head_dim).astype(jnp.bfloat16)


def attend(softmax_state, query_heads, block, visible):
    row_peak, row_total, weighted = softmax_state
    key_count = block.shape[1]
    head_count = query_heads.shape[1]
    key_heads = block[0].reshape(key_count, head_count, HEAD_DIM)
    val_heads = block[1].reshape(key_count, head_count, HEAD_DIM)
    factor = 1.0 / math.sqrt(HEAD_DIM)
    logits = (
        jnp.einsum("qhd,khd->hqk", query_heads, key_heads, preferred_element_type=jnp.float32)
        * factor
    )
    logits = jnp.where(visible[None], logits, masked_score)
    new_peak = jnp.maximum(row_peak, jnp.max(logits, axis=-1))
    rescale = jnp.exp(row_peak - new_peak)
    unnormed = jnp.where(visible[None], jnp.exp(logits - new_peak[..., None]), 0.0)
    row_total = row_total * rescale + jnp.sum(unnormed, axis=-1)
    weighted = weighted * rescale[..., None] + jnp.einsum(
        "hqk,khd->hqd", unnormed.astype(jnp.bfloat16), val_heads, preferred_element_type=jnp.float32
    )
    return (new_peak, row_total, weighted)


def per_device(
    query_proj,
    key_proj,
    value_proj,
    hidden,
    out_weight,
    norm_gain,
    segment_ids,
    pad_mask,
    page_table,
):
    tok_count = query_proj.shape[0]
    feat_count = query_proj.shape[1]
    head_count = feat_count // HEAD_DIM
    seg_count = lax.axis_size("seq") // 2
    reach_count = lax.axis_size("seq") // 2
    device_row = lax.axis_index("seq")
    tok_index = device_row * tok_count + jnp.arange(tok_count, dtype=jnp.int32)
    member = segment_ids[:, None] == jnp.arange(seg_count, dtype=jnp.int32)[None, :]
    local_first = jnp.min(jnp.where(member, tok_index[:, None], far_index), axis=0)
    first_tok = lax.pmin(local_first, "seq")
    position = tok_index - jnp.sum(jnp.where(member, first_tok[None, :], 0), axis=1)
    q_rot = rotate(query_proj, position, head_count, HEAD_DIM)
    k_rot = rotate(key_proj, position, head_count, HEAD_DIM)
    query_heads = q_rot.reshape(tok_count, head_count, HEAD_DIM)
    query_tag = segment_ids + 1
    key_tag = jnp.where(pad_mask == 1, segment_ids + 1, 0)
    own_block = jnp.stack([k_rot, value_proj])
    offsets = jnp.arange(tok_count, dtype=jnp.int32)
    own_visible = (key_tag[None, :] == query_tag[:, None]) & (
        offsets[None, :] <= offsets[:, None]
    ) | (offsets[None, :] == offsets[:, None])
    softmax_state = (
        jnp.full((head_count, tok_count), masked_score, jnp.float32),
        jnp.zeros((head_count, tok_count), jnp.float32),
        jnp.zeros((head_count, tok_count, HEAD_DIM), jnp.float32),
    )
    softmax_state = attend(softmax_state, query_heads, own_block, own_visible)

    def visit_block(current, moved, moved_tags):
        visible = moved_tags[None, :] == query_tag[:, None]
        return attend(current, query_heads, moved, visible)

    def cycle_turn(turn_index, loop_state):
        current, moved, moved_tags = loop_state
        moved, moved_tags = passed_along((moved, moved_tags), "seq", 1)
        return (visit_block(current, moved, moved_tags), moved, moved_tags)

    softmax_state = lax.fori_loop(0, reach_count, cycle_turn, (softmax_state, own_block, key_tag))[
        0
    ]
    row_peak, row_total, weighted = softmax_state
    attn = (
        jnp.transpose(weighted / row_total[..., None], (1, 0, 2))
        .reshape(tok_count, feat_count)
        .astype(jnp.bfloat16)
    )
    partial_value = jnp.dot(attn, out_weight, preferred_element_type=jnp.float32)
    feature_width = hidden.shape[1]
    summed = lax.psum(partial_value.astype(jnp.bfloat16), "tp").astype(jnp.float32)
    own_sum = lax.dynamic_slice_in_dim(
        summed, lax.axis_index("tp") * feature_width, feature_width, 1
    )
    hidden_out = (hidden.astype(jnp.float32) + own_sum).astype(jnp.bfloat16)
    stream_wide = hidden_out.astype(jnp.float32)
    square_total = lax.psum(jnp.sum(stream_wide * stream_wide, axis=1), "tp")
    normed = (
        stream_wide
        * lax.rsqrt(square_total / D + norm_epsilon)[:, None]
        * norm_gain.astype(jnp.float32)[None, :]
    ).astype(jnp.bfloat16)
    pad_scale = pad_mask.astype(jnp.bfloat16)[:, None]
    page_count = tok_count // PAGE
    stacked = jnp.stack([k_rot * pad_scale, value_proj * pad_scale])
    stacked = stacked.reshape(2, page_count, PAGE, feat_count).transpose(1, 0, 2, 3)
    kv_pages = jnp.zeros_like(stacked).at[page_table].set(stacked)
    return (hidden_out, normed, kv_pages)


def solution(mesh):
    placed = (
        P("seq", "tp"),
        P("seq", "tp"),
        P("seq", "tp"),
        P("seq", "tp"),
        P("tp", None),
        P("tp"),
        P("seq"),
        P("seq"),
        P("seq"),
    )
    return jax.shard_map(
        per_device,
        mesh=mesh,
        in_specs=placed,
        out_specs=(P("seq", "tp"), P("seq", "tp"), P("seq", None, None, "tp")),
        check_vma=False,
    )
```

profile of v0, /device:TPU:24, one launch (start us, length us, event | category | flops | bytes accessed | tf_op | source)
XLA Modules:
  0.0 713.3 jit_solution(16163749201808365648)
XLA Ops:
  8.2 27.8 %pmin.7 = s32[32]{0:T(128)S(1)} all-reduce(s32[32]{0:T(128)S(1)} %select_reduce_fusion.1), channel_id=1, replica_groups=mesh['seq'=64,'tp'=8] {'seq'}, use_global_device_ids=true, to_apply=%region_1.2 | all-reduce | flops 32 | bytes 256 | tf_op jit(solution)/shard_map/pmin | solution.py:88
  44.6 480.4 %while.18 = (s32[]{:T(128)}, f32[4,256]{1,0:T(4,128)S(1)}, f32[4,256]{1,0:T(4,128)S(1)}, f32[4,256,96]{1,2,0:T(8,128)S(1)}, bf16[2,256,384]{1,2,0:T(8,128)(2,1)}...) while((s32[]{:T(128)}, f32[4,256]{1,0:T(4,128)S(1)}, ...), condition=%wide.region_8.9_spmd, body=%wide.region_5.8_spmd.sunk | while | flops 103286784 | bytes 8003757 | solution.py:116
  148.3 10.9 %collective-permute-start.1 = (s32[256]{0:T(256)}, s32[256]{0:T(256)S(1)}, u32[]{:S(2)}, u32[]{:S(2)}) collective-permute-start(s32[256]{0:T(256)} %get-tuple-element.160), channel_id=1, source_target_pairs={{0,8},{8,16},{16,24},{24,32},{32,40},{40,48},{48,56},{56,64},{64,7... | collective-permute-start | bytes 3080 | tf_op jit(solution)/shard_map/while/body/eval_jaxpr/ppermute | solution.py:21
  166.8 11.2 %collective-permute-start.1 = (s32[256]{0:T(256)}, s32[256]{0:T(256)S(1)}, u32[]{:S(2)}, u32[]{:S(2)}) collective-permute-start(s32[256]{0:T(256)} %get-tuple-element.160), channel_id=1, source_target_pairs={{0,8},{8,16},{16,24},{24,32},{32,40},{40,48},{48,56},{56,64},{64,7... | collective-permute-start | bytes 3080 | tf_op jit(solution)/shard_map/while/body/eval_jaxpr/ppermute | solution.py:21
  185.5 10.6 %collective-permute-start.1 = (s32[256]{0:T(256)}, s32[256]{0:T(256)S(1)}, u32[]{:S(2)}, u32[]{:S(2)}) collective-permute-start(s32[256]{0:T(256)} %get-tuple-element.160), channel_id=1, source_target_pairs={{0,8},{8,16},{16,24},{24,32},{32,40},{40,48},{48,56},{56,64},{64,7... | collective-permute-start | bytes 3080 | tf_op jit(solution)/shard_map/while/body/eval_jaxpr/ppermute | solution.py:21
  203.6 9.2 %collective-permute-start.1 = (s32[256]{0:T(256)}, s32[256]{0:T(256)S(1)}, u32[]{:S(2)}, u32[]{:S(2)}) collective-permute-start(s32[256]{0:T(256)} %get-tuple-element.160), channel_id=1, source_target_pairs={{0,8},{8,16},{16,24},{24,32},{32,40},{40,48},{48,56},{56,64},{64,7... | collective-permute-start | bytes 3080 | tf_op jit(solution)/shard_map/while/body/eval_jaxpr/ppermute | solution.py:21
  279.9 7.8 %collective-permute-start.1 = (s32[256]{0:T(256)}, s32[256]{0:T(256)S(1)}, u32[]{:S(2)}, u32[]{:S(2)}) collective-permute-start(s32[256]{0:T(256)} %get-tuple-element.160), channel_id=1, source_target_pairs={{0,8},{8,16},{16,24},{24,32},{32,40},{40,48},{48,56},{56,64},{64,7... | collective-permute-start | bytes 3080 | tf_op jit(solution)/shard_map/while/body/eval_jaxpr/ppermute | solution.py:21
  295.5 7.8 %collective-permute-start.1 = (s32[256]{0:T(256)}, s32[256]{0:T(256)S(1)}, u32[]{:S(2)}, u32[]{:S(2)}) collective-permute-start(s32[256]{0:T(256)} %get-tuple-element.160), channel_id=1, source_target_pairs={{0,8},{8,16},{16,24},{24,32},{32,40},{40,48},{48,56},{56,64},{64,7... | collective-permute-start | bytes 3080 | tf_op jit(solution)/shard_map/while/body/eval_jaxpr/ppermute | solution.py:21
  311.1 7.8 %collective-permute-start.1 = (s32[256]{0:T(256)}, s32[256]{0:T(256)S(1)}, u32[]{:S(2)}, u32[]{:S(2)}) collective-permute-start(s32[256]{0:T(256)} %get-tuple-element.160), channel_id=1, source_target_pairs={{0,8},{8,16},{16,24},{24,32},{32,40},{40,48},{48,56},{56,64},{64,7... | collective-permute-start | bytes 3080 | tf_op jit(solution)/shard_map/while/body/eval_jaxpr/ppermute | solution.py:21
  326.7 7.8 %collective-permute-start.1 = (s32[256]{0:T(256)}, s32[256]{0:T(256)S(1)}, u32[]{:S(2)}, u32[]{:S(2)}) collective-permute-start(s32[256]{0:T(256)} %get-tuple-element.160), channel_id=1, source_target_pairs={{0,8},{8,16},{16,24},{24,32},{32,40},{40,48},{48,56},{56,64},{64,7... | collective-permute-start | bytes 3080 | tf_op jit(solution)/shard_map/while/body/eval_jaxpr/ppermute | solution.py:21
  342.2 7.8 %collective-permute-start.1 = (s32[256]{0:T(256)}, s32[256]{0:T(256)S(1)}, u32[]{:S(2)}, u32[]{:S(2)}) collective-permute-start(s32[256]{0:T(256)} %get-tuple-element.160), channel_id=1, source_target_pairs={{0,8},{8,16},{16,24},{24,32},{32,40},{40,48},{48,56},{56,64},{64,7... | collective-permute-start | bytes 3080 | tf_op jit(solution)/shard_map/while/body/eval_jaxpr/ppermute | solution.py:21
  357.8 7.8 %collective-permute-start.1 = (s32[256]{0:T(256)}, s32[256]{0:T(256)S(1)}, u32[]{:S(2)}, u32[]{:S(2)}) collective-permute-start(s32[256]{0:T(256)} %get-tuple-element.160), channel_id=1, source_target_pairs={{0,8},{8,16},{16,24},{24,32},{32,40},{40,48},{48,56},{56,64},{64,7... | collective-permute-start | bytes 3080 | tf_op jit(solution)/shard_map/while/body/eval_jaxpr/ppermute | solution.py:21
  373.4 7.8 %collective-permute-start.1 = (s32[256]{0:T(256)}, s32[256]{0:T(256)S(1)}, u32[]{:S(2)}, u32[]{:S(2)}) collective-permute-start(s32[256]{0:T(256)} %get-tuple-element.160), channel_id=1, source_target_pairs={{0,8},{8,16},{16,24},{24,32},{32,40},{40,48},{48,56},{56,64},{64,7... | collective-permute-start | bytes 3080 | tf_op jit(solution)/shard_map/while/body/eval_jaxpr/ppermute | solution.py:21
  389.0 7.8 %collective-permute-start.1 = (s32[256]{0:T(256)}, s32[256]{0:T(256)S(1)}, u32[]{:S(2)}, u32[]{:S(2)}) collective-permute-start(s32[256]{0:T(256)} %get-tuple-element.160), channel_id=1, source_target_pairs={{0,8},{8,16},{16,24},{24,32},{32,40},{40,48},{48,56},{56,64},{64,7... | collective-permute-start | bytes 3080 | tf_op jit(solution)/shard_map/while/body/eval_jaxpr/ppermute | solution.py:21
  404.5 7.8 %collective-permute-start.1 = (s32[256]{0:T(256)}, s32[256]{0:T(256)S(1)}, u32[]{:S(2)}, u32[]{:S(2)}) collective-permute-start(s32[256]{0:T(256)} %get-tuple-element.160), channel_id=1, source_target_pairs={{0,8},{8,16},{16,24},{24,32},{32,40},{40,48},{48,56},{56,64},{64,7... | collective-permute-start | bytes 3080 | tf_op jit(solution)/shard_map/while/body/eval_jaxpr/ppermute | solution.py:21
  420.1 7.8 %collective-permute-start.1 = (s32[256]{0:T(256)}, s32[256]{0:T(256)S(1)}, u32[]{:S(2)}, u32[]{:S(2)}) collective-permute-start(s32[256]{0:T(256)} %get-tuple-element.160), channel_id=1, source_target_pairs={{0,8},{8,16},{16,24},{24,32},{32,40},{40,48},{48,56},{56,64},{64,7... | collective-permute-start | bytes 3080 | tf_op jit(solution)/shard_map/while/body/eval_jaxpr/ppermute | solution.py:21
  435.7 7.8 %collective-permute-start.1 = (s32[256]{0:T(256)}, s32[256]{0:T(256)S(1)}, u32[]{:S(2)}, u32[]{:S(2)}) collective-permute-start(s32[256]{0:T(256)} %get-tuple-element.160), channel_id=1, source_target_pairs={{0,8},{8,16},{16,24},{24,32},{32,40},{40,48},{48,56},{56,64},{64,7... | collective-permute-start | bytes 3080 | tf_op jit(solution)/shard_map/while/body/eval_jaxpr/ppermute | solution.py:21
  451.3 7.8 %collective-permute-start.1 = (s32[256]{0:T(256)}, s32[256]{0:T(256)S(1)}, u32[]{:S(2)}, u32[]{:S(2)}) collective-permute-start(s32[256]{0:T(256)} %get-tuple-element.160), channel_id=1, source_target_pairs={{0,8},{8,16},{16,24},{24,32},{32,40},{40,48},{48,56},{56,64},{64,7... | collective-permute-start | bytes 3080 | tf_op jit(solution)/shard_map/while/body/eval_jaxpr/ppermute | solution.py:21
  466.9 7.8 %collective-permute-start.1 = (s32[256]{0:T(256)}, s32[256]{0:T(256)S(1)}, u32[]{:S(2)}, u32[]{:S(2)}) collective-permute-start(s32[256]{0:T(256)} %get-tuple-element.160), channel_id=1, source_target_pairs={{0,8},{8,16},{16,24},{24,32},{32,40},{40,48},{48,56},{56,64},{64,7... | collective-permute-start | bytes 3080 | tf_op jit(solution)/shard_map/while/body/eval_jaxpr/ppermute | solution.py:21
  482.4 7.8 %collective-permute-start.1 = (s32[256]{0:T(256)}, s32[256]{0:T(256)S(1)}, u32[]{:S(2)}, u32[]{:S(2)}) collective-permute-start(s32[256]{0:T(256)} %get-tuple-element.160), channel_id=1, source_target_pairs={{0,8},{8,16},{16,24},{24,32},{32,40},{40,48},{48,56},{56,64},{64,7... | collective-permute-start | bytes 3080 | tf_op jit(solution)/shard_map/while/body/eval_jaxpr/ppermute | solution.py:21
  498.0 7.8 %collective-permute-start.1 = (s32[256]{0:T(256)}, s32[256]{0:T(256)S(1)}, u32[]{:S(2)}, u32[]{:S(2)}) collective-permute-start(s32[256]{0:T(256)} %get-tuple-element.160), channel_id=1, source_target_pairs={{0,8},{8,16},{16,24},{24,32},{32,40},{40,48},{48,56},{56,64},{64,7... | collective-permute-start | bytes 3080 | tf_op jit(solution)/shard_map/while/body/eval_jaxpr/ppermute | solution.py:21
  513.6 7.8 %collective-permute-start.1 = (s32[256]{0:T(256)}, s32[256]{0:T(256)S(1)}, u32[]{:S(2)}, u32[]{:S(2)}) collective-permute-start(s32[256]{0:T(256)} %get-tuple-element.160), channel_id=1, source_target_pairs={{0,8},{8,16},{16,24},{24,32},{32,40},{40,48},{48,56},{56,64},{64,7... | collective-permute-start | bytes 3080 | tf_op jit(solution)/shard_map/while/body/eval_jaxpr/ppermute | solution.py:21
  528.6 157.6 %all-reduce.2.cloned.1.call-done = bf16[256,3072]{1,0:T(8,128)(2,1)} async-done(((bf16[256,3072]{1,0:T(8,128)(2,1)}), bf16[256,3072]{1,0:T(8,128)(2,1)}) %all-reduce.2.cloned.1.call-update) | async-done | bytes 1572880 | tf_op jit(solution)/shard_map/psum | solution.py:127
  687.3 18.4 %psum.15 = f32[256]{0:T(256)S(1)} all-reduce(f32[256]{0:T(256)S(1)} %get-tuple-element.66), channel_id=1, replica_groups=mesh['seq'=64,'tp'=8] {'tp'}, use_global_device_ids=true, to_apply=%region_11.12 | all-reduce | flops 256 | bytes 2048 | tf_op jit(solution)/shard_map/psum | solution.py:133
  (491 shorter events, 325.6 us)
Async XLA Ops:
  7.2 679.0 %all-reduce.2.cloned.1.call-start = ((), (), s32[]{:S(2)}) async-start(), calls=%async_computation | async-start | bytes 3145728 | tf_op jit(solution)/shard_map/psum | solution.py:127
  143.7 17.2 %collective-permute-start = (bf16[2,256,384]{1,2,0:T(8,128)(2,1)}, bf16[2,256,384]{1,2,0:T(8,128)(2,1)S(1)}, u32[]{:S(2)}, u32[]{:S(2)}) collective-permute-start(bf16[2,256,384]{1,2,0:T(8,128)(2,1)} %get-tuple-element.159), channel_id=1, source_target_pairs={{0,8},{8,16},{16,24},{24,32},{32,40},{40,48},{48,56},{56,64},{64,7... | collective-permute-start | bytes 1179656 | tf_op jit(solution)/shard_map/while/body/eval_jaxpr/ppermute | solution.py:21
  162.7 17.1 %collective-permute-start = (bf16[2,256,384]{1,2,0:T(8,128)(2,1)}, bf16[2,256,384]{1,2,0:T(8,128)(2,1)S(1)}, u32[]{:S(2)}, u32[]{:S(2)}) collective-permute-start(bf16[2,256,384]{1,2,0:T(8,128)(2,1)} %get-tuple-element.159), channel_id=1, source_target_pairs={{0,8},{8,16},{16,24},{24,32},{32,40},{40,48},{48,56},{56,64},{64,7... | collective-permute-start | bytes 1179656 | tf_op jit(solution)/shard_map/while/body/eval_jaxpr/ppermute | solution.py:21
  181.5 16.3 %collective-permute-start = (bf16[2,256,384]{1,2,0:T(8,128)(2,1)}, bf16[2,256,384]{1,2,0:T(8,128)(2,1)S(1)}, u32[]{:S(2)}, u32[]{:S(2)}) collective-permute-start(bf16[2,256,384]{1,2,0:T(8,128)(2,1)} %get-tuple-element.159), channel_id=1, source_target_pairs={{0,8},{8,16},{16,24},{24,32},{32,40},{40,48},{48,56},{56,64},{64,7... | collective-permute-start | bytes 1179656 | tf_op jit(solution)/shard_map/while/body/eval_jaxpr/ppermute | solution.py:21
  199.6 14.9 %collective-permute-start = (bf16[2,256,384]{1,2,0:T(8,128)(2,1)}, bf16[2,256,384]{1,2,0:T(8,128)(2,1)S(1)}, u32[]{:S(2)}, u32[]{:S(2)}) collective-permute-start(bf16[2,256,384]{1,2,0:T(8,128)(2,1)} %get-tuple-element.159), channel_id=1, source_target_pairs={{0,8},{8,16},{16,24},{24,32},{32,40},{40,48},{48,56},{56,64},{64,7... | collective-permute-start | bytes 1179656 | tf_op jit(solution)/shard_map/while/body/eval_jaxpr/ppermute | solution.py:21
  231.2 13.0 %collective-permute-start = (bf16[2,256,384]{1,2,0:T(8,128)(2,1)}, bf16[2,256,384]{1,2,0:T(8,128)(2,1)S(1)}, u32[]{:S(2)}, u32[]{:S(2)}) collective-permute-start(bf16[2,256,384]{1,2,0:T(8,128)(2,1)} %get-tuple-element.159), channel_id=1, source_target_pairs={{0,8},{8,16},{16,24},{24,32},{32,40},{40,48},{48,56},{56,64},{64,7... | collective-permute-start | bytes 1179656 | tf_op jit(solution)/shard_map/while/body/eval_jaxpr/ppermute | solution.py:21
  246.0 13.0 %collective-permute-start = (bf16[2,256,384]{1,2,0:T(8,128)(2,1)}, bf16[2,256,384]{1,2,0:T(8,128)(2,1)S(1)}, u32[]{:S(2)}, u32[]{:S(2)}) collective-permute-start(bf16[2,256,384]{1,2,0:T(8,128)(2,1)} %get-tuple-element.159), channel_id=1, source_target_pairs={{0,8},{8,16},{16,24},{24,32},{32,40},{40,48},{48,56},{56,64},{64,7... | collective-permute-start | bytes 1179656 | tf_op jit(solution)/shard_map/while/body/eval_jaxpr/ppermute | solution.py:21
  260.8 13.0 %collective-permute-start = (bf16[2,256,384]{1,2,0:T(8,128)(2,1)}, bf16[2,256,384]{1,2,0:T(8,128)(2,1)S(1)}, u32[]{:S(2)}, u32[]{:S(2)}) collective-permute-start(bf16[2,256,384]{1,2,0:T(8,128)(2,1)} %get-tuple-element.159), channel_id=1, source_target_pairs={{0,8},{8,16},{16,24},{24,32},{32,40},{40,48},{48,56},{56,64},{64,7... | collective-permute-start | bytes 1179656 | tf_op jit(solution)/shard_map/while/body/eval_jaxpr/ppermute | solution.py:21
  275.7 13.8 %collective-permute-start = (bf16[2,256,384]{1,2,0:T(8,128)(2,1)}, bf16[2,256,384]{1,2,0:T(8,128)(2,1)S(1)}, u32[]{:S(2)}, u32[]{:S(2)}) collective-permute-start(bf16[2,256,384]{1,2,0:T(8,128)(2,1)} %get-tuple-element.159), channel_id=1, source_target_pairs={{0,8},{8,16},{16,24},{24,32},{32,40},{40,48},{48,56},{56,64},{64,7... | collective-permute-start | bytes 1179656 | tf_op jit(solution)/shard_map/while/body/eval_jaxpr/ppermute | solution.py:21
  291.2 13.8 %collective-permute-start = (bf16[2,256,384]{1,2,0:T(8,128)(2,1)}, bf16[2,256,384]{1,2,0:T(8,128)(2,1)S(1)}, u32[]{:S(2)}, u32[]{:S(2)}) collective-permute-start(bf16[2,256,384]{1,2,0:T(8,128)(2,1)} %get-tuple-element.159), channel_id=1, source_target_pairs={{0,8},{8,16},{16,24},{24,32},{32,40},{40,48},{48,56},{56,64},{64,7... | collective-permute-start | bytes 1179656 | tf_op jit(solution)/shard_map/while/body/eval_jaxpr/ppermute | solution.py:21
  306.8 13.8 %collective-permute-start = (bf16[2,256,384]{1,2,0:T(8,128)(2,1)}, bf16[2,256,384]{1,2,0:T(8,128)(2,1)S(1)}, u32[]{:S(2)}, u32[]{:S(2)}) collective-permute-start(bf16[2,256,384]{1,2,0:T(8,128)(2,1)} %get-tuple-element.159), channel_id=1, source_target_pairs={{0,8},{8,16},{16,24},{24,32},{32,40},{40,48},{48,56},{56,64},{64,7... | collective-permute-start | bytes 1179656 | tf_op jit(solution)/shard_map/while/body/eval_jaxpr/ppermute | solution.py:21
  322.4 13.8 %collective-permute-start = (bf16[2,256,384]{1,2,0:T(8,128)(2,1)}, bf16[2,256,384]{1,2,0:T(8,128)(2,1)S(1)}, u32[]{:S(2)}, u32[]{:S(2)}) collective-permute-start(bf16[2,256,384]{1,2,0:T(8,128)(2,1)} %get-tuple-element.159), channel_id=1, source_target_pairs={{0,8},{8,16},{16,24},{24,32},{32,40},{40,48},{48,56},{56,64},{64,7... | collective-permute-start | bytes 1179656 | tf_op jit(solution)/shard_map/while/body/eval_jaxpr/ppermute | solution.py:21
  338.0 13.8 %collective-permute-start = (bf16[2,256,384]{1,2,0:T(8,128)(2,1)}, bf16[2,256,384]{1,2,0:T(8,128)(2,1)S(1)}, u32[]{:S(2)}, u32[]{:S(2)}) collective-permute-start(bf16[2,256,384]{1,2,0:T(8,128)(2,1)} %get-tuple-element.159), channel_id=1, source_target_pairs={{0,8},{8,16},{16,24},{24,32},{32,40},{40,48},{48,56},{56,64},{64,7... | collective-permute-start | bytes 1179656 | tf_op jit(solution)/shard_map/while/body/eval_jaxpr/ppermute | solution.py:21
  353.6 13.8 %collective-permute-start = (bf16[2,256,384]{1,2,0:T(8,128)(2,1)}, bf16[2,256,384]{1,2,0:T(8,128)(2,1)S(1)}, u32[]{:S(2)}, u32[]{:S(2)}) collective-permute-start(bf16[2,256,384]{1,2,0:T(8,128)(2,1)} %get-tuple-element.159), channel_id=1, source_target_pairs={{0,8},{8,16},{16,24},{24,32},{32,40},{40,48},{48,56},{56,64},{64,7... | collective-permute-start | bytes 1179656 | tf_op jit(solution)/shard_map/while/body/eval_jaxpr/ppermute | solution.py:21
  369.1 13.8 %collective-permute-start = (bf16[2,256,384]{1,2,0:T(8,128)(2,1)}, bf16[2,256,384]{1,2,0:T(8,128)(2,1)S(1)}, u32[]{:S(2)}, u32[]{:S(2)}) collective-permute-start(bf16[2,256,384]{1,2,0:T(8,128)(2,1)} %get-tuple-element.159), channel_id=1, source_target_pairs={{0,8},{8,16},{16,24},{24,32},{32,40},{40,48},{48,56},{56,64},{64,7... | collective-permute-start | bytes 1179656 | tf_op jit(solution)/shard_map/while/body/eval_jaxpr/ppermute | solution.py:21
  384.7 13.8 %collective-permute-start = (bf16[2,256,384]{1,2,0:T(8,128)(2,1)}, bf16[2,256,384]{1,2,0:T(8,128)(2,1)S(1)}, u32[]{:S(2)}, u32[]{:S(2)}) collective-permute-start(bf16[2,256,384]{1,2,0:T(8,128)(2,1)} %get-tuple-element.159), channel_id=1, source_target_pairs={{0,8},{8,16},{16,24},{24,32},{32,40},{40,48},{48,56},{56,64},{64,7... | collective-permute-start | bytes 1179656 | tf_op jit(solution)/shard_map/while/body/eval_jaxpr/ppermute | solution.py:21
  400.3 13.8 %collective-permute-start = (bf16[2,256,384]{1,2,0:T(8,128)(2,1)}, bf16[2,256,384]{1,2,0:T(8,128)(2,1)S(1)}, u32[]{:S(2)}, u32[]{:S(2)}) collective-permute-start(bf16[2,256,384]{1,2,0:T(8,128)(2,1)} %get-tuple-element.159), channel_id=1, source_target_pairs={{0,8},{8,16},{16,24},{24,32},{32,40},{40,48},{48,56},{56,64},{64,7... | collective-permute-start | bytes 1179656 | tf_op jit(solution)/shard_map/while/body/eval_jaxpr/ppermute | solution.py:21
  415.9 13.8 %collective-permute-start = (bf16[2,256,384]{1,2,0:T(8,128)(2,1)}, bf16[2,256,384]{1,2,0:T(8,128)(2,1)S(1)}, u32[]{:S(2)}, u32[]{:S(2)}) collective-permute-start(bf16[2,256,384]{1,2,0:T(8,128)(2,1)} %get-tuple-element.159), channel_id=1, source_target_pairs={{0,8},{8,16},{16,24},{24,32},{32,40},{40,48},{48,56},{56,64},{64,7... | collective-permute-start | bytes 1179656 | tf_op jit(solution)/shard_map/while/body/eval_jaxpr/ppermute | solution.py:21
  431.5 13.8 %collective-permute-start = (bf16[2,256,384]{1,2,0:T(8,128)(2,1)}, bf16[2,256,384]{1,2,0:T(8,128)(2,1)S(1)}, u32[]{:S(2)}, u32[]{:S(2)}) collective-permute-start(bf16[2,256,384]{1,2,0:T(8,128)(2,1)} %get-tuple-element.159), channel_id=1, source_target_pairs={{0,8},{8,16},{16,24},{24,32},{32,40},{40,48},{48,56},{56,64},{64,7... | collective-permute-start | bytes 1179656 | tf_op jit(solution)/shard_map/while/body/eval_jaxpr/ppermute | solution.py:21
  447.0 13.8 %collective-permute-start = (bf16[2,256,384]{1,2,0:T(8,128)(2,1)}, bf16[2,256,384]{1,2,0:T(8,128)(2,1)S(1)}, u32[]{:S(2)}, u32[]{:S(2)}) collective-permute-start(bf16[2,256,384]{1,2,0:T(8,128)(2,1)} %get-tuple-element.159), channel_id=1, source_target_pairs={{0,8},{8,16},{16,24},{24,32},{32,40},{40,48},{48,56},{56,64},{64,7... | collective-permute-start | bytes 1179656 | tf_op jit(solution)/shard_map/while/body/eval_jaxpr/ppermute | solution.py:21
  462.6 13.8 %collective-permute-start = (bf16[2,256,384]{1,2,0:T(8,128)(2,1)}, bf16[2,256,384]{1,2,0:T(8,128)(2,1)S(1)}, u32[]{:S(2)}, u32[]{:S(2)}) collective-permute-start(bf16[2,256,384]{1,2,0:T(8,128)(2,1)} %get-tuple-element.159), channel_id=1, source_target_pairs={{0,8},{8,16},{16,24},{24,32},{32,40},{40,48},{48,56},{56,64},{64,7... | collective-permute-start | bytes 1179656 | tf_op jit(solution)/shard_map/while/body/eval_jaxpr/ppermute | solution.py:21
  478.2 13.8 %collective-permute-start = (bf16[2,256,384]{1,2,0:T(8,128)(2,1)}, bf16[2,256,384]{1,2,0:T(8,128)(2,1)S(1)}, u32[]{:S(2)}, u32[]{:S(2)}) collective-permute-start(bf16[2,256,384]{1,2,0:T(8,128)(2,1)} %get-tuple-element.159), channel_id=1, source_target_pairs={{0,8},{8,16},{16,24},{24,32},{32,40},{40,48},{48,56},{56,64},{64,7... | collective-permute-start | bytes 1179656 | tf_op jit(solution)/shard_map/while/body/eval_jaxpr/ppermute | solution.py:21
  493.8 13.8 %collective-permute-start = (bf16[2,256,384]{1,2,0:T(8,128)(2,1)}, bf16[2,256,384]{1,2,0:T(8,128)(2,1)S(1)}, u32[]{:S(2)}, u32[]{:S(2)}) collective-permute-start(bf16[2,256,384]{1,2,0:T(8,128)(2,1)} %get-tuple-element.159), channel_id=1, source_target_pairs={{0,8},{8,16},{16,24},{24,32},{32,40},{40,48},{48,56},{56,64},{64,7... | collective-permute-start | bytes 1179656 | tf_op jit(solution)/shard_map/while/body/eval_jaxpr/ppermute | solution.py:21
  509.4 13.8 %collective-permute-start = (bf16[2,256,384]{1,2,0:T(8,128)(2,1)}, bf16[2,256,384]{1,2,0:T(8,128)(2,1)S(1)}, u32[]{:S(2)}, u32[]{:S(2)}) collective-permute-start(bf16[2,256,384]{1,2,0:T(8,128)(2,1)} %get-tuple-element.159), channel_id=1, source_target_pairs={{0,8},{8,16},{16,24},{24,32},{32,40},{40,48},{48,56},{56,64},{64,7... | collective-permute-start | bytes 1179656 | tf_op jit(solution)/shard_map/while/body/eval_jaxpr/ppermute | solution.py:21
  (54 other events, 1324.7 us)
Sparse Core Ops, SparseCore 0:
  527.3 158.8 all-reduce.1
where the time goes:
time: 716 us; the launch traced here: 713 us
  starting transfers between devices  360 us (50%)
  waiting for transfers between devices  199 us (28%)
  local copies, waits for them, and re-layouts  47.7 us (7%)
  blocking collectives  46.2 us (6%)
  matrix products  28.1 us (4%)
  other arithmetic  16.5 us (2%)
  between operations  14.3 us (2%)
    ppermute x64, starting transfers between devices, passed_along(): return lax.ppermute(block, axis, route)  360 us
    psum x1, waiting for transfers between devices, per_device(): lax.psum(partial_value.astype(jnp.bfloat16), 'tp').astype(jnp.float32)  158 us
    while x96, local copies, waits for them, and re-layouts  42 us
    ppermute x64, waiting for transfers between devices, passed_along(): return lax.ppermute(block, axis, route)  40.9 us
    pmin x1, blocking collectives, per_device(): first_tok = lax.pmin(local_first, 'seq')  27.8 us
    psum x1, blocking collectives, per_device(): square_total = lax.psum(jnp.sum(stream_wide * stream_wide, axis=1), 'tp')  18.4 us
  transfers between devices with their start and end apart: 65, of which 33 were waited for; matrix products, arithmetic and copies ran while one was open for 3% of the time, Pallas kernels for 0%

commit v1 on v0

--- a/solution.py
+++ b/solution.py
@@ -92,7 +92,11 @@
     query_heads = q_rot.reshape(tok_count, head_count, HEAD_DIM)
     query_tag = segment_ids + 1
     key_tag = jnp.where(pad_mask == 1, segment_ids + 1, 0)
-    own_block = jnp.stack([k_rot, value_proj])
+    tag_rows = -(-tok_count // feat_count)
+    tag_block = jnp.pad(key_tag.astype(jnp.bfloat16), (0, tag_rows * feat_count - tok_count))
+    own_block = jnp.concatenate(
+        [k_rot, value_proj, tag_block.reshape(tag_rows, feat_count)], axis=0
+    )
     offsets = jnp.arange(tok_count, dtype=jnp.int32)
     own_visible = (key_tag[None, :] == query_tag[:, None]) & (
         offsets[None, :] <= offsets[:, None]
@@ -102,20 +106,23 @@
         jnp.zeros((head_count, tok_count), jnp.float32),
         jnp.zeros((head_count, tok_count, HEAD_DIM), jnp.float32),
     )
-    softmax_state = attend(softmax_state, query_heads, own_block, own_visible)
+    softmax_state = attend(softmax_state, query_heads, jnp.stack([k_rot, value_proj]), own_visible)
+    query_tag_wide = query_tag.astype(jnp.bfloat16)
 
-    def visit_block(current, moved, moved_tags):
-        visible = moved_tags[None, :] == query_tag[:, None]
-        return attend(current, query_heads, moved, visible)
+    def visit_block(current, moved):
+        pair = moved[: 2 * tok_count].reshape(2, tok_count, feat_count)
+        moved_tags = moved[2 * tok_count :].reshape(-1)[:tok_count]
+        visible = moved_tags[None, :] == query_tag_wide[:, None]
+        return attend(current, query_heads, pair, visible)
 
     def cycle_turn(turn_index, loop_state):
-        current, moved, moved_tags = loop_state
-        moved, moved_tags = passed_along((moved, moved_tags), "seq", 1)
-        return (visit_block(current, moved, moved_tags), moved, moved_tags)
+        current, moved = loop_state
+        following = passed_along(moved, "seq", 1)
+        return (visit_block(current, moved), following)
 
-    softmax_state = lax.fori_loop(0, reach_count, cycle_turn, (softmax_state, own_block, key_tag))[
-        0
-    ]
+    moved = passed_along(own_block, "seq", 1)
+    softmax_state, moved = lax.fori_loop(0, reach_count - 1, cycle_turn, (softmax_state, moved))
+    softmax_state = visit_block(softmax_state, moved)
     row_peak, row_total, weighted = softmax_state
     attn = (
         jnp.transpose(weighted / row_total[..., None], (1, 0, 2))
@@ -124,10 +131,9 @@
     )
     partial_value = jnp.dot(attn, out_weight, preferred_element_type=jnp.float32)
     feature_width = hidden.shape[1]
-    summed = lax.psum(partial_value.astype(jnp.bfloat16), "tp").astype(jnp.float32)
-    own_sum = lax.dynamic_slice_in_dim(
-        summed, lax.axis_index("tp") * feature_width, feature_width, 1
-    )
+    own_sum = lax.psum_scatter(
+        partial_value.astype(jnp.bfloat16), "tp", scatter_dimension=1, tiled=True
+    ).astype(jnp.float32)
     hidden_out = (hidden.astype(jnp.float32) + own_sum).astype(jnp.bfloat16)
     stream_wide = hidden_out.astype(jnp.float32)
     square_total = lax.psum(jnp.sum(stream_wide * stream_wide, axis=1), "tp")

time: 716 us -> 684 us (0.955)
  the two profiles are of different devices: /device:TPU:24 before, /device:TPU:8 now
where the time goes in v1:
time: 684 us; the launch traced here: 679 us
  local copies, waits for them, and re-layouts  171 us (25%)
  starting transfers between devices  162 us (24%)
  waiting for transfers between devices  147 us (21%)
  matrix products  118 us (17%)
  blocking collectives  46.7 us (7%)
  other arithmetic  18.6 us (3%)
  between operations  14.4 us (2%)
    ppermute x32, starting transfers between devices, passed_along(): return lax.ppermute(block, axis, route)  162 us
    unnamed x2, waiting for transfers between devices  147 us
    dot_general x33, matrix products, attend(): jnp.einsum('hqk,khd->hqd', unnormed.astype(jnp.bfloat16), val_heads, pref...  69.6 us
    slice x64, local copies, waits for them, and re-layouts, attend(): val_heads = block[1].reshape(key_count, head_count, HEAD_DIM)  59.8 us
    another operation x31, local copies, waits for them, and re-layouts  55 us
    dot_general x33, matrix products, attend(): jnp.einsum('qhd,khd->hqk', query_heads, key_heads, preferred_element_type...  45.9 us
    pmin x1, blocking collectives, per_device(): first_tok = lax.pmin(local_first, 'seq')  28.3 us
    slice x32, local copies, waits for them, and re-layouts, attend(): key_heads = block[0].reshape(key_count, head_count, HEAD_DIM)  25.6 us
  transfers between devices with their start and end apart: 33, of which 2 were waited for; matrix products, arithmetic and copies ran while one was open for 35% of the time, Pallas kernels for 0%

profile of v1, /device:TPU:8, one launch (start us, length us, event | category | flops | bytes accessed | tf_op | source)
XLA Modules:
  0.0 678.9 jit_solution(2169950836960678962)
XLA Ops:
  8.2 28.3 %pmin.7 = s32[32]{0:T(128)S(1)} all-reduce(s32[32]{0:T(128)S(1)} %select_reduce_fusion.1), channel_id=1, replica_groups=mesh['seq'=64,'tp'=8] {'seq'}, use_global_device_ids=true, to_apply=%region_1.2 | all-reduce | flops 32 | bytes 256 | tf_op jit(solution)/shard_map/pmin | solution.py:88
  50.9 443.5 %while.16 = (s32[]{:T(128)}, f32[4,256]{1,0:T(4,128)S(1)}, f32[4,256]{1,0:T(4,128)S(1)}, f32[4,256,96]{1,2,0:T(8,128)}, bf16[513,384]{1,0:T(8,128)(2,1)}, /*inde...) while((s32[]{:T(128)}, f32[4,256]{1,0:T(4,128)S(1)}, f32[4,256]{1,0:T(4,128)S(1)}, ...), condition=%wide.region_8.9_spmd, body=%wide.region_5.8_spmd.sunk | while | flops 103286784 | bytes 8788605 | solution.py:124
  111.1 3.4 collective-permute-start
  160.9 3.3 collective-permute-start
  210.7 3.5 collective-permute-start
  223.4 9.2 %collective-permute-start = (bf16[513,384]{1,0:T(8,128)(2,1)}, bf16[513,384]{1,0:T(8,128)(2,1)}, u32[]{:S(2)}, u32[]{:S(2)}) collective-permute-start(bf16[513,384]{1,0:T(8,128)(2,1)} %copy.78), channel_id=1, source_target_pairs={{0,8},{8,16},{16,24},{24,32},{32,40},{40,48},{48,56},{56,64},{64,7... | collective-permute-start | bytes 1181960 | tf_op jit(solution)/shard_map/while/body/eval_jaxpr/ppermute | solution.py:21
  241.7 8.9 %collective-permute-start = (bf16[513,384]{1,0:T(8,128)(2,1)}, bf16[513,384]{1,0:T(8,128)(2,1)}, u32[]{:S(2)}, u32[]{:S(2)}) collective-permute-start(bf16[513,384]{1,0:T(8,128)(2,1)} %copy.78), channel_id=1, source_target_pairs={{0,8},{8,16},{16,24},{24,32},{32,40},{40,48},{48,56},{56,64},{64,7... | collective-permute-start | bytes 1181960 | tf_op jit(solution)/shard_map/while/body/eval_jaxpr/ppermute | solution.py:21
  259.8 9.4 %collective-permute-start = (bf16[513,384]{1,0:T(8,128)(2,1)}, bf16[513,384]{1,0:T(8,128)(2,1)}, u32[]{:S(2)}, u32[]{:S(2)}) collective-permute-start(bf16[513,384]{1,0:T(8,128)(2,1)} %copy.78), channel_id=1, source_target_pairs={{0,8},{8,16},{16,24},{24,32},{32,40},{40,48},{48,56},{56,64},{64,7... | collective-permute-start | bytes 1181960 | tf_op jit(solution)/shard_map/while/body/eval_jaxpr/ppermute | solution.py:21
  278.3 9.2 %collective-permute-start = (bf16[513,384]{1,0:T(8,128)(2,1)}, bf16[513,384]{1,0:T(8,128)(2,1)}, u32[]{:S(2)}, u32[]{:S(2)}) collective-permute-start(bf16[513,384]{1,0:T(8,128)(2,1)} %copy.78), channel_id=1, source_target_pairs={{0,8},{8,16},{16,24},{24,32},{32,40},{40,48},{48,56},{56,64},{64,7... | collective-permute-start | bytes 1181960 | tf_op jit(solution)/shard_map/while/body/eval_jaxpr/ppermute | solution.py:21
  296.6 8.4 %collective-permute-start = (bf16[513,384]{1,0:T(8,128)(2,1)}, bf16[513,384]{1,0:T(8,128)(2,1)}, u32[]{:S(2)}, u32[]{:S(2)}) collective-permute-start(bf16[513,384]{1,0:T(8,128)(2,1)} %copy.78), channel_id=1, source_target_pairs={{0,8},{8,16},{16,24},{24,32},{32,40},{40,48},{48,56},{56,64},{64,7... | collective-permute-start | bytes 1181960 | tf_op jit(solution)/shard_map/while/body/eval_jaxpr/ppermute | solution.py:21
  314.2 7.1 %collective-permute-start = (bf16[513,384]{1,0:T(8,128)(2,1)}, bf16[513,384]{1,0:T(8,128)(2,1)}, u32[]{:S(2)}, u32[]{:S(2)}) collective-permute-start(bf16[513,384]{1,0:T(8,128)(2,1)} %copy.78), channel_id=1, source_target_pairs={{0,8},{8,16},{16,24},{24,32},{32,40},{40,48},{48,56},{56,64},{64,7... | collective-permute-start | bytes 1181960 | tf_op jit(solution)/shard_map/while/body/eval_jaxpr/ppermute | solution.py:21
  330.4 5.1 collective-permute-start
  344.7 5.1 collective-permute-start
  358.9 5.1 collective-permute-start
  373.2 5.7 collective-permute-start
  388.1 6.5 collective-permute-start
  403.6 6.5 collective-permute-start
  419.3 6.4 collective-permute-start
  434.7 6.3 collective-permute-start
  450.2 6.2 collective-permute-start
  465.5 6.2 collective-permute-start
  480.8 6.2 collective-permute-start
  504.7 146.8 %reduce-scatter.4.cloned.1.call-done = bf16[384,256]{1,0:T(8,128)(2,1)} async-done(((bf16[3072,256]{1,0:T(8,128)(2,1)}), bf16[384,256]{1,0:T(8,128)(2,1)}) %reduce-scatter.4.cloned.1.call-update) | async-done | bytes 196624
  652.8 18.4 %psum.7 = f32[256]{0:T(256)S(1)} all-reduce(f32[256]{0:T(256)S(1)} %get-tuple-element.63), channel_id=1, replica_groups=mesh['seq'=64,'tp'=8] {'tp'}, use_global_device_ids=true, to_apply=%region_13.14 | all-reduce | flops 256 | bytes 2048 | tf_op jit(solution)/shard_map/psum | solution.py:139
  (497 shorter events, 341.9 us)
Async XLA Ops:
  7.2 644.4 %reduce-scatter.4.cloned.1.call-start = ((), (), s32[]{:S(2)}) async-start(), calls=%async_computation.1 | async-start | bytes 1769472
  111.1 10.7 %collective-permute-start = (bf16[513,384]{1,0:T(8,128)(2,1)}, bf16[513,384]{1,0:T(8,128)(2,1)}, u32[]{:S(2)}, u32[]{:S(2)}) collective-permute-start(bf16[513,384]{1,0:T(8,128)(2,1)} %copy.78), channel_id=1, source_target_pairs={{0,8},{8,16},{16,24},{24,32},{32,40},{40,48},{48,56},{56,64},{64,7... | collective-permute-start | bytes 1181960 | tf_op jit(solution)/shard_map/while/body/eval_jaxpr/ppermute | solution.py:21
  123.6 10.7 %collective-permute-start = (bf16[513,384]{1,0:T(8,128)(2,1)}, bf16[513,384]{1,0:T(8,128)(2,1)}, u32[]{:S(2)}, u32[]{:S(2)}) collective-permute-start(bf16[513,384]{1,0:T(8,128)(2,1)} %copy.78), channel_id=1, source_target_pairs={{0,8},{8,16},{16,24},{24,32},{32,40},{40,48},{48,56},{56,64},{64,7... | collective-permute-start | bytes 1181960 | tf_op jit(solution)/shard_map/while/body/eval_jaxpr/ppermute | solution.py:21
  160.9 10.7 %collective-permute-start = (bf16[513,384]{1,0:T(8,128)(2,1)}, bf16[513,384]{1,0:T(8,128)(2,1)}, u32[]{:S(2)}, u32[]{:S(2)}) collective-permute-start(bf16[513,384]{1,0:T(8,128)(2,1)} %copy.78), channel_id=1, source_target_pairs={{0,8},{8,16},{16,24},{24,32},{32,40},{40,48},{48,56},{56,64},{64,7... | collective-permute-start | bytes 1181960 | tf_op jit(solution)/shard_map/while/body/eval_jaxpr/ppermute | solution.py:21
  173.4 10.7 %collective-permute-start = (bf16[513,384]{1,0:T(8,128)(2,1)}, bf16[513,384]{1,0:T(8,128)(2,1)}, u32[]{:S(2)}, u32[]{:S(2)}) collective-permute-start(bf16[513,384]{1,0:T(8,128)(2,1)} %copy.78), channel_id=1, source_target_pairs={{0,8},{8,16},{16,24},{24,32},{32,40},{40,48},{48,56},{56,64},{64,7... | collective-permute-start | bytes 1181960 | tf_op jit(solution)/shard_map/while/body/eval_jaxpr/ppermute | solution.py:21
  198.3 10.7 %collective-permute-start = (bf16[513,384]{1,0:T(8,128)(2,1)}, bf16[513,384]{1,0:T(8,128)(2,1)}, u32[]{:S(2)}, u32[]{:S(2)}) collective-permute-start(bf16[513,384]{1,0:T(8,128)(2,1)} %copy.78), channel_id=1, source_target_pairs={{0,8},{8,16},{16,24},{24,32},{32,40},{40,48},{48,56},{56,64},{64,7... | collective-permute-start | bytes 1181960 | tf_op jit(solution)/shard_map/while/body/eval_jaxpr/ppermute | solution.py:21
  210.7 10.9 %collective-permute-start = (bf16[513,384]{1,0:T(8,128)(2,1)}, bf16[513,384]{1,0:T(8,128)(2,1)}, u32[]{:S(2)}, u32[]{:S(2)}) collective-permute-start(bf16[513,384]{1,0:T(8,128)(2,1)} %copy.78), channel_id=1, source_target_pairs={{0,8},{8,16},{16,24},{24,32},{32,40},{40,48},{48,56},{56,64},{64,7... | collective-permute-start | bytes 1181960 | tf_op jit(solution)/shard_map/while/body/eval_jaxpr/ppermute | solution.py:21
  223.4 16.5 %collective-permute-start = (bf16[513,384]{1,0:T(8,128)(2,1)}, bf16[513,384]{1,0:T(8,128)(2,1)}, u32[]{:S(2)}, u32[]{:S(2)}) collective-permute-start(bf16[513,384]{1,0:T(8,128)(2,1)} %copy.78), channel_id=1, source_target_pairs={{0,8},{8,16},{16,24},{24,32},{32,40},{40,48},{48,56},{56,64},{64,7... | collective-permute-start | bytes 1181960 | tf_op jit(solution)/shard_map/while/body/eval_jaxpr/ppermute | solution.py:21
  241.7 16.3 %collective-permute-start = (bf16[513,384]{1,0:T(8,128)(2,1)}, bf16[513,384]{1,0:T(8,128)(2,1)}, u32[]{:S(2)}, u32[]{:S(2)}) collective-permute-start(bf16[513,384]{1,0:T(8,128)(2,1)} %copy.78), channel_id=1, source_target_pairs={{0,8},{8,16},{16,24},{24,32},{32,40},{40,48},{48,56},{56,64},{64,7... | collective-permute-start | bytes 1181960 | tf_op jit(solution)/shard_map/while/body/eval_jaxpr/ppermute | solution.py:21
  259.8 16.8 %collective-permute-start = (bf16[513,384]{1,0:T(8,128)(2,1)}, bf16[513,384]{1,0:T(8,128)(2,1)}, u32[]{:S(2)}, u32[]{:S(2)}) collective-permute-start(bf16[513,384]{1,0:T(8,128)(2,1)} %copy.78), channel_id=1, source_target_pairs={{0,8},{8,16},{16,24},{24,32},{32,40},{40,48},{48,56},{56,64},{64,7... | collective-permute-start | bytes 1181960 | tf_op jit(solution)/shard_map/while/body/eval_jaxpr/ppermute | solution.py:21
  278.3 16.6 %collective-permute-start = (bf16[513,384]{1,0:T(8,128)(2,1)}, bf16[513,384]{1,0:T(8,128)(2,1)}, u32[]{:S(2)}, u32[]{:S(2)}) collective-permute-start(bf16[513,384]{1,0:T(8,128)(2,1)} %copy.78), channel_id=1, source_target_pairs={{0,8},{8,16},{16,24},{24,32},{32,40},{40,48},{48,56},{56,64},{64,7... | collective-permute-start | bytes 1181960 | tf_op jit(solution)/shard_map/while/body/eval_jaxpr/ppermute | solution.py:21
  296.6 15.8 %collective-permute-start = (bf16[513,384]{1,0:T(8,128)(2,1)}, bf16[513,384]{1,0:T(8,128)(2,1)}, u32[]{:S(2)}, u32[]{:S(2)}) collective-permute-start(bf16[513,384]{1,0:T(8,128)(2,1)} %copy.78), channel_id=1, source_target_pairs={{0,8},{8,16},{16,24},{24,32},{32,40},{40,48},{48,56},{56,64},{64,7... | collective-permute-start | bytes 1181960 | tf_op jit(solution)/shard_map/while/body/eval_jaxpr/ppermute | solution.py:21
  314.2 14.5 %collective-permute-start = (bf16[513,384]{1,0:T(8,128)(2,1)}, bf16[513,384]{1,0:T(8,128)(2,1)}, u32[]{:S(2)}, u32[]{:S(2)}) collective-permute-start(bf16[513,384]{1,0:T(8,128)(2,1)} %copy.78), channel_id=1, source_target_pairs={{0,8},{8,16},{16,24},{24,32},{32,40},{40,48},{48,56},{56,64},{64,7... | collective-permute-start | bytes 1181960 | tf_op jit(solution)/shard_map/while/body/eval_jaxpr/ppermute | solution.py:21
  330.4 12.5 %collective-permute-start = (bf16[513,384]{1,0:T(8,128)(2,1)}, bf16[513,384]{1,0:T(8,128)(2,1)}, u32[]{:S(2)}, u32[]{:S(2)}) collective-permute-start(bf16[513,384]{1,0:T(8,128)(2,1)} %copy.78), channel_id=1, source_target_pairs={{0,8},{8,16},{16,24},{24,32},{32,40},{40,48},{48,56},{56,64},{64,7... | collective-permute-start | bytes 1181960 | tf_op jit(solution)/shard_map/while/body/eval_jaxpr/ppermute | solution.py:21
  344.7 12.5 %collective-permute-start = (bf16[513,384]{1,0:T(8,128)(2,1)}, bf16[513,384]{1,0:T(8,128)(2,1)}, u32[]{:S(2)}, u32[]{:S(2)}) collective-permute-start(bf16[513,384]{1,0:T(8,128)(2,1)} %copy.78), channel_id=1, source_target_pairs={{0,8},{8,16},{16,24},{24,32},{32,40},{40,48},{48,56},{56,64},{64,7... | collective-permute-start | bytes 1181960 | tf_op jit(solution)/shard_map/while/body/eval_jaxpr/ppermute | solution.py:21
  358.9 12.5 %collective-permute-start = (bf16[513,384]{1,0:T(8,128)(2,1)}, bf16[513,384]{1,0:T(8,128)(2,1)}, u32[]{:S(2)}, u32[]{:S(2)}) collective-permute-start(bf16[513,384]{1,0:T(8,128)(2,1)} %copy.78), channel_id=1, source_target_pairs={{0,8},{8,16},{16,24},{24,32},{32,40},{40,48},{48,56},{56,64},{64,7... | collective-permute-start | bytes 1181960 | tf_op jit(solution)/shard_map/while/body/eval_jaxpr/ppermute | solution.py:21
  373.2 13.1 %collective-permute-start = (bf16[513,384]{1,0:T(8,128)(2,1)}, bf16[513,384]{1,0:T(8,128)(2,1)}, u32[]{:S(2)}, u32[]{:S(2)}) collective-permute-start(bf16[513,384]{1,0:T(8,128)(2,1)} %copy.78), channel_id=1, source_target_pairs={{0,8},{8,16},{16,24},{24,32},{32,40},{40,48},{48,56},{56,64},{64,7... | collective-permute-start | bytes 1181960 | tf_op jit(solution)/shard_map/while/body/eval_jaxpr/ppermute | solution.py:21
  388.1 13.8 %collective-permute-start = (bf16[513,384]{1,0:T(8,128)(2,1)}, bf16[513,384]{1,0:T(8,128)(2,1)}, u32[]{:S(2)}, u32[]{:S(2)}) collective-permute-start(bf16[513,384]{1,0:T(8,128)(2,1)} %copy.78), channel_id=1, source_target_pairs={{0,8},{8,16},{16,24},{24,32},{32,40},{40,48},{48,56},{56,64},{64,7... | collective-permute-start | bytes 1181960 | tf_op jit(solution)/shard_map/while/body/eval_jaxpr/ppermute | solution.py:21
  403.6 13.8 %collective-permute-start = (bf16[513,384]{1,0:T(8,128)(2,1)}, bf16[513,384]{1,0:T(8,128)(2,1)}, u32[]{:S(2)}, u32[]{:S(2)}) collective-permute-start(bf16[513,384]{1,0:T(8,128)(2,1)} %copy.78), channel_id=1, source_target_pairs={{0,8},{8,16},{16,24},{24,32},{32,40},{40,48},{48,56},{56,64},{64,7... | collective-permute-start | bytes 1181960 | tf_op jit(solution)/shard_map/while/body/eval_jaxpr/ppermute | solution.py:21
  419.3 13.7 %collective-permute-start = (bf16[513,384]{1,0:T(8,128)(2,1)}, bf16[513,384]{1,0:T(8,128)(2,1)}, u32[]{:S(2)}, u32[]{:S(2)}) collective-permute-start(bf16[513,384]{1,0:T(8,128)(2,1)} %copy.78), channel_id=1, source_target_pairs={{0,8},{8,16},{16,24},{24,32},{32,40},{40,48},{48,56},{56,64},{64,7... | collective-permute-start | bytes 1181960 | tf_op jit(solution)/shard_map/while/body/eval_jaxpr/ppermute | solution.py:21
  434.7 13.6 %collective-permute-start = (bf16[513,384]{1,0:T(8,128)(2,1)}, bf16[513,384]{1,0:T(8,128)(2,1)}, u32[]{:S(2)}, u32[]{:S(2)}) collective-permute-start(bf16[513,384]{1,0:T(8,128)(2,1)} %copy.78), channel_id=1, source_target_pairs={{0,8},{8,16},{16,24},{24,32},{32,40},{40,48},{48,56},{56,64},{64,7... | collective-permute-start | bytes 1181960 | tf_op jit(solution)/shard_map/while/body/eval_jaxpr/ppermute | solution.py:21
  450.2 13.6 %collective-permute-start = (bf16[513,384]{1,0:T(8,128)(2,1)}, bf16[513,384]{1,0:T(8,128)(2,1)}, u32[]{:S(2)}, u32[]{:S(2)}) collective-permute-start(bf16[513,384]{1,0:T(8,128)(2,1)} %copy.78), channel_id=1, source_target_pairs={{0,8},{8,16},{16,24},{24,32},{32,40},{40,48},{48,56},{56,64},{64,7... | collective-permute-start | bytes 1181960 | tf_op jit(solution)/shard_map/while/body/eval_jaxpr/ppermute | solution.py:21
  465.5 13.6 %collective-permute-start = (bf16[513,384]{1,0:T(8,128)(2,1)}, bf16[513,384]{1,0:T(8,128)(2,1)}, u32[]{:S(2)}, u32[]{:S(2)}) collective-permute-start(bf16[513,384]{1,0:T(8,128)(2,1)} %copy.78), channel_id=1, source_target_pairs={{0,8},{8,16},{16,24},{24,32},{32,40},{40,48},{48,56},{56,64},{64,7... | collective-permute-start | bytes 1181960 | tf_op jit(solution)/shard_map/while/body/eval_jaxpr/ppermute | solution.py:21
  480.8 13.5 %collective-permute-start = (bf16[513,384]{1,0:T(8,128)(2,1)}, bf16[513,384]{1,0:T(8,128)(2,1)}, u32[]{:S(2)}, u32[]{:S(2)}) collective-permute-start(bf16[513,384]{1,0:T(8,128)(2,1)} %copy.78), channel_id=1, source_target_pairs={{0,8},{8,16},{16,24},{24,32},{32,40},{40,48},{48,56},{56,64},{64,7... | collective-permute-start | bytes 1181960 | tf_op jit(solution)/shard_map/while/body/eval_jaxpr/ppermute | solution.py:21
  (24 other events, 978.3 us)
Sparse Core Ops, SparseCore 0:
  503.5 148.0 reduce-scatter.3

commit v2 on v1

v2 whole, which is shorter than its diff:
```python
import math

import jax
import jax.numpy as jnp
from jax import lax
from jax.sharding import Mesh, PartitionSpec as P

D = 3072
HEAD_DIM = 96
PAGE = 128


far_index = 1073741824
masked_score = -1e30
norm_epsilon = 1e-05


def passed_along(block, axis, distance):
    devices = range(lax.axis_size(axis))
    route = [(i - distance, i) for i in devices if i - distance in devices]
    return lax.ppermute(block, axis, route)


def rotate(values_in, position, head_count, head_dim):
    count_rows = values_in.shape[0]
    half_dim = head_dim // 2
    frequency = jnp.exp(
        jnp.arange(half_dim, dtype=jnp.float32) * (-2.0 * math.log(10000.0) / head_dim)
    )
    angles = position.astype(jnp.float32)[:, None] * frequency[None, :]
    cosine = jnp.cos(angles)[:, None, :]
    sine_part = jnp.sin(angles)[:, None, :]
    as_float = values_in.astype(jnp.float32).reshape(count_rows, head_count, head_dim)
    lower_half = as_float[..., :half_dim]
    upper_half = as_float[..., half_dim:]
    rotated = jnp.concatenate(
        [
            lower_half * cosine - upper_half * sine_part,
            upper_half * cosine + lower_half * sine_part,
        ],
        axis=-1,
    )
    return rotated.reshape(count_rows, head_count * head_dim).astype(jnp.bfloat16)


def attend(softmax_state, query_heads, key_heads, val_heads, visible):
    row_peak, row_total, weighted = softmax_state
    factor = 1.0 / math.sqrt(HEAD_DIM)
    logits = (
        jnp.einsum("qd,kd->qk", query_heads, key_heads, preferred_element_type=jnp.float32)
        * factor
    )
    logits = jnp.where(visible, logits, masked_score)
    new_peak = jnp.maximum(row_peak, jnp.max(logits, axis=-1))
    rescale = jnp.exp(row_peak - new_peak)
    unnormed = jnp.where(visible, jnp.exp(logits - new_peak[..., None]), 0.0)
    row_total = row_total * rescale + jnp.sum(unnormed, axis=-1)
    weighted = weighted * rescale[..., None] + jnp.einsum(
        "qk,kd->qd", unnormed.astype(jnp.bfloat16), val_heads, preferred_element_type=jnp.float32
    )
    return (new_peak, row_total, weighted)


def per_device(
    query_proj,
    key_proj,
    value_proj,
    hidden,
    out_weight,
    norm_gain,
    segment_ids,
    pad_mask,
    page_table,
):
    tok_count = query_proj.shape[0]
    feat_count = query_proj.shape[1]
    head_count = feat_count // HEAD_DIM
    lo_count = lax.axis_size("seq_lo")
    hi_count = lax.axis_size("seq_hi")
    seq_axes = ("seq_hi", "seq_lo")
    seg_count = lo_count * hi_count // 2
    device_row = lax.axis_index("seq_hi") * lo_count + lax.axis_index("seq_lo")
    tok_index = device_row * tok_count + jnp.arange(tok_count, dtype=jnp.int32)
    member = segment_ids[:, None] == jnp.arange(seg_count, dtype=jnp.int32)[None, :]
    local_first = jnp.min(jnp.where(member, tok_index[:, None], far_index), axis=0)
    first_tok = lax.pmin(local_first, seq_axes)
    position = tok_index - jnp.sum(jnp.where(member, first_tok[None, :], 0), axis=1)
    q_rot = rotate(query_proj, position, head_count, HEAD_DIM)
    k_rot = rotate(key_proj, position, head_count, HEAD_DIM)
    query_tag = segment_ids + 1
    key_tag = jnp.where(pad_mask == 1, segment_ids + 1, 0)

    tags = jnp.stack([key_tag, query_tag], axis=-1).astype(jnp.bfloat16)
    payload = jnp.concatenate(
        [
            q_rot.reshape(tok_count, head_count, HEAD_DIM),
            k_rot.reshape(tok_count, head_count, HEAD_DIM),
            value_proj.reshape(tok_count, head_count, HEAD_DIM),
            jnp.broadcast_to(tags[:, None, :], (tok_count, head_count, 2)),
        ],
        axis=-1,
    ).transpose(1, 0, 2)
    chunk = lax.all_to_all(payload, "seq_lo", 0, 0, tiled=True)
    chunk_count = lo_count * tok_count
    chunk = chunk.reshape(chunk_count, 3 * HEAD_DIM + 2)
    chunk_q = chunk[:, :HEAD_DIM]
    chunk_k = chunk[:, HEAD_DIM : 2 * HEAD_DIM]
    chunk_v = chunk[:, 2 * HEAD_DIM : 3 * HEAD_DIM]
    chunk_ktag = chunk[:, 3 * HEAD_DIM]
    chunk_qtag = chunk[:, 3 * HEAD_DIM + 1]
    ring_own = chunk[:, HEAD_DIM : 3 * HEAD_DIM + 1]

    offsets = jnp.arange(chunk_count, dtype=jnp.int32)
    own_visible = (chunk_ktag[None, :] == chunk_qtag[:, None]) & (
        offsets[None, :] <= offsets[:, None]
    ) | (offsets[None, :] == offsets[:, None])
    softmax_state = (
        jnp.full((chunk_count,), masked_score, jnp.float32),
        jnp.zeros((chunk_count,), jnp.float32),
        jnp.zeros((chunk_count, HEAD_DIM), jnp.float32),
    )
    softmax_state = attend(softmax_state, chunk_q, chunk_k, chunk_v, own_visible)

    def visit_block(current, moved):
        visible = moved[:, 2 * HEAD_DIM][None, :] == chunk_qtag[:, None]
        return attend(
            current, chunk_q, moved[:, :HEAD_DIM], moved[:, HEAD_DIM : 2 * HEAD_DIM], visible
        )

    def cycle_turn(turn_index, loop_state):
        current, moved = loop_state
        following = passed_along(moved, "seq_hi", 1)
        return (visit_block(current, moved), following)

    reach_count = lo_count * hi_count // 2 * tok_count // chunk_count
    moved = passed_along(ring_own, "seq_hi", 1)
    softmax_state, moved = lax.fori_loop(0, reach_count - 1, cycle_turn, (softmax_state, moved))
    softmax_state = visit_block(softmax_state, moved)
    row_peak, row_total, weighted = softmax_state
    chunk_attn = (weighted / row_total[:, None]).astype(jnp.bfloat16)
    back = lax.all_to_all(
        chunk_attn.reshape(lo_count, tok_count, HEAD_DIM), "seq_lo", 0, 0, tiled=True
    )
    attn = back.transpose(1, 0, 2).reshape(tok_count, feat_count)
    partial_value = jnp.dot(attn, out_weight, preferred_element_type=jnp.float32)
    feature_width = hidden.shape[1]
    tp_count = lax.axis_size("tp")
    pieces = (
        partial_value.astype(jnp.bfloat16)
        .reshape(tok_count, tp_count, feature_width)
        .transpose(1, 0, 2)
    )
    gathered = lax.all_to_all(pieces, "tp", 0, 0, tiled=True)
    own_sum = jnp.sum(gathered.astype(jnp.float32), axis=0)
    hidden_out = (hidden.astype(jnp.float32) + own_sum).astype(jnp.bfloat16)
    stream_wide = hidden_out.astype(jnp.float32)
    square_total = lax.psum(jnp.sum(stream_wide * stream_wide, axis=1), "tp")
    normed = (
        stream_wide
        * lax.rsqrt(square_total / D + norm_epsilon)[:, None]
        * norm_gain.astype(jnp.float32)[None, :]
    ).astype(jnp.bfloat16)
    pad_scale = pad_mask.astype(jnp.bfloat16)[:, None]
    page_count = tok_count // PAGE
    stacked = jnp.stack([k_rot * pad_scale, value_proj * pad_scale])
    stacked = stacked.reshape(2, page_count, PAGE, feat_count).transpose(1, 0, 2, 3)
    kv_pages = jnp.zeros_like(stacked).at[page_table].set(stacked)
    return (hidden_out, normed, kv_pages)


def solution(mesh):
    seq_count = mesh.shape["seq"]
    head_count = D // mesh.shape["tp"] // HEAD_DIM
    grouped = Mesh(
        mesh.devices.reshape(seq_count // head_count, head_count, mesh.shape["tp"]),
        ("seq_hi", "seq_lo", "tp"),
    )
    rows = ("seq_hi", "seq_lo")
    placed = (
        P(rows, "tp"),
        P(rows, "tp"),
        P(rows, "tp"),
        P(rows, "tp"),
        P("tp", None),
        P("tp"),
        P(rows),
        P(rows),
        P(rows),
    )
    return jax.shard_map(
        per_device,
        mesh=grouped,
        in_specs=placed,
        out_specs=(P(rows, "tp"), P(rows, "tp"), P(rows, None, None, "tp")),
        check_vma=False,
    )
```

time: 684 us -> 323 us (0.47)
  the two profiles are of different devices: /device:TPU:8 before, /device:TPU:48 now
where the time goes in v2:
time: 323 us; the launch traced here: 322 us
  starting transfers between devices  84.6 us (26%)
  waiting for transfers between devices  84.4 us (26%)
  blocking collectives  56.9 us (18%)
  matrix products  50.8 us (16%)
  local copies, waits for them, and re-layouts  24.5 us (8%)
  other arithmetic  19.2 us (6%)
    ppermute x8, starting transfers between devices, passed_along(): return lax.ppermute(block, axis, route)  60.6 us
    ppermute x8, waiting for transfers between devices, passed_along(): return lax.ppermute(block, axis, route)  55.5 us
    dot_general x9, matrix products, attend(): jnp.einsum('qk,kd->qd', unnormed.astype(jnp.bfloat16), val_heads, preferr...  34.5 us
    pmin x1, blocking collectives, per_device(): first_tok = lax.pmin(local_first, seq_axes)  25.1 us
    all_to_all x1, starting transfers between devices, per_device(): gathered = lax.all_to_all(pieces, 'tp', 0, 0, tiled=True)  20.5 us
    all_to_all x1, waiting for transfers between devices, per_device(): gathered = lax.all_to_all(pieces, 'tp', 0, 0, tiled=True)  19.2 us
    psum x1, blocking collectives, per_device(): square_total = lax.psum(jnp.sum(stream_wide * stream_wide, axis=1), 'tp')  17.4 us
    dot_general x9, matrix products, attend(): jnp.einsum('qd,kd->qk', query_heads, key_heads, preferred_element_type=jn...  15.3 us
  transfers between devices with their start and end apart: 10, of which 9 were waited for; matrix products, arithmetic and copies ran while one was open for 18% of the time, Pallas kernels for 0%

profile of v2, /device:TPU:48, one launch (start us, length us, event | category | flops | bytes accessed | tf_op | source)
XLA Modules:
  0.0 321.9 jit_solution(11359111580186473750)
XLA Ops:
  1.6 25.1 %pmin.7 = s32[32]{0:T(128)S(1)} all-reduce(s32[32]{0:T(128)S(1)} %select_reduce_fusion.1), channel_id=1, replica_groups=mesh['seq_hi'=16,'seq_lo'=4,'tp'=8] {'seq_hi','seq_lo'}, use_global_device_ids=true, to_apply=%region_1.2 | all-reduce | flops 32 | bytes 256 | tf_op jit(solution)/shard_map/pmin | solution.py:86
  37.0 9.7 %all-to-all-done = bf16[4,256,290]{1,2,0:T(8,128)(2,1)S(1)} async-done(((bf16[4,256,290]{1,2,0:T(8,128)(2,1)}), bf16[4,256,290]{1,2,0:T(8,128)(2,1)S(1)}, u32[]{:S(2)}, u32[]{:S(2)}) %all-to-all-start) | async-done | bytes 593952 | tf_op jit(solution)/shard_map/all_to_all | solution.py:103
  52.5 5.6 %collective-permute-start.1 = (bf16[1024,193]{0,1:T(8,128)(2,1)}, bf16[1024,193]{0,1:T(8,128)(2,1)S(1)}, u32[]{:S(2)}, u32[]{:S(2)}) collective-permute-start(bf16[1024,193]{0,1:T(8,128)(2,1)} %slice.70), channel_id=1, source_target_pairs={{0,32},{32,64},{64,96},{96,128},{128,160},{160,192},{192,224},{224... | collective-permute-start | bytes 1185800 | tf_op jit(solution)/shard_map/ppermute | solution.py:21
  63.9 10.8 %collective-permute-done.1 = bf16[1024,193]{0,1:T(8,128)(2,1)S(1)} collective-permute-done((bf16[1024,193]{0,1:T(8,128)(2,1)}, bf16[1024,193]{0,1:T(8,128)(2,1)S(1)}, u32[]{:S(2)}, u32[]{:S(2)}) %collective-permute-start.1) | collective-permute-done | bytes 395296 | tf_op jit(solution)/shard_map/ppermute | solution.py:21
  74.7 164.1 %while.16 = (s32[]{:T(128)}, f32[1024]{0:T(1024)S(1)}, f32[1024]{0:T(1024)S(1)}, f32[1024,96]{0,1:T(8,128)}, bf16[1024,193]{0,1:T(8,128)(2,1)S(1)}, /*index=5*/b...) while((s32[]{:T(128)}, f32[1024]{0:T(1024)S(1)}, f32[1024]{0:T(1024)S(1)}, ...), condition=%wide.region_8.9_spmd, body=%wide.region_5.8_spmd.sunk | while | flops 419629056 | bytes 33194148 | solution.py:137
  74.7 9.2 %collective-permute-start = (bf16[1024,193]{0,1:T(8,128)(2,1)S(1)}, bf16[1024,193]{0,1:T(8,128)(2,1)S(1)}, u32[]{:S(2)}, u32[]{:S(2)}) collective-permute-start(bf16[1024,193]{0,1:T(8,128)(2,1)S(1)} %copy.77), channel_id=1, source_target_pairs={{0,32},{32,64},{64,96},{96,128},{128,160},{160,192},{192,224},{224... | collective-permute-start | bytes 1185800 | tf_op jit(solution)/shard_map/while/body/eval_jaxpr/ppermute | solution.py:21
  93.1 6.2 %collective-permute-done = bf16[1024,193]{0,1:T(8,128)(2,1)S(1)} collective-permute-done((bf16[1024,193]{0,1:T(8,128)(2,1)S(1)}, bf16[1024,193]{0,1:T(8,128)(2,1)S(1)}, u32[]{:S(2)}, u32[]{:S(2)}) %collective-permute-start) | collective-permute-done | bytes 395296 | tf_op jit(solution)/shard_map/while/body/eval_jaxpr/ppermute | solution.py:21
  99.3 11.8 %collective-permute-start = (bf16[1024,193]{0,1:T(8,128)(2,1)S(1)}, bf16[1024,193]{0,1:T(8,128)(2,1)S(1)}, u32[]{:S(2)}, u32[]{:S(2)}) collective-permute-start(bf16[1024,193]{0,1:T(8,128)(2,1)S(1)} %copy.77), channel_id=1, source_target_pairs={{0,32},{32,64},{64,96},{96,128},{128,160},{160,192},{192,224},{224... | collective-permute-start | bytes 1185800 | tf_op jit(solution)/shard_map/while/body/eval_jaxpr/ppermute | solution.py:21
  120.3 9.4 %collective-permute-done = bf16[1024,193]{0,1:T(8,128)(2,1)S(1)} collective-permute-done((bf16[1024,193]{0,1:T(8,128)(2,1)S(1)}, bf16[1024,193]{0,1:T(8,128)(2,1)S(1)}, u32[]{:S(2)}, u32[]{:S(2)}) %collective-permute-start) | collective-permute-done | bytes 395296 | tf_op jit(solution)/shard_map/while/body/eval_jaxpr/ppermute | solution.py:21
  129.7 8.4 %collective-permute-start = (bf16[1024,193]{0,1:T(8,128)(2,1)S(1)}, bf16[1024,193]{0,1:T(8,128)(2,1)S(1)}, u32[]{:S(2)}, u32[]{:S(2)}) collective-permute-start(bf16[1024,193]{0,1:T(8,128)(2,1)S(1)} %copy.77), channel_id=1, source_target_pairs={{0,32},{32,64},{64,96},{96,128},{128,160},{160,192},{192,224},{224... | collective-permute-start | bytes 1185800 | tf_op jit(solution)/shard_map/while/body/eval_jaxpr/ppermute | solution.py:21
  147.3 9.3 %collective-permute-done = bf16[1024,193]{0,1:T(8,128)(2,1)S(1)} collective-permute-done((bf16[1024,193]{0,1:T(8,128)(2,1)S(1)}, bf16[1024,193]{0,1:T(8,128)(2,1)S(1)}, u32[]{:S(2)}, u32[]{:S(2)}) %collective-permute-start) | collective-permute-done | bytes 395296 | tf_op jit(solution)/shard_map/while/body/eval_jaxpr/ppermute | solution.py:21
  156.6 4.2 %collective-permute-start = (bf16[1024,193]{0,1:T(8,128)(2,1)S(1)}, bf16[1024,193]{0,1:T(8,128)(2,1)S(1)}, u32[]{:S(2)}, u32[]{:S(2)}) collective-permute-start(bf16[1024,193]{0,1:T(8,128)(2,1)S(1)} %copy.77), channel_id=1, source_target_pairs={{0,32},{32,64},{64,96},{96,128},{128,160},{160,192},{192,224},{224... | collective-permute-start | bytes 1185800 | tf_op jit(solution)/shard_map/while/body/eval_jaxpr/ppermute | solution.py:21
  170.0 7.6 %collective-permute-done = bf16[1024,193]{0,1:T(8,128)(2,1)S(1)} collective-permute-done((bf16[1024,193]{0,1:T(8,128)(2,1)S(1)}, bf16[1024,193]{0,1:T(8,128)(2,1)S(1)}, u32[]{:S(2)}, u32[]{:S(2)}) %collective-permute-start) | collective-permute-done | bytes 395296 | tf_op jit(solution)/shard_map/while/body/eval_jaxpr/ppermute | solution.py:21
  177.6 6.1 %collective-permute-start = (bf16[1024,193]{0,1:T(8,128)(2,1)S(1)}, bf16[1024,193]{0,1:T(8,128)(2,1)S(1)}, u32[]{:S(2)}, u32[]{:S(2)}) collective-permute-start(bf16[1024,193]{0,1:T(8,128)(2,1)S(1)} %copy.77), channel_id=1, source_target_pairs={{0,32},{32,64},{64,96},{96,128},{128,160},{160,192},{192,224},{224... | collective-permute-start | bytes 1185800 | tf_op jit(solution)/shard_map/while/body/eval_jaxpr/ppermute | solution.py:21
  192.8 4.5 %collective-permute-done = bf16[1024,193]{0,1:T(8,128)(2,1)S(1)} collective-permute-done((bf16[1024,193]{0,1:T(8,128)(2,1)S(1)}, bf16[1024,193]{0,1:T(8,128)(2,1)S(1)}, u32[]{:S(2)}, u32[]{:S(2)}) %collective-permute-start) | collective-permute-done | bytes 395296 | tf_op jit(solution)/shard_map/while/body/eval_jaxpr/ppermute | solution.py:21
  197.3 10.6 %collective-permute-start = (bf16[1024,193]{0,1:T(8,128)(2,1)S(1)}, bf16[1024,193]{0,1:T(8,128)(2,1)S(1)}, u32[]{:S(2)}, u32[]{:S(2)}) collective-permute-start(bf16[1024,193]{0,1:T(8,128)(2,1)S(1)} %copy.77), channel_id=1, source_target_pairs={{0,32},{32,64},{64,96},{96,128},{128,160},{160,192},{192,224},{224... | collective-permute-start | bytes 1185800 | tf_op jit(solution)/shard_map/while/body/eval_jaxpr/ppermute | solution.py:21
  212.9 4.2 %fusion.74 = f32[1024,96]{0,1:T(8,128)} fusion(f32[1024,1024]{0,1:T(8,128)} %copy-done.1, f32[1024]{0:T(1024)S(1)} %max.8, bf16[1024]{0:T(1024)(128)(2,1)S(1)} %reduce.12, bf16[1024]{0:T(1024)(128)(2,1)S(1)} %slice_reduce_fusion.5, f32[1024,96]{0,1:T(8,128)} %get-tuple-element.186, bf16[1024,193]{0,1:T(8,128)(2,1)S(1)} %copy.77, ...), kind=kOutput, calls=%fused_computation.7.clone.1 | convolution fusion | flops 207814656 | bytes 5189632 | tf_op jit(solution)/shard_map/while/body/eval_jaxpr/qk,kd->qd/dot_general | solution.py:58
  217.1 7.9 %collective-permute-done = bf16[1024,193]{0,1:T(8,128)(2,1)S(1)} collective-permute-done((bf16[1024,193]{0,1:T(8,128)(2,1)S(1)}, bf16[1024,193]{0,1:T(8,128)(2,1)S(1)}, u32[]{:S(2)}, u32[]{:S(2)}) %collective-permute-start) | collective-permute-done | bytes 395296 | tf_op jit(solution)/shard_map/while/body/eval_jaxpr/ppermute | solution.py:21
  225.0 4.6 %collective-permute-start = (bf16[1024,193]{0,1:T(8,128)(2,1)S(1)}, bf16[1024,193]{0,1:T(8,128)(2,1)S(1)}, u32[]{:S(2)}, u32[]{:S(2)}) collective-permute-start(bf16[1024,193]{0,1:T(8,128)(2,1)S(1)} %copy.77), channel_id=1, source_target_pairs={{0,32},{32,64},{64,96},{96,128},{128,160},{160,192},{192,224},{224... | collective-permute-start | bytes 1185800 | tf_op jit(solution)/shard_map/while/body/eval_jaxpr/ppermute | solution.py:21
  234.6 4.2 %fusion.74 = f32[1024,96]{0,1:T(8,128)} fusion(f32[1024,1024]{0,1:T(8,128)} %copy-done.1, f32[1024]{0:T(1024)S(1)} %max.8, bf16[1024]{0:T(1024)(128)(2,1)S(1)} %reduce.12, bf16[1024]{0:T(1024)(128)(2,1)S(1)} %slice_reduce_fusion.5, f32[1024,96]{0,1:T(8,128)} %get-tuple-element.186, bf16[1024,193]{0,1:T(8,128)(2,1)S(1)} %copy.77, ...), kind=kOutput, calls=%fused_computation.7.clone.1 | convolution fusion | flops 207814656 | bytes 5189632 | tf_op jit(solution)/shard_map/while/body/eval_jaxpr/qk,kd->qd/dot_general | solution.py:58
  243.1 14.4 %all_to_all.15 = bf16[4,256,96]{1,2,0:T(8,128)(2,1)S(1)} all-to-all(bf16[4,256,96]{1,2,0:T(8,128)(2,1)S(1)} %bitcast.55), channel_id=1, replica_groups=mesh['seq_hi'=16,'seq_lo'=4,'tp'=8] {'seq_lo'}, dimensions={0} | all-to-all | bytes 393216 | tf_op jit(solution)/shard_map/all_to_all | solution.py:141
  259.9 20.5 %all-to-all-start.2 = ((bf16[8,256,384]{2,1,0:T(8,128)(2,1)}), bf16[8,256,384]{2,1,0:T(8,128)(2,1)}, u32[]{:S(2)}, u32[]{:S(2)}) async-start(bf16[8,256,384]{2,1,0:T(8,128)(2,1)} %bitcast.41), calls=%async_computation.2 | async-start | bytes 3145728 | tf_op jit(solution)/shard_map/all_to_all | solution.py:153
  282.6 19.2 %all-to-all-done.2 = bf16[8,256,384]{2,1,0:T(8,128)(2,1)} async-done(((bf16[8,256,384]{2,1,0:T(8,128)(2,1)}), bf16[8,256,384]{2,1,0:T(8,128)(2,1)}, u32[]{:S(2)}, u32[]{:S(2)}) %all-to-all-start.2) | async-done | bytes 1572896 | tf_op jit(solution)/shard_map/all_to_all | solution.py:153
  303.6 17.4 %psum.7 = f32[256]{0:T(256)S(1)} all-reduce(f32[256]{0:T(256)S(1)} %get-tuple-element.100), channel_id=1, replica_groups=mesh['seq_hi'=16,'seq_lo'=4,'tp'=8] {'tp'}, use_global_device_ids=true, to_apply=%region_13.14 | all-reduce | flops 256 | bytes 2048 | tf_op jit(solution)/shard_map/psum | solution.py:157
  (157 shorter events, 89.6 us)
Async XLA Ops:
  0.6 256.9 %copy-start = (bf16[384,3072]{1,0:T(8,128)(2,1)S(1)}, bf16[384,3072]{1,0:T(8,128)(2,1)}, u32[]{:S(2)}) copy-start(bf16[384,3072]{1,0:T(8,128)(2,1)} %param.15) | copy-start | bytes 7077892
  33.5 13.1 %all-to-all-start = ((bf16[4,256,290]{1,2,0:T(8,128)(2,1)}), bf16[4,256,290]{1,2,0:T(8,128)(2,1)S(1)}, u32[]{:S(2)}, u32[]{:S(2)}) async-start(bf16[4,256,290]{1,2,0:T(8,128)(2,1)} %bitcast.51), calls=%async_computation | async-start | bytes 1212416 | tf_op jit(solution)/shard_map/all_to_all | solution.py:103
  47.2 12.7 %copy-start.3 = (bf16[37,8,4,256]{3,1,2,0:T(8,128)(2,1)}, bf16[37,8,4,256]{3,1,2,0:T(8,128)(2,1)S(1)}, u32[]{:S(2)}) copy-start(bf16[37,8,4,256]{3,1,2,0:T(8,128)(2,1)S(1)} %copy.57) | copy-start | bytes 1818628
  49.8 2.7 copy-start.2
  52.5 22.2 %collective-permute-start.1 = (bf16[1024,193]{0,1:T(8,128)(2,1)}, bf16[1024,193]{0,1:T(8,128)(2,1)S(1)}, u32[]{:S(2)}, u32[]{:S(2)}) collective-permute-start(bf16[1024,193]{0,1:T(8,128)(2,1)} %slice.70), channel_id=1, source_target_pairs={{0,32},{32,64},{64,96},{96,128},{128,160},{160,192},{192,224},{224... | collective-permute-start | bytes 1185800 | tf_op jit(solution)/shard_map/ppermute | solution.py:21
  74.7 24.6 %collective-permute-start = (bf16[1024,193]{0,1:T(8,128)(2,1)S(1)}, bf16[1024,193]{0,1:T(8,128)(2,1)S(1)}, u32[]{:S(2)}, u32[]{:S(2)}) collective-permute-start(bf16[1024,193]{0,1:T(8,128)(2,1)S(1)} %copy.77), channel_id=1, source_target_pairs={{0,32},{32,64},{64,96},{96,128},{128,160},{160,192},{192,224},{224... | collective-permute-start | bytes 1185800 | tf_op jit(solution)/shard_map/while/body/eval_jaxpr/ppermute | solution.py:21
  99.3 30.4 %collective-permute-start = (bf16[1024,193]{0,1:T(8,128)(2,1)S(1)}, bf16[1024,193]{0,1:T(8,128)(2,1)S(1)}, u32[]{:S(2)}, u32[]{:S(2)}) collective-permute-start(bf16[1024,193]{0,1:T(8,128)(2,1)S(1)} %copy.77), channel_id=1, source_target_pairs={{0,32},{32,64},{64,96},{96,128},{128,160},{160,192},{192,224},{224... | collective-permute-start | bytes 1185800 | tf_op jit(solution)/shard_map/while/body/eval_jaxpr/ppermute | solution.py:21
  113.0 1.9 copy-start.1
  129.7 26.8 %collective-permute-start = (bf16[1024,193]{0,1:T(8,128)(2,1)S(1)}, bf16[1024,193]{0,1:T(8,128)(2,1)S(1)}, u32[]{:S(2)}, u32[]{:S(2)}) collective-permute-start(bf16[1024,193]{0,1:T(8,128)(2,1)S(1)} %copy.77), channel_id=1, source_target_pairs={{0,32},{32,64},{64,96},{96,128},{128,160},{160,192},{192,224},{224... | collective-permute-start | bytes 1185800 | tf_op jit(solution)/shard_map/while/body/eval_jaxpr/ppermute | solution.py:21
  156.6 21.0 %collective-permute-start = (bf16[1024,193]{0,1:T(8,128)(2,1)S(1)}, bf16[1024,193]{0,1:T(8,128)(2,1)S(1)}, u32[]{:S(2)}, u32[]{:S(2)}) collective-permute-start(bf16[1024,193]{0,1:T(8,128)(2,1)S(1)} %copy.77), channel_id=1, source_target_pairs={{0,32},{32,64},{64,96},{96,128},{128,160},{160,192},{192,224},{224... | collective-permute-start | bytes 1185800 | tf_op jit(solution)/shard_map/while/body/eval_jaxpr/ppermute | solution.py:21
  162.7 1.9 copy-start.1
  177.6 19.7 %collective-permute-start = (bf16[1024,193]{0,1:T(8,128)(2,1)S(1)}, bf16[1024,193]{0,1:T(8,128)(2,1)S(1)}, u32[]{:S(2)}, u32[]{:S(2)}) collective-permute-start(bf16[1024,193]{0,1:T(8,128)(2,1)S(1)} %copy.77), channel_id=1, source_target_pairs={{0,32},{32,64},{64,96},{96,128},{128,160},{160,192},{192,224},{224... | collective-permute-start | bytes 1185800 | tf_op jit(solution)/shard_map/while/body/eval_jaxpr/ppermute | solution.py:21
  185.5 1.9 copy-start.1
  197.3 27.6 %collective-permute-start = (bf16[1024,193]{0,1:T(8,128)(2,1)S(1)}, bf16[1024,193]{0,1:T(8,128)(2,1)S(1)}, u32[]{:S(2)}, u32[]{:S(2)}) collective-permute-start(bf16[1024,193]{0,1:T(8,128)(2,1)S(1)} %copy.77), channel_id=1, source_target_pairs={{0,32},{32,64},{64,96},{96,128},{128,160},{160,192},{192,224},{224... | collective-permute-start | bytes 1185800 | tf_op jit(solution)/shard_map/while/body/eval_jaxpr/ppermute | solution.py:21
  225.0 13.8 %collective-permute-start = (bf16[1024,193]{0,1:T(8,128)(2,1)S(1)}, bf16[1024,193]{0,1:T(8,128)(2,1)S(1)}, u32[]{:S(2)}, u32[]{:S(2)}) collective-permute-start(bf16[1024,193]{0,1:T(8,128)(2,1)S(1)} %copy.77), channel_id=1, source_target_pairs={{0,32},{32,64},{64,96},{96,128},{128,160},{160,192},{192,224},{224... | collective-permute-start | bytes 1185800 | tf_op jit(solution)/shard_map/while/body/eval_jaxpr/ppermute | solution.py:21
  238.8 3.0 copy-start.12
  257.5 22.9 %copy-start.10 = (bf16[384]{0:T(512)(128)(2,1)S(1)}, bf16[384]{0:T(512)(128)(2,1)}, u32[]{:S(2)}) copy-start(bf16[384]{0:T(512)(128)(2,1)} %param.16) | copy-start | bytes 2308
  257.5 22.9 %copy-start.7 = (bf16[256,4,96]{0,2,1:T(8,128)(2,1)S(1)}, bf16[256,4,96]{0,2,1:T(8,128)(2,1)}, u32[]{:S(2)}) copy-start(bf16[256,4,96]{0,2,1:T(8,128)(2,1)} %get-tuple-element.105) | copy-start | bytes 589828
  258.5 21.9 %copy-start.6 = (bf16[256,384]{1,0:T(8,128)(2,1)S(1)}, bf16[256,384]{1,0:T(8,128)(2,1)}, u32[]{:S(2)}) copy-start(bf16[256,384]{1,0:T(8,128)(2,1)} %param.13) | copy-start | bytes 589828
  258.5 23.3 %copy-start.11 = (s32[2]{0:T(128)S(1)}, s32[2]{0:T(128)}, u32[]{:S(2)}) copy-start(s32[2]{0:T(128)} %param.19) | copy-start | bytes 28
  259.9 43.6 %copy-start.9 = (bf16[256,384]{1,0:T(8,128)(2,1)S(1)}, bf16[256,384]{1,0:T(8,128)(2,1)}, u32[]{:S(2)}) copy-start(bf16[256,384]{1,0:T(8,128)(2,1)} %param.14) | copy-start | bytes 589828
  259.9 41.9 %all-to-all-start.2 = ((bf16[8,256,384]{2,1,0:T(8,128)(2,1)}), bf16[8,256,384]{2,1,0:T(8,128)(2,1)}, u32[]{:S(2)}, u32[]{:S(2)}) async-start(bf16[8,256,384]{2,1,0:T(8,128)(2,1)} %bitcast.41), calls=%async_computation.2 | async-start | bytes 3145728 | tf_op jit(solution)/shard_map/all_to_all | solution.py:153
  282.6 39.3 %copy-start.4 = (bf16[2,2,128,384]{3,2,1,0:T(8,128)(2,1)}, bf16[2,2,128,384]{3,2,1,0:T(8,128)(2,1)S(1)}, u32[]{:S(2)}) copy-start(bf16[2,2,128,384]{3,2,1,0:T(8,128)(2,1)S(1)} %scatter_fusion) | copy-start | bytes 1179652
  303.6 18.3 %copy-start.8 = (bf16[256,384]{1,0:T(8,128)(2,1)}, bf16[256,384]{1,0:T(8,128)(2,1)S(1)}, u32[]{:S(2)}) copy-start(bf16[256,384]{1,0:T(8,128)(2,1)S(1)} %get-tuple-element.101) | copy-start | bytes 589828
  (5 other events, 8.5 us)

commit v3 on v2

--- a/solution.py
+++ b/solution.py
@@ -77,24 +77,24 @@
     head_count = feat_count // HEAD_DIM
     lo_count = lax.axis_size("seq_lo")
     hi_count = lax.axis_size("seq_hi")
-    seq_axes = ("seq_hi", "seq_lo")
     seg_count = lo_count * hi_count // 2
     device_row = lax.axis_index("seq_hi") * lo_count + lax.axis_index("seq_lo")
     tok_index = device_row * tok_count + jnp.arange(tok_count, dtype=jnp.int32)
-    member = segment_ids[:, None] == jnp.arange(seg_count, dtype=jnp.int32)[None, :]
-    local_first = jnp.min(jnp.where(member, tok_index[:, None], far_index), axis=0)
-    first_tok = lax.pmin(local_first, seq_axes)
-    position = tok_index - jnp.sum(jnp.where(member, first_tok[None, :], 0), axis=1)
-    q_rot = rotate(query_proj, position, head_count, HEAD_DIM)
-    k_rot = rotate(key_proj, position, head_count, HEAD_DIM)
+    q_rot = rotate(query_proj, tok_index, head_count, HEAD_DIM)
+    k_abs = rotate(key_proj, tok_index, head_count, HEAD_DIM)
     query_tag = segment_ids + 1
     key_tag = jnp.where(pad_mask == 1, segment_ids + 1, 0)
+    seg_tags = jnp.arange(1, seg_count + 1, dtype=jnp.int32)
+
+    def first_of(tag_values, index_values):
+        hit = tag_values[:, None] == seg_tags[None, :].astype(tag_values.dtype)
+        return jnp.min(jnp.where(hit, index_values[:, None], far_index), axis=0)
 
     tags = jnp.stack([key_tag, query_tag], axis=-1).astype(jnp.bfloat16)
     payload = jnp.concatenate(
         [
             q_rot.reshape(tok_count, head_count, HEAD_DIM),
-            k_rot.reshape(tok_count, head_count, HEAD_DIM),
+            k_abs.reshape(tok_count, head_count, HEAD_DIM),
             value_proj.reshape(tok_count, head_count, HEAD_DIM),
             jnp.broadcast_to(tags[:, None, :], (tok_count, head_count, 2)),
         ],
@@ -108,7 +108,9 @@
     chunk_v = chunk[:, 2 * HEAD_DIM : 3 * HEAD_DIM]
     chunk_ktag = chunk[:, 3 * HEAD_DIM]
     chunk_qtag = chunk[:, 3 * HEAD_DIM + 1]
-    ring_own = chunk[:, HEAD_DIM : 3 * HEAD_DIM + 1]
+    ring_own = chunk[:, HEAD_DIM : 3 * HEAD_DIM + 2]
+    chunk_row = lax.axis_index("seq_hi")
+    chunk_offsets = jnp.arange(chunk_count, dtype=jnp.int32)
 
     offsets = jnp.arange(chunk_count, dtype=jnp.int32)
     own_visible = (chunk_ktag[None, :] == chunk_qtag[:, None]) & (
@@ -121,21 +123,31 @@
     )
     softmax_state = attend(softmax_state, chunk_q, chunk_k, chunk_v, own_visible)
 
-    def visit_block(current, moved):
+    def visit_block(current, moved, distance):
+        state, seen_first = current
         visible = moved[:, 2 * HEAD_DIM][None, :] == chunk_qtag[:, None]
-        return attend(
-            current, chunk_q, moved[:, :HEAD_DIM], moved[:, HEAD_DIM : 2 * HEAD_DIM], visible
+        state = attend(
+            state, chunk_q, moved[:, :HEAD_DIM], moved[:, HEAD_DIM : 2 * HEAD_DIM], visible
         )
+        moved_index = (chunk_row - distance) * chunk_count + chunk_offsets
+        seen_first = jnp.minimum(seen_first, first_of(moved[:, 2 * HEAD_DIM + 1], moved_index))
+        return (state, seen_first)
 
     def cycle_turn(turn_index, loop_state):
         current, moved = loop_state
         following = passed_along(moved, "seq_hi", 1)
-        return (visit_block(current, moved), following)
+        return (visit_block(current, moved, turn_index + 1), following)
 
     reach_count = lo_count * hi_count // 2 * tok_count // chunk_count
+    seen_first = first_of(chunk_qtag, chunk_row * chunk_count + chunk_offsets)
     moved = passed_along(ring_own, "seq_hi", 1)
-    softmax_state, moved = lax.fori_loop(0, reach_count - 1, cycle_turn, (softmax_state, moved))
-    softmax_state = visit_block(softmax_state, moved)
+    (softmax_state, seen_first), moved = lax.fori_loop(
+        0, reach_count - 1, cycle_turn, ((softmax_state, seen_first), moved)
+    )
+    softmax_state, first_tok = visit_block((softmax_state, seen_first), moved, reach_count)
+    member = segment_ids[:, None] == jnp.arange(seg_count, dtype=jnp.int32)[None, :]
+    position = tok_index - jnp.sum(jnp.where(member, first_tok[None, :], 0), axis=1)
+    k_rot = rotate(key_proj, position, head_count, HEAD_DIM)
     row_peak, row_total, weighted = softmax_state
     chunk_attn = (weighted / row_total[:, None]).astype(jnp.bfloat16)
     back = lax.all_to_all(
@@ -154,7 +166,13 @@
     own_sum = jnp.sum(gathered.astype(jnp.float32), axis=0)
     hidden_out = (hidden.astype(jnp.float32) + own_sum).astype(jnp.bfloat16)
     stream_wide = hidden_out.astype(jnp.float32)
-    square_total = lax.psum(jnp.sum(stream_wide * stream_wide, axis=1), "tp")
+    square_part = jnp.sum(stream_wide * stream_wide, axis=1)
+    square_total = jnp.sum(
+        lax.all_to_all(
+            jnp.broadcast_to(square_part[None, :], (tp_count, tok_count)), "tp", 0, 0, tiled=True
+        ),
+        axis=0,
+    )
     normed = (
         stream_wide
         * lax.rsqrt(square_total / D + norm_epsilon)[:, None]

time: 323 us -> 294 us (0.910)
  the two profiles are of different devices: /device:TPU:48 before, /device:TPU:176 now
where the time goes in v3:
time: 294 us; the launch traced here: 293 us
  starting transfers between devices  94.8 us (32%)
  waiting for transfers between devices  93.8 us (32%)
  matrix products  50.8 us (17%)
  local copies, waits for them, and re-layouts  25.2 us (9%)
  other arithmetic  18.9 us (6%)
  blocking collectives  7.67 us (3%)
    ppermute x8, starting transfers between devices, passed_along(): return lax.ppermute(block, axis, route)  83.6 us
    ppermute x8, waiting for transfers between devices, passed_along(): return lax.ppermute(block, axis, route)  59.9 us
    dot_general x9, matrix products, attend(): jnp.einsum('qk,kd->qd', unnormed.astype(jnp.bfloat16), val_heads, preferr...  34.5 us
    all_to_all x1, waiting for transfers between devices, per_device(): gathered = lax.all_to_all(pieces, 'tp', 0, 0, tiled=True)  20 us
    dot_general x9, matrix products, attend(): jnp.einsum('qd,kd->qk', query_heads, key_heads, preferred_element_type=jn...  15.3 us
    while x28, local copies, waits for them, and re-layouts  13.6 us
    reduce_sum x9, other arithmetic, attend(): row_total = row_total * rescale + jnp.sum(unnormed, axis=-1)  12 us
    all_to_all x1, waiting for transfers between devices, per_device(): chunk = lax.all_to_all(payload, 'seq_lo', 0, 0, tiled=True)  9.62 us
  transfers between devices with their start and end apart: 11, of which 9 were waited for; matrix products, arithmetic and copies ran while one was open for 21% of the time, Pallas kernels for 0%

profile of v3, /device:TPU:176, one launch (start us, length us, event | category | flops | bytes accessed | tf_op | source)
XLA Modules:
  0.0 293.1 jit_solution(9467878183348044537)
XLA Ops:
  8.8 9.6 %all-to-all-done = bf16[4,256,290]{1,2,0:T(8,128)(2,1)S(1)} async-done(((bf16[4,256,290]{1,2,0:T(8,128)(2,1)}), bf16[4,256,290]{1,2,0:T(8,128)(2,1)S(1)}, u32[]{:S(2)}, u32[]{:S(2)}) %all-to-all-start) | async-done | bytes 593952 | tf_op jit(solution)/shard_map/all_to_all | solution.py:103
  24.3 6.8 %collective-permute-start.1 = (bf16[1024,194]{0,1:T(8,128)(2,1)}, bf16[1024,194]{0,1:T(8,128)(2,1)S(1)}, u32[]{:S(2)}, u32[]{:S(2)}) collective-permute-start(bf16[1024,194]{0,1:T(8,128)(2,1)} %slice.107), channel_id=1, source_target_pairs={{0,32},{32,64},{64,96},{96,128},{128,160},{160,192},{192,224},{224... | collective-permute-start | bytes 1191944 | tf_op jit(solution)/shard_map/ppermute | solution.py:21
  37.1 11.0 %collective-permute-done.1 = bf16[1024,194]{0,1:T(8,128)(2,1)S(1)} collective-permute-done((bf16[1024,194]{0,1:T(8,128)(2,1)}, bf16[1024,194]{0,1:T(8,128)(2,1)S(1)}, u32[]{:S(2)}, u32[]{:S(2)}) %collective-permute-start.1) | collective-permute-done | bytes 397344 | tf_op jit(solution)/shard_map/ppermute | solution.py:21
  48.1 191.8 %while.24 = (s32[]{:T(128)}, f32[1024]{0:T(1024)S(1)}, f32[1024]{0:T(1024)S(1)}, f32[1024,96]{0,1:T(8,128)}, s32[32]{0:T(128)S(1)}, /*index=5*/bf16[1024,194]{0,...) while((s32[]{:T(128)}, f32[1024]{0:T(1024)S(1)}, ...), condition=%wide.region_7.8_spmd.clone, body=%wide.region_3.7_spmd.clone.sunk | while | flops 419728448 | bytes 33221464 | solution.py:144
  48.1 11.6 %collective-permute-start = (bf16[1024,194]{0,1:T(8,128)(2,1)S(1)}, bf16[1024,194]{0,1:T(8,128)(2,1)S(1)}, u32[]{:S(2)}, u32[]{:S(2)}) collective-permute-start(bf16[1024,194]{0,1:T(8,128)(2,1)S(1)} %copy.91), channel_id=1, source_target_pairs={{0,32},{32,64},{64,96},{96,128},{128,160},{160,192},{192,224},{224... | collective-permute-start | bytes 1191944 | tf_op jit(solution)/shard_map/while/body/eval_jaxpr/ppermute | solution.py:21
  64.9 4.2 %fusion.81 = f32[1024,96]{0,1:T(8,128)} fusion(f32[1024,1024]{0,1:T(8,128)} %copy-done.1, f32[1024]{0:T(1024)S(1)} %max.15, bf16[1024]{0:T(1024)(128)(2,1)S(1)} %reduce.17, bf16[1024]{0:T(1024)(128)(2,1)S(1)} %get-tuple-element.450, f32[1024,96]{0,1:T(8,128)} %get-tuple-element.471, bf16[1024,194]{0,1:T(8,128)(2,1)S(1)} %copy.91, ...), kind=kOutput, calls=%fused_computation.9.clone.1 | convolution fusion | flops 207814656 | bytes 5189632 | tf_op jit(solution)/shard_map/while/body/eval_jaxpr/qk,kd->qd/dot_general | solution.py:58
  69.1 7.8 %collective-permute-done = bf16[1024,194]{0,1:T(8,128)(2,1)S(1)} collective-permute-done((bf16[1024,194]{0,1:T(8,128)(2,1)S(1)}, bf16[1024,194]{0,1:T(8,128)(2,1)S(1)}, u32[]{:S(2)}, u32[]{:S(2)}) %collective-permute-start) | collective-permute-done | bytes 397344 | tf_op jit(solution)/shard_map/while/body/eval_jaxpr/ppermute | solution.py:21
  77.0 10.2 %collective-permute-start = (bf16[1024,194]{0,1:T(8,128)(2,1)S(1)}, bf16[1024,194]{0,1:T(8,128)(2,1)S(1)}, u32[]{:S(2)}, u32[]{:S(2)}) collective-permute-start(bf16[1024,194]{0,1:T(8,128)(2,1)S(1)} %copy.91), channel_id=1, source_target_pairs={{0,32},{32,64},{64,96},{96,128},{128,160},{160,192},{192,224},{224... | collective-permute-start | bytes 1191944 | tf_op jit(solution)/shard_map/while/body/eval_jaxpr/ppermute | solution.py:21
  96.6 9.9 %collective-permute-done = bf16[1024,194]{0,1:T(8,128)(2,1)S(1)} collective-permute-done((bf16[1024,194]{0,1:T(8,128)(2,1)S(1)}, bf16[1024,194]{0,1:T(8,128)(2,1)S(1)}, u32[]{:S(2)}, u32[]{:S(2)}) %collective-permute-start) | collective-permute-done | bytes 397344 | tf_op jit(solution)/shard_map/while/body/eval_jaxpr/ppermute | solution.py:21
  106.6 9.5 %collective-permute-start = (bf16[1024,194]{0,1:T(8,128)(2,1)S(1)}, bf16[1024,194]{0,1:T(8,128)(2,1)S(1)}, u32[]{:S(2)}, u32[]{:S(2)}) collective-permute-start(bf16[1024,194]{0,1:T(8,128)(2,1)S(1)} %copy.91), channel_id=1, source_target_pairs={{0,32},{32,64},{64,96},{96,128},{128,160},{160,192},{192,224},{224... | collective-permute-start | bytes 1191944 | tf_op jit(solution)/shard_map/while/body/eval_jaxpr/ppermute | solution.py:21
  125.5 9.4 %collective-permute-done = bf16[1024,194]{0,1:T(8,128)(2,1)S(1)} collective-permute-done((bf16[1024,194]{0,1:T(8,128)(2,1)S(1)}, bf16[1024,194]{0,1:T(8,128)(2,1)S(1)}, u32[]{:S(2)}, u32[]{:S(2)}) %collective-permute-start) | collective-permute-done | bytes 397344 | tf_op jit(solution)/shard_map/while/body/eval_jaxpr/ppermute | solution.py:21
  135.0 12.4 %collective-permute-start = (bf16[1024,194]{0,1:T(8,128)(2,1)S(1)}, bf16[1024,194]{0,1:T(8,128)(2,1)S(1)}, u32[]{:S(2)}, u32[]{:S(2)}) collective-permute-start(bf16[1024,194]{0,1:T(8,128)(2,1)S(1)} %copy.91), channel_id=1, source_target_pairs={{0,32},{32,64},{64,96},{96,128},{128,160},{160,192},{192,224},{224... | collective-permute-start | bytes 1191944 | tf_op jit(solution)/shard_map/while/body/eval_jaxpr/ppermute | solution.py:21
  152.5 4.2 %fusion.81 = f32[1024,96]{0,1:T(8,128)} fusion(f32[1024,1024]{0,1:T(8,128)} %copy-done.1, f32[1024]{0:T(1024)S(1)} %max.15, bf16[1024]{0:T(1024)(128)(2,1)S(1)} %reduce.17, bf16[1024]{0:T(1024)(128)(2,1)S(1)} %get-tuple-element.450, f32[1024,96]{0,1:T(8,128)} %get-tuple-element.471, bf16[1024,194]{0,1:T(8,128)(2,1)S(1)} %copy.91, ...), kind=kOutput, calls=%fused_computation.9.clone.1 | convolution fusion | flops 207814656 | bytes 5189632 | tf_op jit(solution)/shard_map/while/body/eval_jaxpr/qk,kd->qd/dot_general | solution.py:58
  156.7 13.7 %collective-permute-done = bf16[1024,194]{0,1:T(8,128)(2,1)S(1)} collective-permute-done((bf16[1024,194]{0,1:T(8,128)(2,1)S(1)}, bf16[1024,194]{0,1:T(8,128)(2,1)S(1)}, u32[]{:S(2)}, u32[]{:S(2)}) %collective-permute-start) | collective-permute-done | bytes 397344 | tf_op jit(solution)/shard_map/while/body/eval_jaxpr/ppermute | solution.py:21
  170.5 9.7 %collective-permute-start = (bf16[1024,194]{0,1:T(8,128)(2,1)S(1)}, bf16[1024,194]{0,1:T(8,128)(2,1)S(1)}, u32[]{:S(2)}, u32[]{:S(2)}) collective-permute-start(bf16[1024,194]{0,1:T(8,128)(2,1)S(1)} %copy.91), channel_id=1, source_target_pairs={{0,32},{32,64},{64,96},{96,128},{128,160},{160,192},{192,224},{224... | collective-permute-start | bytes 1191944 | tf_op jit(solution)/shard_map/while/body/eval_jaxpr/ppermute | solution.py:21
  189.6 8.0 %collective-permute-done = bf16[1024,194]{0,1:T(8,128)(2,1)S(1)} collective-permute-done((bf16[1024,194]{0,1:T(8,128)(2,1)S(1)}, bf16[1024,194]{0,1:T(8,128)(2,1)S(1)}, u32[]{:S(2)}, u32[]{:S(2)}) %collective-permute-start) | collective-permute-done | bytes 397344 | tf_op jit(solution)/shard_map/while/body/eval_jaxpr/ppermute | solution.py:21
  197.7 11.1 %collective-permute-start = (bf16[1024,194]{0,1:T(8,128)(2,1)S(1)}, bf16[1024,194]{0,1:T(8,128)(2,1)S(1)}, u32[]{:S(2)}, u32[]{:S(2)}) collective-permute-start(bf16[1024,194]{0,1:T(8,128)(2,1)S(1)} %copy.91), channel_id=1, source_target_pairs={{0,32},{32,64},{64,96},{96,128},{128,160},{160,192},{192,224},{224... | collective-permute-start | bytes 1191944 | tf_op jit(solution)/shard_map/while/body/eval_jaxpr/ppermute | solution.py:21
  214.1 4.2 %fusion.81 = f32[1024,96]{0,1:T(8,128)} fusion(f32[1024,1024]{0,1:T(8,128)} %copy-done.1, f32[1024]{0:T(1024)S(1)} %max.15, bf16[1024]{0:T(1024)(128)(2,1)S(1)} %reduce.17, bf16[1024]{0:T(1024)(128)(2,1)S(1)} %get-tuple-element.450, f32[1024,96]{0,1:T(8,128)} %get-tuple-element.471, bf16[1024,194]{0,1:T(8,128)(2,1)S(1)} %copy.91, ...), kind=kOutput, calls=%fused_computation.9.clone.1 | convolution fusion | flops 207814656 | bytes 5189632 | tf_op jit(solution)/shard_map/while/body/eval_jaxpr/qk,kd->qd/dot_general | solution.py:58
  218.3 12.2 %collective-permute-start = (bf16[1024,194]{0,1:T(8,128)(2,1)S(1)}, bf16[1024,194]{0,1:T(8,128)(2,1)S(1)}, u32[]{:S(2)}, u32[]{:S(2)}) collective-permute-start(bf16[1024,194]{0,1:T(8,128)(2,1)S(1)} %copy.91), channel_id=1, source_target_pairs={{0,32},{32,64},{64,96},{96,128},{128,160},{160,192},{192,224},{224... | collective-permute-start | bytes 1191944 | tf_op jit(solution)/shard_map/while/body/eval_jaxpr/ppermute | solution.py:21
  235.7 4.2 %fusion.81 = f32[1024,96]{0,1:T(8,128)} fusion(f32[1024,1024]{0,1:T(8,128)} %copy-done.1, f32[1024]{0:T(1024)S(1)} %max.15, bf16[1024]{0:T(1024)(128)(2,1)S(1)} %reduce.17, bf16[1024]{0:T(1024)(128)(2,1)S(1)} %get-tuple-element.450, f32[1024,96]{0,1:T(8,128)} %get-tuple-element.471, bf16[1024,194]{0,1:T(8,128)(2,1)S(1)} %copy.91, ...), kind=kOutput, calls=%fused_computation.9.clone.1 | convolution fusion | flops 207814656 | bytes 5189632 | tf_op jit(solution)/shard_map/while/body/eval_jaxpr/qk,kd->qd/dot_general | solution.py:58
  244.2 7.7 %all_to_all.21 = bf16[4,256,96]{1,2,0:T(8,128)(2,1)S(1)} all-to-all(bf16[4,256,96]{1,2,0:T(8,128)(2,1)S(1)} %bitcast.59), channel_id=1, replica_groups=mesh['seq_hi'=16,'seq_lo'=4,'tp'=8] {'seq_lo'}, dimensions={0} | all-to-all | bytes 393216 | tf_op jit(solution)/shard_map/all_to_all | solution.py:153
  254.3 4.4 %all-to-all-start.2 = ((bf16[8,256,384]{2,1,0:T(8,128)(2,1)}), bf16[8,256,384]{2,1,0:T(8,128)(2,1)}, u32[]{:S(2)}, u32[]{:S(2)}) async-start(bf16[8,256,384]{2,1,0:T(8,128)(2,1)} %bitcast.45), calls=%async_computation.2 | async-start | bytes 3145728 | tf_op jit(solution)/shard_map/all_to_all | solution.py:165
  260.3 20.0 %all-to-all-done.2 = bf16[8,256,384]{2,1,0:T(8,128)(2,1)} async-done(((bf16[8,256,384]{2,1,0:T(8,128)(2,1)}), bf16[8,256,384]{2,1,0:T(8,128)(2,1)}, u32[]{:S(2)}, u32[]{:S(2)}) %all-to-all-start.2) | async-done | bytes 1572896 | tf_op jit(solution)/shard_map/all_to_all | solution.py:165
  287.9 4.3 %all-to-all-done.3 = f32[8,1,256]{2,1,0:T(1,128)S(1)} async-done(((f32[8,1,256]{2,1,0:T(1,128)}), f32[8,1,256]{2,1,0:T(1,128)S(1)}, u32[]{:S(2)}, u32[]{:S(2)}) %all-to-all-start.3) | async-done | bytes 8224 | tf_op jit(solution)/shard_map/all_to_all | solution.py:171
  (214 shorter events, 85.1 us)
Async XLA Ops:
  0.6 251.3 %copy-start = (bf16[384,3072]{1,0:T(8,128)(2,1)S(1)}, bf16[384,3072]{1,0:T(8,128)(2,1)}, u32[]{:S(2)}) copy-start(bf16[384,3072]{1,0:T(8,128)(2,1)} %param.15) | copy-start | bytes 7077892
  5.3 13.1 %all-to-all-start = ((bf16[4,256,290]{1,2,0:T(8,128)(2,1)}), bf16[4,256,290]{1,2,0:T(8,128)(2,1)S(1)}, u32[]{:S(2)}, u32[]{:S(2)}) async-start(bf16[4,256,290]{1,2,0:T(8,128)(2,1)} %bitcast.55), calls=%async_computation | async-start | bytes 1212416 | tf_op jit(solution)/shard_map/all_to_all | solution.py:103
  8.8 24.1 %copy-start.13 = (bf16[32]{0:T(256)(128)(2,1)}, bf16[32]{0:T(256)(128)(2,1)S(1)}, u32[]{:S(2)}) copy-start(bf16[32]{0:T(256)(128)(2,1)S(1)} %add_convert_fusion.5) | copy-start | bytes 196
  19.0 14.0 %copy-start.5 = (bf16[37,8,4,256]{3,1,2,0:T(8,128)(2,1)}, bf16[37,8,4,256]{3,1,2,0:T(8,128)(2,1)S(1)}, u32[]{:S(2)}) copy-start(bf16[37,8,4,256]{3,1,2,0:T(8,128)(2,1)S(1)} %copy.68) | copy-start | bytes 1818628
  24.3 23.8 %collective-permute-start.1 = (bf16[1024,194]{0,1:T(8,128)(2,1)}, bf16[1024,194]{0,1:T(8,128)(2,1)S(1)}, u32[]{:S(2)}, u32[]{:S(2)}) collective-permute-start(bf16[1024,194]{0,1:T(8,128)(2,1)} %slice.107), channel_id=1, source_target_pairs={{0,32},{32,64},{64,96},{96,128},{128,160},{160,192},{192,224},{224... | collective-permute-start | bytes 1191944 | tf_op jit(solution)/shard_map/ppermute | solution.py:21
  48.1 28.8 %collective-permute-start = (bf16[1024,194]{0,1:T(8,128)(2,1)S(1)}, bf16[1024,194]{0,1:T(8,128)(2,1)S(1)}, u32[]{:S(2)}, u32[]{:S(2)}) collective-permute-start(bf16[1024,194]{0,1:T(8,128)(2,1)S(1)} %copy.91), channel_id=1, source_target_pairs={{0,32},{32,64},{64,96},{96,128},{128,160},{160,192},{192,224},{224... | collective-permute-start | bytes 1191944 | tf_op jit(solution)/shard_map/while/body/eval_jaxpr/ppermute | solution.py:21
  77.0 29.6 %collective-permute-start = (bf16[1024,194]{0,1:T(8,128)(2,1)S(1)}, bf16[1024,194]{0,1:T(8,128)(2,1)S(1)}, u32[]{:S(2)}, u32[]{:S(2)}) collective-permute-start(bf16[1024,194]{0,1:T(8,128)(2,1)S(1)} %copy.91), channel_id=1, source_target_pairs={{0,32},{32,64},{64,96},{96,128},{128,160},{160,192},{192,224},{224... | collective-permute-start | bytes 1191944 | tf_op jit(solution)/shard_map/while/body/eval_jaxpr/ppermute | solution.py:21
  106.6 28.4 %collective-permute-start = (bf16[1024,194]{0,1:T(8,128)(2,1)S(1)}, bf16[1024,194]{0,1:T(8,128)(2,1)S(1)}, u32[]{:S(2)}, u32[]{:S(2)}) collective-permute-start(bf16[1024,194]{0,1:T(8,128)(2,1)S(1)} %copy.91), channel_id=1, source_target_pairs={{0,32},{32,64},{64,96},{96,128},{128,160},{160,192},{192,224},{224... | collective-permute-start | bytes 1191944 | tf_op jit(solution)/shard_map/while/body/eval_jaxpr/ppermute | solution.py:21
  135.0 35.5 %collective-permute-start = (bf16[1024,194]{0,1:T(8,128)(2,1)S(1)}, bf16[1024,194]{0,1:T(8,128)(2,1)S(1)}, u32[]{:S(2)}, u32[]{:S(2)}) collective-permute-start(bf16[1024,194]{0,1:T(8,128)(2,1)S(1)} %copy.91), channel_id=1, source_target_pairs={{0,32},{32,64},{64,96},{96,128},{128,160},{160,192},{192,224},{224... | collective-permute-start | bytes 1191944 | tf_op jit(solution)/shard_map/while/body/eval_jaxpr/ppermute | solution.py:21
  170.5 27.2 %collective-permute-start = (bf16[1024,194]{0,1:T(8,128)(2,1)S(1)}, bf16[1024,194]{0,1:T(8,128)(2,1)S(1)}, u32[]{:S(2)}, u32[]{:S(2)}) collective-permute-start(bf16[1024,194]{0,1:T(8,128)(2,1)S(1)} %copy.91), channel_id=1, source_target_pairs={{0,32},{32,64},{64,96},{96,128},{128,160},{160,192},{192,224},{224... | collective-permute-start | bytes 1191944 | tf_op jit(solution)/shard_map/while/body/eval_jaxpr/ppermute | solution.py:21
  197.7 20.5 %collective-permute-start = (bf16[1024,194]{0,1:T(8,128)(2,1)S(1)}, bf16[1024,194]{0,1:T(8,128)(2,1)S(1)}, u32[]{:S(2)}, u32[]{:S(2)}) collective-permute-start(bf16[1024,194]{0,1:T(8,128)(2,1)S(1)} %copy.91), channel_id=1, source_target_pairs={{0,32},{32,64},{64,96},{96,128},{128,160},{160,192},{192,224},{224... | collective-permute-start | bytes 1191944 | tf_op jit(solution)/shard_map/while/body/eval_jaxpr/ppermute | solution.py:21
  218.3 21.6 %collective-permute-start = (bf16[1024,194]{0,1:T(8,128)(2,1)S(1)}, bf16[1024,194]{0,1:T(8,128)(2,1)S(1)}, u32[]{:S(2)}, u32[]{:S(2)}) collective-permute-start(bf16[1024,194]{0,1:T(8,128)(2,1)S(1)} %copy.91), channel_id=1, source_target_pairs={{0,32},{32,64},{64,96},{96,128},{128,160},{160,192},{192,224},{224... | collective-permute-start | bytes 1191944 | tf_op jit(solution)/shard_map/while/body/eval_jaxpr/ppermute | solution.py:21
  251.9 6.8 %copy-start.9 = (bf16[256,384]{1,0:T(8,128)(2,1)S(1)}, bf16[256,384]{1,0:T(8,128)(2,1)}, u32[]{:S(2)}) copy-start(bf16[256,384]{1,0:T(8,128)(2,1)} %param.13) | copy-start | bytes 589828
  252.9 6.1 %copy-start.16 = (bf16[384]{0:T(512)(128)(2,1)S(1)}, bf16[384]{0:T(512)(128)(2,1)}, u32[]{:S(2)}) copy-start(bf16[384]{0:T(512)(128)(2,1)} %param.16) | copy-start | bytes 2308
  252.9 6.1 %copy-start.20 = (s32[2]{0:T(128)S(1)}, s32[2]{0:T(128)}, u32[]{:S(2)}) copy-start(s32[2]{0:T(128)} %param.19) | copy-start | bytes 28
  252.9 6.6 %copy-start.14 = (bf16[32]{0:T(256)(128)(2,1)S(1)}, bf16[32]{0:T(256)(128)(2,1)}, u32[]{:S(2)}) copy-start(bf16[32]{0:T(256)(128)(2,1)} %copy-done.13) | copy-start | bytes 196
  252.9 6.8 %copy-start.19 = (s32[32]{0:T(128)S(1)}, s32[32]{0:T(128)}, u32[]{:S(2)}) copy-start(s32[32]{0:T(128)} %copy-done.18) | copy-start | bytes 388
  252.9 7.2 %copy-start.3 = (f32[256,4,96]{0,2,1:T(8,128)S(1)}, f32[256,4,96]{0,2,1:T(8,128)}, u32[]{:S(2)}) copy-start(f32[256,4,96]{0,2,1:T(8,128)} %copy-done.2) | copy-start | bytes 1179652
  254.3 27.7 %copy-start.11 = (bf16[256,384]{1,0:T(8,128)(2,1)S(1)}, bf16[256,384]{1,0:T(8,128)(2,1)}, u32[]{:S(2)}) copy-start(bf16[256,384]{1,0:T(8,128)(2,1)} %param.14) | copy-start | bytes 589828
  254.3 26.0 %all-to-all-start.2 = ((bf16[8,256,384]{2,1,0:T(8,128)(2,1)}), bf16[8,256,384]{2,1,0:T(8,128)(2,1)}, u32[]{:S(2)}, u32[]{:S(2)}) async-start(bf16[8,256,384]{2,1,0:T(8,128)(2,1)} %bitcast.45), calls=%async_computation.2 | async-start | bytes 3145728 | tf_op jit(solution)/shard_map/all_to_all | solution.py:165
  259.9 27.3 %copy-start.17 = (s32[2]{0:T(128)S(1)}, s32[2]{0:T(128)}, u32[]{:S(2)}) copy-start(s32[2]{0:T(128)} %compare_select_fusion.4) | copy-start | bytes 28
  282.1 11.0 %copy-start.10 = (bf16[256,384]{1,0:T(8,128)(2,1)}, bf16[256,384]{1,0:T(8,128)(2,1)S(1)}, u32[]{:S(2)}) copy-start(bf16[256,384]{1,0:T(8,128)(2,1)S(1)} %get-tuple-element.368) | copy-start | bytes 589828
  282.8 9.5 %all-to-all-start.3 = ((f32[8,1,256]{2,1,0:T(1,128)}), f32[8,1,256]{2,1,0:T(1,128)S(1)}, u32[]{:S(2)}, u32[]{:S(2)}) async-start(f32[8,1,256]{2,1,0:T(1,128)} %broadcast_in_dim.164), calls=%async_computation.3 | async-start | bytes 16384 | tf_op jit(solution)/shard_map/all_to_all | solution.py:171
  287.9 5.2 %copy-start.6 = (bf16[2,2,128,384]{3,2,1,0:T(8,128)(2,1)}, bf16[2,2,128,384]{3,2,1,0:T(8,128)(2,1)S(1)}, u32[]{:S(2)}) copy-start(bf16[2,2,128,384]{3,2,1,0:T(8,128)(2,1)S(1)} %scatter_fusion) | copy-start | bytes 1179652
  (15 other events, 34.8 us)

commit v4 on v3

--- a/solution.py
+++ b/solution.py
@@ -90,6 +90,9 @@
         hit = tag_values[:, None] == seg_tags[None, :].astype(tag_values.dtype)
         return jnp.min(jnp.where(hit, index_values[:, None], far_index), axis=0)
 
+    signed_tag = jnp.where(pad_mask == 1, query_tag, -query_tag)
+    all_tags = lax.all_gather(signed_tag, ("seq_hi", "seq_lo"), tiled=True)
+
     tags = jnp.stack([key_tag, query_tag], axis=-1).astype(jnp.bfloat16)
     payload = jnp.concatenate(
         [
@@ -108,7 +111,7 @@
     chunk_v = chunk[:, 2 * HEAD_DIM : 3 * HEAD_DIM]
     chunk_ktag = chunk[:, 3 * HEAD_DIM]
     chunk_qtag = chunk[:, 3 * HEAD_DIM + 1]
-    ring_own = chunk[:, HEAD_DIM : 3 * HEAD_DIM + 2]
+    ring_own = chunk[:, HEAD_DIM : 3 * HEAD_DIM]
     chunk_row = lax.axis_index("seq_hi")
     chunk_offsets = jnp.arange(chunk_count, dtype=jnp.int32)
 
@@ -124,14 +127,15 @@
     softmax_state = attend(softmax_state, chunk_q, chunk_k, chunk_v, own_visible)
 
     def visit_block(current, moved, distance):
-        state, seen_first = current
-        visible = moved[:, 2 * HEAD_DIM][None, :] == chunk_qtag[:, None]
-        state = attend(
-            state, chunk_q, moved[:, :HEAD_DIM], moved[:, HEAD_DIM : 2 * HEAD_DIM], visible
+        source_row = chunk_row - distance
+        moved_tags = lax.dynamic_slice_in_dim(
+            all_tags, jnp.maximum(source_row, 0) * chunk_count, chunk_count
         )
-        moved_index = (chunk_row - distance) * chunk_count + chunk_offsets
-        seen_first = jnp.minimum(seen_first, first_of(moved[:, 2 * HEAD_DIM + 1], moved_index))
-        return (state, seen_first)
+        moved_tags = jnp.where(source_row >= 0, moved_tags, 0).astype(jnp.bfloat16)
+        visible = moved_tags[None, :] == chunk_qtag[:, None]
+        return attend(
+            current, chunk_q, moved[:, :HEAD_DIM], moved[:, HEAD_DIM : 2 * HEAD_DIM], visible
+        )
 
     def cycle_turn(turn_index, loop_state):
         current, moved = loop_state
@@ -139,12 +143,12 @@
         return (visit_block(current, moved, turn_index + 1), following)
 
     reach_count = lo_count * hi_count // 2 * tok_count // chunk_count
-    seen_first = first_of(chunk_qtag, chunk_row * chunk_count + chunk_offsets)
     moved = passed_along(ring_own, "seq_hi", 1)
-    (softmax_state, seen_first), moved = lax.fori_loop(
-        0, reach_count - 1, cycle_turn, ((softmax_state, seen_first), moved)
-    )
-    softmax_state, first_tok = visit_block((softmax_state, seen_first), moved, reach_count)
+    softmax_state, moved = lax.fori_loop(0, reach_count - 1, cycle_turn, (softmax_state, moved))
+    softmax_state = visit_block(softmax_state, moved, reach_count)
+    first_tok = first_of(
+        jnp.abs(all_tags), jnp.arange(hi_count * chunk_count, dtype=jnp.int32)
+    )
     member = segment_ids[:, None] == jnp.arange(seg_count, dtype=jnp.int32)[None, :]
     position = tok_index - jnp.sum(jnp.where(member, first_tok[None, :], 0), axis=1)
     k_rot = rotate(key_proj, position, head_count, HEAD_DIM)

time: 294 us -> 417 us (1.42)
  the two profiles are of different devices: /device:TPU:176 before, /device:TPU:256 now
where the time goes in v4:
time: 417 us; the launch traced here: 416 us
  waiting for transfers between devices  227 us (54%)
  blocking collectives  85.6 us (21%)
  matrix products  30.2 us (7%)
  starting transfers between devices  28.2 us (7%)
  other arithmetic  26.9 us (6%)
  local copies, waits for them, and re-layouts  16.2 us (4%)
    ppermute x8, waiting for transfers between devices, passed_along(): return lax.ppermute(block, axis, route)  193 us
    all_gather x1, blocking collectives, per_device(): all_tags = lax.all_gather(signed_tag, ('seq_hi', 'seq_lo'), tiled=True)  77.9 us
    all_to_all x1, waiting for transfers between devices, per_device(): gathered = lax.all_to_all(pieces, 'tp', 0, 0, tiled=True)  20.9 us
    ppermute x8, starting transfers between devices, passed_along(): return lax.ppermute(block, axis, route)  15.5 us
    dot_general x9, matrix products, attend(): jnp.einsum('qd,kd->qk', query_heads, key_heads, preferred_element_type=jn...  14.9 us
    dot_general x9, matrix products, attend(): jnp.einsum('qk,kd->qd', unnormed.astype(jnp.bfloat16), val_heads, preferr...  14.3 us
    reduce_sum x9, other arithmetic, attend(): row_total = row_total * rescale + jnp.sum(unnormed, axis=-1)  11.9 us
    all_to_all x1, waiting for transfers between devices, per_device(): chunk = lax.all_to_all(payload, 'seq_lo', 0, 0, tiled=True)  9.07 us
  transfers between devices with their start and end apart: 11, of which 11 were waited for; matrix products, arithmetic and copies ran while one was open for 10% of the time, Pallas kernels for 0%

profile of v4, /device:TPU:256, one launch (start us, length us, event | category | flops | bytes accessed | tf_op | source)
XLA Modules:
  0.0 416.2 jit_solution(11990734366100682264)
XLA Ops:
  2.0 77.9 %all-gather = s32[64,1,256]{2,1,0:T(1,128)S(1)} all-gather(s32[1,1,256]{2,1,0:T(1,128)S(1)} %bitcast.68), channel_id=1, replica_groups=mesh['seq_hi'=16,'seq_lo'=4,'tp'=8] {'seq_hi','seq_lo'}, dimensions={0}, use_global_device_ids=true | all-gather | bytes 66560 | tf_op jit(solution)/shard_map/all_gather | solution.py:94
  89.9 3.5 all-to-all-start
  94.0 9.1 %all-to-all-done = bf16[4,256,290]{1,2,0:T(8,128)(2,1)S(1)} async-done(((bf16[4,256,290]{1,2,0:T(8,128)(2,1)}), bf16[4,256,290]{1,2,0:T(8,128)(2,1)S(1)}, u32[]{:S(2)}, u32[]{:S(2)}) %all-to-all-start) | async-done | bytes 593952 | tf_op jit(solution)/shard_map/all_to_all | solution.py:106
  108.2 2.6 fusion.23
  110.8 2.1 collective-permute-start.1
  113.8 4.0 fusion.28
  117.8 27.4 %collective-permute-done.1 = bf16[1024,192]{0,1:T(8,128)(2,1)} collective-permute-done((bf16[1024,192]{0,1:T(8,128)(2,1)}, bf16[1024,192]{0,1:T(8,128)(2,1)}, u32[]{:S(2)}, u32[]{:S(2)}) %collective-permute-start.1) | collective-permute-done | bytes 393248 | tf_op jit(solution)/shard_map/ppermute | solution.py:21
  146.4 214.6 %while.19 = (s32[]{:T(128)}, f32[1024]{0:T(1024)S(1)}, f32[1024]{0:T(1024)S(1)}, f32[1024,96]{0,1:T(8,128)}, bf16[1024,192]{1,0:T(8,128)(2,1)S(1)}, /*index=5*/s...) while((s32[]{:T(128)}, f32[1024]{0:T(1024)S(1)}, ...), condition=%wide.region_5.6_spmd, body=%wide.region_2.5_spmd.sunk | while | flops 419631104 | bytes 19683644 | solution.py:147
  146.5 1.9 collective-permute-start
  153.4 26.2 %collective-permute-done = bf16[1024,192]{1,0:T(8,128)(2,1)S(1)} collective-permute-done((bf16[1024,192]{1,0:T(8,128)(2,1)S(1)}, bf16[1024,192]{1,0:T(8,128)(2,1)S(1)}, u32[]{:S(2)}, u32[]{:S(2)}) %collective-permute-start) | collective-permute-done | bytes 393248 | tf_op jit(solution)/shard_map/while/body/eval_jaxpr/ppermute | solution.py:21
  179.6 1.9 collective-permute-start
  186.6 28.6 %collective-permute-done = bf16[1024,192]{1,0:T(8,128)(2,1)S(1)} collective-permute-done((bf16[1024,192]{1,0:T(8,128)(2,1)S(1)}, bf16[1024,192]{1,0:T(8,128)(2,1)S(1)}, u32[]{:S(2)}, u32[]{:S(2)}) %collective-permute-start) | collective-permute-done | bytes 393248 | tf_op jit(solution)/shard_map/while/body/eval_jaxpr/ppermute | solution.py:21
  215.2 1.9 collective-permute-start
  222.1 31.0 %collective-permute-done = bf16[1024,192]{1,0:T(8,128)(2,1)S(1)} collective-permute-done((bf16[1024,192]{1,0:T(8,128)(2,1)S(1)}, bf16[1024,192]{1,0:T(8,128)(2,1)S(1)}, u32[]{:S(2)}, u32[]{:S(2)}) %collective-permute-start) | collective-permute-done | bytes 393248 | tf_op jit(solution)/shard_map/while/body/eval_jaxpr/ppermute | solution.py:21
  253.2 1.9 collective-permute-start
  260.2 30.5 %collective-permute-done = bf16[1024,192]{1,0:T(8,128)(2,1)S(1)} collective-permute-done((bf16[1024,192]{1,0:T(8,128)(2,1)S(1)}, bf16[1024,192]{1,0:T(8,128)(2,1)S(1)}, u32[]{:S(2)}, u32[]{:S(2)}) %collective-permute-start) | collective-permute-done | bytes 393248 | tf_op jit(solution)/shard_map/while/body/eval_jaxpr/ppermute | solution.py:21
  297.6 21.1 %collective-permute-done = bf16[1024,192]{1,0:T(8,128)(2,1)S(1)} collective-permute-done((bf16[1024,192]{1,0:T(8,128)(2,1)S(1)}, bf16[1024,192]{1,0:T(8,128)(2,1)S(1)}, u32[]{:S(2)}, u32[]{:S(2)}) %collective-permute-start) | collective-permute-done | bytes 393248 | tf_op jit(solution)/shard_map/while/body/eval_jaxpr/ppermute | solution.py:21
  325.7 16.1 %collective-permute-done = bf16[1024,192]{1,0:T(8,128)(2,1)S(1)} collective-permute-done((bf16[1024,192]{1,0:T(8,128)(2,1)S(1)}, bf16[1024,192]{1,0:T(8,128)(2,1)S(1)}, u32[]{:S(2)}, u32[]{:S(2)}) %collective-permute-start) | collective-permute-done | bytes 393248 | tf_op jit(solution)/shard_map/while/body/eval_jaxpr/ppermute | solution.py:21
  348.9 12.1 %collective-permute-done = bf16[1024,192]{1,0:T(8,128)(2,1)S(1)} collective-permute-done((bf16[1024,192]{1,0:T(8,128)(2,1)S(1)}, bf16[1024,192]{1,0:T(8,128)(2,1)S(1)}, u32[]{:S(2)}, u32[]{:S(2)}) %collective-permute-start) | collective-permute-done | bytes 393248 | tf_op jit(solution)/shard_map/while/body/eval_jaxpr/ppermute | solution.py:21
  365.2 7.7 %all_to_all.21 = bf16[4,256,96]{1,2,0:T(8,128)(2,1)S(1)} all-to-all(bf16[4,256,96]{1,2,0:T(8,128)(2,1)S(1)} %bitcast.57), channel_id=1, replica_groups=mesh['seq_hi'=16,'seq_lo'=4,'tp'=8] {'seq_lo'}, dimensions={0} | all-to-all | bytes 393216 | tf_op jit(solution)/shard_map/all_to_all | solution.py:157
  375.3 5.8 %all-to-all-start.2 = ((bf16[8,256,384]{2,1,0:T(8,128)(2,1)}), bf16[8,256,384]{2,1,0:T(8,128)(2,1)}, u32[]{:S(2)}, u32[]{:S(2)}) async-start(bf16[8,256,384]{2,1,0:T(8,128)(2,1)} %bitcast.43), calls=%async_computation.2 | async-start | bytes 3145728 | tf_op jit(solution)/shard_map/all_to_all | solution.py:169
  381.6 20.9 %all-to-all-done.2 = bf16[8,256,384]{2,1,0:T(8,128)(2,1)} async-done(((bf16[8,256,384]{2,1,0:T(8,128)(2,1)}), bf16[8,256,384]{2,1,0:T(8,128)(2,1)}, u32[]{:S(2)}, u32[]{:S(2)}) %all-to-all-start.2) | async-done | bytes 1572896 | tf_op jit(solution)/shard_map/all_to_all | solution.py:169
  405.9 3.3 all-to-all-start.3
  411.0 4.3 %all-to-all-done.3 = f32[8,1,256]{2,1,0:T(1,128)S(1)} async-done(((f32[8,1,256]{2,1,0:T(1,128)}), f32[8,1,256]{2,1,0:T(1,128)S(1)}, u32[]{:S(2)}, u32[]{:S(2)}) %all-to-all-start.3) | async-done | bytes 8224 | tf_op jit(solution)/shard_map/all_to_all | solution.py:175
  (191 shorter events, 72.5 us)
Async XLA Ops:
  0.6 372.3 %copy-start = (bf16[384,3072]{1,0:T(8,128)(2,1)S(1)}, bf16[384,3072]{1,0:T(8,128)(2,1)}, u32[]{:S(2)}) copy-start(bf16[384,3072]{1,0:T(8,128)(2,1)} %param.15) | copy-start | bytes 7077892
  79.9 23.6 %copy-start.10 = (s32[64,1,256]{2,1,0:T(1,128)}, s32[64,1,256]{2,1,0:T(1,128)S(1)}, u32[]{:S(2)}) copy-start(s32[64,1,256]{2,1,0:T(1,128)S(1)} %all-gather) | copy-start | bytes 196612
  86.2 20.0 %copy-start.1 = (f32[256,4,96]{0,2,1:T(8,128)}, f32[256,4,96]{0,2,1:T(8,128)S(1)}, u32[]{:S(2)}) copy-start(f32[256,4,96]{0,2,1:T(8,128)S(1)} %convert.37) | copy-start | bytes 1179652
  89.9 13.1 %all-to-all-start = ((bf16[4,256,290]{1,2,0:T(8,128)(2,1)}), bf16[4,256,290]{1,2,0:T(8,128)(2,1)S(1)}, u32[]{:S(2)}, u32[]{:S(2)}) async-start(bf16[4,256,290]{1,2,0:T(8,128)(2,1)} %bitcast.53), calls=%async_computation | async-start | bytes 1212416 | tf_op jit(solution)/shard_map/all_to_all | solution.py:106
  110.8 34.4 %collective-permute-start.1 = (bf16[1024,192]{0,1:T(8,128)(2,1)}, bf16[1024,192]{0,1:T(8,128)(2,1)}, u32[]{:S(2)}, u32[]{:S(2)}) collective-permute-start(bf16[1024,192]{0,1:T(8,128)(2,1)} %slice.73), channel_id=1, source_target_pairs={{0,32},{32,64},{64,96},{96,128},{128,160},{160,192},{192,224},{224... | collective-permute-start | bytes 1179656 | tf_op jit(solution)/shard_map/ppermute | solution.py:21
  146.4 214.6 %copy-start.13 = (bf16[1024]{0:T(1024)(128)(2,1)S(1)}, bf16[1024]{0:T(1024)(128)(2,1)}, u32[]{:S(2)}) copy-start(bf16[1024]{0:T(1024)(128)(2,1)} %select_convert_fusion.1) | copy-start | bytes 6148
  146.5 33.1 %collective-permute-start = (bf16[1024,192]{1,0:T(8,128)(2,1)S(1)}, bf16[1024,192]{1,0:T(8,128)(2,1)S(1)}, u32[]{:S(2)}, u32[]{:S(2)}) collective-permute-start(bf16[1024,192]{1,0:T(8,128)(2,1)S(1)} %copy.92), channel_id=1, source_target_pairs={{0,32},{32,64},{64,96},{96,128},{128,160},{160,192},{192,224},{224... | collective-permute-start | bytes 1179656 | tf_op jit(solution)/shard_map/while/body/eval_jaxpr/ppermute | solution.py:21
  153.4 26.2 %copy-start.18 = (f32[1024,96]{0,1:T(8,128)}, f32[1024,96]{0,1:T(8,128)S(1)}, u32[]{:S(2)}) copy-start(f32[1024,96]{0,1:T(8,128)S(1)} %fusion.75) | copy-start | bytes 1179652 | tf_op jit(solution)/shard_map/while
  179.6 35.5 %collective-permute-start = (bf16[1024,192]{1,0:T(8,128)(2,1)S(1)}, bf16[1024,192]{1,0:T(8,128)(2,1)S(1)}, u32[]{:S(2)}, u32[]{:S(2)}) collective-permute-start(bf16[1024,192]{1,0:T(8,128)(2,1)S(1)} %copy.92), channel_id=1, source_target_pairs={{0,32},{32,64},{64,96},{96,128},{128,160},{160,192},{192,224},{224... | collective-permute-start | bytes 1179656 | tf_op jit(solution)/shard_map/while/body/eval_jaxpr/ppermute | solution.py:21
  186.6 28.6 %copy-start.18 = (f32[1024,96]{0,1:T(8,128)}, f32[1024,96]{0,1:T(8,128)S(1)}, u32[]{:S(2)}) copy-start(f32[1024,96]{0,1:T(8,128)S(1)} %fusion.75) | copy-start | bytes 1179652 | tf_op jit(solution)/shard_map/while
  215.2 38.0 %collective-permute-start = (bf16[1024,192]{1,0:T(8,128)(2,1)S(1)}, bf16[1024,192]{1,0:T(8,128)(2,1)S(1)}, u32[]{:S(2)}, u32[]{:S(2)}) collective-permute-start(bf16[1024,192]{1,0:T(8,128)(2,1)S(1)} %copy.92), channel_id=1, source_target_pairs={{0,32},{32,64},{64,96},{96,128},{128,160},{160,192},{192,224},{224... | collective-permute-start | bytes 1179656 | tf_op jit(solution)/shard_map/while/body/eval_jaxpr/ppermute | solution.py:21
  222.1 31.0 %copy-start.18 = (f32[1024,96]{0,1:T(8,128)}, f32[1024,96]{0,1:T(8,128)S(1)}, u32[]{:S(2)}) copy-start(f32[1024,96]{0,1:T(8,128)S(1)} %fusion.75) | copy-start | bytes 1179652 | tf_op jit(solution)/shard_map/while
  253.2 37.4 %collective-permute-start = (bf16[1024,192]{1,0:T(8,128)(2,1)S(1)}, bf16[1024,192]{1,0:T(8,128)(2,1)S(1)}, u32[]{:S(2)}, u32[]{:S(2)}) collective-permute-start(bf16[1024,192]{1,0:T(8,128)(2,1)S(1)} %copy.92), channel_id=1, source_target_pairs={{0,32},{32,64},{64,96},{96,128},{128,160},{160,192},{192,224},{224... | collective-permute-start | bytes 1179656 | tf_op jit(solution)/shard_map/while/body/eval_jaxpr/ppermute | solution.py:21
  260.1 30.5 %copy-start.18 = (f32[1024,96]{0,1:T(8,128)}, f32[1024,96]{0,1:T(8,128)S(1)}, u32[]{:S(2)}) copy-start(f32[1024,96]{0,1:T(8,128)S(1)} %fusion.75) | copy-start | bytes 1179652 | tf_op jit(solution)/shard_map/while
  290.7 28.1 %collective-permute-start = (bf16[1024,192]{1,0:T(8,128)(2,1)S(1)}, bf16[1024,192]{1,0:T(8,128)(2,1)S(1)}, u32[]{:S(2)}, u32[]{:S(2)}) collective-permute-start(bf16[1024,192]{1,0:T(8,128)(2,1)S(1)} %copy.92), channel_id=1, source_target_pairs={{0,32},{32,64},{64,96},{96,128},{128,160},{160,192},{192,224},{224... | collective-permute-start | bytes 1179656 | tf_op jit(solution)/shard_map/while/body/eval_jaxpr/ppermute | solution.py:21
  297.6 21.1 %copy-start.18 = (f32[1024,96]{0,1:T(8,128)}, f32[1024,96]{0,1:T(8,128)S(1)}, u32[]{:S(2)}) copy-start(f32[1024,96]{0,1:T(8,128)S(1)} %fusion.75) | copy-start | bytes 1179652 | tf_op jit(solution)/shard_map/while
  318.8 23.1 %collective-permute-start = (bf16[1024,192]{1,0:T(8,128)(2,1)S(1)}, bf16[1024,192]{1,0:T(8,128)(2,1)S(1)}, u32[]{:S(2)}, u32[]{:S(2)}) collective-permute-start(bf16[1024,192]{1,0:T(8,128)(2,1)S(1)} %copy.92), channel_id=1, source_target_pairs={{0,32},{32,64},{64,96},{96,128},{128,160},{160,192},{192,224},{224... | collective-permute-start | bytes 1179656 | tf_op jit(solution)/shard_map/while/body/eval_jaxpr/ppermute | solution.py:21
  325.7 16.1 %copy-start.18 = (f32[1024,96]{0,1:T(8,128)}, f32[1024,96]{0,1:T(8,128)S(1)}, u32[]{:S(2)}) copy-start(f32[1024,96]{0,1:T(8,128)S(1)} %fusion.75) | copy-start | bytes 1179652 | tf_op jit(solution)/shard_map/while
  341.9 19.1 %collective-permute-start = (bf16[1024,192]{1,0:T(8,128)(2,1)S(1)}, bf16[1024,192]{1,0:T(8,128)(2,1)S(1)}, u32[]{:S(2)}, u32[]{:S(2)}) collective-permute-start(bf16[1024,192]{1,0:T(8,128)(2,1)S(1)} %copy.92), channel_id=1, source_target_pairs={{0,32},{32,64},{64,96},{96,128},{128,160},{160,192},{192,224},{224... | collective-permute-start | bytes 1179656 | tf_op jit(solution)/shard_map/while/body/eval_jaxpr/ppermute | solution.py:21
  348.8 12.2 %copy-start.18 = (f32[1024,96]{0,1:T(8,128)}, f32[1024,96]{0,1:T(8,128)S(1)}, u32[]{:S(2)}) copy-start(f32[1024,96]{0,1:T(8,128)S(1)} %fusion.75) | copy-start | bytes 1179652 | tf_op jit(solution)/shard_map/while
  375.3 34.5 %copy-start.15 = (bf16[384]{0:T(512)(128)(2,1)S(1)}, bf16[384]{0:T(512)(128)(2,1)}, u32[]{:S(2)}) copy-start(bf16[384]{0:T(512)(128)(2,1)} %param.16) | copy-start | bytes 2308
  375.3 27.2 %all-to-all-start.2 = ((bf16[8,256,384]{2,1,0:T(8,128)(2,1)}), bf16[8,256,384]{2,1,0:T(8,128)(2,1)}, u32[]{:S(2)}, u32[]{:S(2)}) async-start(bf16[8,256,384]{2,1,0:T(8,128)(2,1)} %bitcast.43), calls=%async_computation.2 | async-start | bytes 3145728 | tf_op jit(solution)/shard_map/all_to_all | solution.py:169
  405.2 11.0 %copy-start.9 = (bf16[256,384]{1,0:T(8,128)(2,1)}, bf16[256,384]{1,0:T(8,128)(2,1)S(1)}, u32[]{:S(2)}) copy-start(bf16[256,384]{1,0:T(8,128)(2,1)S(1)} %get-tuple-element.241) | copy-start | bytes 589828
  405.9 9.5 %all-to-all-start.3 = ((f32[8,1,256]{2,1,0:T(1,128)}), f32[8,1,256]{2,1,0:T(1,128)S(1)}, u32[]{:S(2)}, u32[]{:S(2)}) async-start(f32[8,1,256]{2,1,0:T(1,128)} %broadcast_in_dim.134), calls=%async_computation.3 | async-start | bytes 16384 | tf_op jit(solution)/shard_map/all_to_all | solution.py:175
  (19 other events, 95.3 us)

commit v5 on v3

--- a/solution.py
+++ b/solution.py
@@ -108,7 +108,8 @@
     chunk_v = chunk[:, 2 * HEAD_DIM : 3 * HEAD_DIM]
     chunk_ktag = chunk[:, 3 * HEAD_DIM]
     chunk_qtag = chunk[:, 3 * HEAD_DIM + 1]
-    ring_own = chunk[:, HEAD_DIM : 3 * HEAD_DIM + 2]
+    signed_tag = jnp.where(chunk_ktag > 0, chunk_qtag, -chunk_qtag)
+    ring_own = (chunk[:, HEAD_DIM : 3 * HEAD_DIM], signed_tag.reshape(-1, 128))
     chunk_row = lax.axis_index("seq_hi")
     chunk_offsets = jnp.arange(chunk_count, dtype=jnp.int32)
 
@@ -125,12 +126,14 @@
 
     def visit_block(current, moved, distance):
         state, seen_first = current
-        visible = moved[:, 2 * HEAD_DIM][None, :] == chunk_qtag[:, None]
+        moved_kv, moved_tags = moved
+        moved_tags = moved_tags.reshape(-1)
+        visible = moved_tags[None, :] == chunk_qtag[:, None]
         state = attend(
-            state, chunk_q, moved[:, :HEAD_DIM], moved[:, HEAD_DIM : 2 * HEAD_DIM], visible
+            state, chunk_q, moved_kv[:, :HEAD_DIM], moved_kv[:, HEAD_DIM:], visible
         )
         moved_index = (chunk_row - distance) * chunk_count + chunk_offsets
-        seen_first = jnp.minimum(seen_first, first_of(moved[:, 2 * HEAD_DIM + 1], moved_index))
+        seen_first = jnp.minimum(seen_first, first_of(jnp.abs(moved_tags), moved_index))
         return (state, seen_first)
 
     def cycle_turn(turn_index, loop_state):

time: 294 us -> 352 us (1.20)
  the two profiles are of different devices: /device:TPU:176 before, /device:TPU:256 now
where the time goes in v5:
time: 352 us; the launch traced here: 351 us
  waiting for transfers between devices  235 us (67%)
  starting transfers between devices  48.6 us (14%)
  matrix products  28.1 us (8%)
  other arithmetic  19 us (5%)
  local copies, waits for them, and re-layouts  10.8 us (3%)
  blocking collectives  7.67 us (2%)
    ppermute x16, waiting for transfers between devices, passed_along(): return lax.ppermute(block, axis, route)  201 us
    ppermute x16, starting transfers between devices, passed_along(): return lax.ppermute(block, axis, route)  37.3 us
    all_to_all x1, waiting for transfers between devices, per_device(): gathered = lax.all_to_all(pieces, 'tp', 0, 0, tiled=True)  19.9 us
    dot_general x9, matrix products, attend(): jnp.einsum('qd,kd->qk', query_heads, key_heads, preferred_element_type=jn...  15 us
    dot_general x9, matrix products, attend(): jnp.einsum('qk,kd->qd', unnormed.astype(jnp.bfloat16), val_heads, preferr...  12.2 us
    reduce_sum x9, other arithmetic, attend(): row_total = row_total * rescale + jnp.sum(unnormed, axis=-1)  12 us
    all_to_all x1, waiting for transfers between devices, per_device(): chunk = lax.all_to_all(payload, 'seq_lo', 0, 0, tiled=True)  9.62 us
    all_to_all x1, blocking collectives, per_device(): lax.all_to_all(chunk_attn.reshape(lo_count, tok_count, HEAD_DIM), 'seq_lo...  7.67 us
  transfers between devices with their start and end apart: 19, of which 11 were waited for; matrix products, arithmetic and copies ran while one was open for 12% of the time, Pallas kernels for 0%

profile of v5, /device:TPU:256, one launch (start us, length us, event | category | flops | bytes accessed | tf_op | source)
XLA Modules:
  0.0 351.1 jit_solution(7849640205522062857)
XLA Ops:
  5.3 3.5 all-to-all-start
  8.8 9.6 %all-to-all-done = bf16[4,256,290]{1,2,0:T(8,128)(2,1)S(1)} async-done(((bf16[4,256,290]{1,2,0:T(8,128)(2,1)}), bf16[4,256,290]{1,2,0:T(8,128)(2,1)S(1)}, u32[]{:S(2)}, u32[]{:S(2)}) %all-to-all-start) | async-done | bytes 593952 | tf_op jit(solution)/shard_map/all_to_all | solution.py:103
  20.0 4.5 %collective-permute-start.3 = (bf16[8,128]{1,0:T(8,128)(2,1)S(1)}, bf16[8,128]{1,0:T(8,128)(2,1)S(1)}, u32[]{:S(2)}, u32[]{:S(2)}) collective-permute-start(bf16[8,128]{1,0:T(8,128)(2,1)S(1)} %bitcast_select_fusion), channel_id=1, source_target_pairs={{0,32},{32,64},{64,96},{96,128},{128,160},{160,192},{192,224},{224... | collective-permute-start | bytes 6152 | tf_op jit(solution)/shard_map/ppermute | solution.py:21
  25.4 2.7 fusion.27
  28.1 5.9 %collective-permute-start.2 = (bf16[1024,192]{0,1:T(8,128)(2,1)}, bf16[1024,192]{0,1:T(8,128)(2,1)S(1)}, u32[]{:S(2)}, u32[]{:S(2)}) collective-permute-start(bf16[1024,192]{0,1:T(8,128)(2,1)} %slice.79), channel_id=1, source_target_pairs={{0,32},{32,64},{64,96},{96,128},{128,160},{160,192},{192,224},{224... | collective-permute-start | bytes 1179656 | tf_op jit(solution)/shard_map/ppermute | solution.py:21
  37.0 17.6 %collective-permute-done.2 = bf16[1024,192]{0,1:T(8,128)(2,1)S(1)} collective-permute-done((bf16[1024,192]{0,1:T(8,128)(2,1)}, bf16[1024,192]{0,1:T(8,128)(2,1)S(1)}, u32[]{:S(2)}, u32[]{:S(2)}) %collective-permute-start.2) | collective-permute-done | bytes 393248 | tf_op jit(solution)/shard_map/ppermute | solution.py:21
  54.8 242.7 %while.26 = (s32[]{:T(128)}, f32[1024]{0:T(1024)S(1)}, f32[1024]{0:T(1024)S(1)}, f32[1024,96]{0,1:T(8,128)}, s32[32]{0:T(128)S(1)}, /*index=5*/bf16[1024,192]{1,...) while((s32[]{:T(128)}, f32[1024]{0:T(1024)S(1)}, ...), condition=%wide.region_7.8_spmd.clone, body=%wide.region_3.7_spmd.clone.sunk | while | flops 419729472 | bytes 19704740 | solution.py:147
  54.9 1.9 collective-permute-start
  56.8 1.9 collective-permute-start.1
  63.3 27.3 %collective-permute-done.1 = bf16[8,128]{1,0:T(8,128)(2,1)S(1)} collective-permute-done((bf16[8,128]{1,0:T(8,128)(2,1)S(1)}, bf16[8,128]{1,0:T(8,128)(2,1)S(1)}, u32[]{:S(2)}, u32[]{:S(2)}) %collective-permute-start.1) | collective-permute-done | bytes 2080 | tf_op jit(solution)/shard_map/while/body/eval_jaxpr/ppermute | solution.py:21
  90.6 1.9 collective-permute-start
  99.1 35.2 %collective-permute-done.1 = bf16[8,128]{1,0:T(8,128)(2,1)S(1)} collective-permute-done((bf16[8,128]{1,0:T(8,128)(2,1)S(1)}, bf16[8,128]{1,0:T(8,128)(2,1)S(1)}, u32[]{:S(2)}, u32[]{:S(2)}) %collective-permute-start.1) | collective-permute-done | bytes 2080 | tf_op jit(solution)/shard_map/while/body/eval_jaxpr/ppermute | solution.py:21
  142.8 38.1 %collective-permute-done.1 = bf16[8,128]{1,0:T(8,128)(2,1)S(1)} collective-permute-done((bf16[8,128]{1,0:T(8,128)(2,1)S(1)}, bf16[8,128]{1,0:T(8,128)(2,1)S(1)}, u32[]{:S(2)}, u32[]{:S(2)}) %collective-permute-start.1) | collective-permute-done | bytes 2080 | tf_op jit(solution)/shard_map/while/body/eval_jaxpr/ppermute | solution.py:21
  189.3 34.6 %collective-permute-done.1 = bf16[8,128]{1,0:T(8,128)(2,1)S(1)} collective-permute-done((bf16[8,128]{1,0:T(8,128)(2,1)S(1)}, bf16[8,128]{1,0:T(8,128)(2,1)S(1)}, u32[]{:S(2)}, u32[]{:S(2)}) %collective-permute-start.1) | collective-permute-done | bytes 2080 | tf_op jit(solution)/shard_map/while/body/eval_jaxpr/ppermute | solution.py:21
  232.4 22.6 %collective-permute-done.1 = bf16[8,128]{1,0:T(8,128)(2,1)S(1)} collective-permute-done((bf16[8,128]{1,0:T(8,128)(2,1)S(1)}, bf16[8,128]{1,0:T(8,128)(2,1)S(1)}, u32[]{:S(2)}, u32[]{:S(2)}) %collective-permute-start.1) | collective-permute-done | bytes 2080 | tf_op jit(solution)/shard_map/while/body/eval_jaxpr/ppermute | solution.py:21
  255.1 1.9 collective-permute-start
  263.5 17.7 %collective-permute-done.1 = bf16[8,128]{1,0:T(8,128)(2,1)S(1)} collective-permute-done((bf16[8,128]{1,0:T(8,128)(2,1)S(1)}, bf16[8,128]{1,0:T(8,128)(2,1)S(1)}, u32[]{:S(2)}, u32[]{:S(2)}) %collective-permute-start.1) | collective-permute-done | bytes 2080 | tf_op jit(solution)/shard_map/while/body/eval_jaxpr/ppermute | solution.py:21
  283.3 1.9 collective-permute-start.1
  289.8 7.8 %collective-permute-done.1 = bf16[8,128]{1,0:T(8,128)(2,1)S(1)} collective-permute-done((bf16[8,128]{1,0:T(8,128)(2,1)S(1)}, bf16[8,128]{1,0:T(8,128)(2,1)S(1)}, u32[]{:S(2)}, u32[]{:S(2)}) %collective-permute-start.1) | collective-permute-done | bytes 2080 | tf_op jit(solution)/shard_map/while/body/eval_jaxpr/ppermute | solution.py:21
  302.3 7.7 %all_to_all.21 = bf16[4,256,96]{1,2,0:T(8,128)(2,1)S(1)} all-to-all(bf16[4,256,96]{1,2,0:T(8,128)(2,1)S(1)} %bitcast.72), channel_id=1, replica_groups=mesh['seq_hi'=16,'seq_lo'=4,'tp'=8] {'seq_lo'}, dimensions={0} | all-to-all | bytes 393216 | tf_op jit(solution)/shard_map/all_to_all | solution.py:156
  312.3 4.5 %all-to-all-start.2 = ((bf16[8,256,384]{2,1,0:T(8,128)(2,1)}), bf16[8,256,384]{2,1,0:T(8,128)(2,1)}, u32[]{:S(2)}, u32[]{:S(2)}) async-start(bf16[8,256,384]{2,1,0:T(8,128)(2,1)} %bitcast.57), calls=%async_computation.2 | async-start | bytes 3145728 | tf_op jit(solution)/shard_map/all_to_all | solution.py:168
  318.5 19.9 %all-to-all-done.2 = bf16[8,256,384]{2,1,0:T(8,128)(2,1)} async-done(((bf16[8,256,384]{2,1,0:T(8,128)(2,1)}), bf16[8,256,384]{2,1,0:T(8,128)(2,1)}, u32[]{:S(2)}, u32[]{:S(2)}) %all-to-all-start.2) | async-done | bytes 1572896 | tf_op jit(solution)/shard_map/all_to_all | solution.py:168
  340.8 3.3 all-to-all-start.3
  345.9 4.3 %all-to-all-done.3 = f32[8,1,256]{2,1,0:T(1,128)S(1)} async-done(((f32[8,1,256]{2,1,0:T(1,128)}), f32[8,1,256]{2,1,0:T(1,128)S(1)}, u32[]{:S(2)}, u32[]{:S(2)}) %all-to-all-start.3) | async-done | bytes 8224 | tf_op jit(solution)/shard_map/all_to_all | solution.py:174
  (256 shorter events, 72.6 us)
Async XLA Ops:
  0.6 309.3 %copy-start = (bf16[384,3072]{1,0:T(8,128)(2,1)S(1)}, bf16[384,3072]{1,0:T(8,128)(2,1)}, u32[]{:S(2)}) copy-start(bf16[384,3072]{1,0:T(8,128)(2,1)} %param.15) | copy-start | bytes 7077892
  5.3 13.1 %all-to-all-start = ((bf16[4,256,290]{1,2,0:T(8,128)(2,1)}), bf16[4,256,290]{1,2,0:T(8,128)(2,1)S(1)}, u32[]{:S(2)}, u32[]{:S(2)}) async-start(bf16[4,256,290]{1,2,0:T(8,128)(2,1)} %bitcast.68), calls=%async_computation | async-start | bytes 1212416 | tf_op jit(solution)/shard_map/all_to_all | solution.py:103
  20.0 34.8 %collective-permute-start.3 = (bf16[8,128]{1,0:T(8,128)(2,1)S(1)}, bf16[8,128]{1,0:T(8,128)(2,1)S(1)}, u32[]{:S(2)}, u32[]{:S(2)}) collective-permute-start(bf16[8,128]{1,0:T(8,128)(2,1)S(1)} %bitcast_select_fusion), channel_id=1, source_target_pairs={{0,32},{32,64},{64,96},{96,128},{128,160},{160,192},{192,224},{224... | collective-permute-start | bytes 6152 | tf_op jit(solution)/shard_map/ppermute | solution.py:21
  28.1 26.5 %collective-permute-start.2 = (bf16[1024,192]{0,1:T(8,128)(2,1)}, bf16[1024,192]{0,1:T(8,128)(2,1)S(1)}, u32[]{:S(2)}, u32[]{:S(2)}) collective-permute-start(bf16[1024,192]{0,1:T(8,128)(2,1)} %slice.79), channel_id=1, source_target_pairs={{0,32},{32,64},{64,96},{96,128},{128,160},{160,192},{192,224},{224... | collective-permute-start | bytes 1179656 | tf_op jit(solution)/shard_map/ppermute | solution.py:21
  54.9 35.7 %collective-permute-start = (bf16[1024,192]{1,0:T(8,128)(2,1)S(1)}, bf16[1024,192]{1,0:T(8,128)(2,1)S(1)}, u32[]{:S(2)}, u32[]{:S(2)}) collective-permute-start(bf16[1024,192]{1,0:T(8,128)(2,1)S(1)} %copy.95), channel_id=1, source_target_pairs={{0,32},{32,64},{64,96},{96,128},{128,160},{160,192},{192,224},{224... | collective-permute-start | bytes 1179656 | tf_op jit(solution)/shard_map/while/body/eval_jaxpr/ppermute | solution.py:21
  56.8 33.8 %collective-permute-start.1 = (bf16[8,128]{1,0:T(8,128)(2,1)S(1)}, bf16[8,128]{1,0:T(8,128)(2,1)S(1)}, u32[]{:S(2)}, u32[]{:S(2)}) collective-permute-start(bf16[8,128]{1,0:T(8,128)(2,1)S(1)} %copy.96), channel_id=1, source_target_pairs={{0,32},{32,64},{64,96},{96,128},{128,160},{160,192},{192,224},{224... | collective-permute-start | bytes 6152 | tf_op jit(solution)/shard_map/while/body/eval_jaxpr/ppermute | solution.py:21
  90.6 43.6 %collective-permute-start = (bf16[1024,192]{1,0:T(8,128)(2,1)S(1)}, bf16[1024,192]{1,0:T(8,128)(2,1)S(1)}, u32[]{:S(2)}, u32[]{:S(2)}) collective-permute-start(bf16[1024,192]{1,0:T(8,128)(2,1)S(1)} %copy.95), channel_id=1, source_target_pairs={{0,32},{32,64},{64,96},{96,128},{128,160},{160,192},{192,224},{224... | collective-permute-start | bytes 1179656 | tf_op jit(solution)/shard_map/while/body/eval_jaxpr/ppermute | solution.py:21
  92.6 41.7 %collective-permute-start.1 = (bf16[8,128]{1,0:T(8,128)(2,1)S(1)}, bf16[8,128]{1,0:T(8,128)(2,1)S(1)}, u32[]{:S(2)}, u32[]{:S(2)}) collective-permute-start(bf16[8,128]{1,0:T(8,128)(2,1)S(1)} %copy.96), channel_id=1, source_target_pairs={{0,32},{32,64},{64,96},{96,128},{128,160},{160,192},{192,224},{224... | collective-permute-start | bytes 6152 | tf_op jit(solution)/shard_map/while/body/eval_jaxpr/ppermute | solution.py:21
  98.8 35.4 %copy-start.22 = (f32[1024,96]{0,1:T(8,128)}, f32[1024,96]{0,1:T(8,128)S(1)}, u32[]{:S(2)}) copy-start(f32[1024,96]{0,1:T(8,128)S(1)} %fusion.81) | copy-start | bytes 1179652 | tf_op jit(solution)/shard_map/while
  134.3 46.5 %collective-permute-start = (bf16[1024,192]{1,0:T(8,128)(2,1)S(1)}, bf16[1024,192]{1,0:T(8,128)(2,1)S(1)}, u32[]{:S(2)}, u32[]{:S(2)}) collective-permute-start(bf16[1024,192]{1,0:T(8,128)(2,1)S(1)} %copy.95), channel_id=1, source_target_pairs={{0,32},{32,64},{64,96},{96,128},{128,160},{160,192},{192,224},{224... | collective-permute-start | bytes 1179656 | tf_op jit(solution)/shard_map/while/body/eval_jaxpr/ppermute | solution.py:21
  136.3 44.6 %collective-permute-start.1 = (bf16[8,128]{1,0:T(8,128)(2,1)S(1)}, bf16[8,128]{1,0:T(8,128)(2,1)S(1)}, u32[]{:S(2)}, u32[]{:S(2)}) collective-permute-start(bf16[8,128]{1,0:T(8,128)(2,1)S(1)} %copy.96), channel_id=1, source_target_pairs={{0,32},{32,64},{64,96},{96,128},{128,160},{160,192},{192,224},{224... | collective-permute-start | bytes 6152 | tf_op jit(solution)/shard_map/while/body/eval_jaxpr/ppermute | solution.py:21
  142.5 38.3 %copy-start.22 = (f32[1024,96]{0,1:T(8,128)}, f32[1024,96]{0,1:T(8,128)S(1)}, u32[]{:S(2)}) copy-start(f32[1024,96]{0,1:T(8,128)S(1)} %fusion.81) | copy-start | bytes 1179652 | tf_op jit(solution)/shard_map/while
  180.9 43.0 %collective-permute-start = (bf16[1024,192]{1,0:T(8,128)(2,1)S(1)}, bf16[1024,192]{1,0:T(8,128)(2,1)S(1)}, u32[]{:S(2)}, u32[]{:S(2)}) collective-permute-start(bf16[1024,192]{1,0:T(8,128)(2,1)S(1)} %copy.95), channel_id=1, source_target_pairs={{0,32},{32,64},{64,96},{96,128},{128,160},{160,192},{192,224},{224... | collective-permute-start | bytes 1179656 | tf_op jit(solution)/shard_map/while/body/eval_jaxpr/ppermute | solution.py:21
  182.8 41.1 %collective-permute-start.1 = (bf16[8,128]{1,0:T(8,128)(2,1)S(1)}, bf16[8,128]{1,0:T(8,128)(2,1)S(1)}, u32[]{:S(2)}, u32[]{:S(2)}) collective-permute-start(bf16[8,128]{1,0:T(8,128)(2,1)S(1)} %copy.96), channel_id=1, source_target_pairs={{0,32},{32,64},{64,96},{96,128},{128,160},{160,192},{192,224},{224... | collective-permute-start | bytes 6152 | tf_op jit(solution)/shard_map/while/body/eval_jaxpr/ppermute | solution.py:21
  189.1 34.8 %copy-start.22 = (f32[1024,96]{0,1:T(8,128)}, f32[1024,96]{0,1:T(8,128)S(1)}, u32[]{:S(2)}) copy-start(f32[1024,96]{0,1:T(8,128)S(1)} %fusion.81) | copy-start | bytes 1179652 | tf_op jit(solution)/shard_map/while
  224.0 31.1 %collective-permute-start = (bf16[1024,192]{1,0:T(8,128)(2,1)S(1)}, bf16[1024,192]{1,0:T(8,128)(2,1)S(1)}, u32[]{:S(2)}, u32[]{:S(2)}) collective-permute-start(bf16[1024,192]{1,0:T(8,128)(2,1)S(1)} %copy.95), channel_id=1, source_target_pairs={{0,32},{32,64},{64,96},{96,128},{128,160},{160,192},{192,224},{224... | collective-permute-start | bytes 1179656 | tf_op jit(solution)/shard_map/while/body/eval_jaxpr/ppermute | solution.py:21
  225.9 29.1 %collective-permute-start.1 = (bf16[8,128]{1,0:T(8,128)(2,1)S(1)}, bf16[8,128]{1,0:T(8,128)(2,1)S(1)}, u32[]{:S(2)}, u32[]{:S(2)}) collective-permute-start(bf16[8,128]{1,0:T(8,128)(2,1)S(1)} %copy.96), channel_id=1, source_target_pairs={{0,32},{32,64},{64,96},{96,128},{128,160},{160,192},{192,224},{224... | collective-permute-start | bytes 6152 | tf_op jit(solution)/shard_map/while/body/eval_jaxpr/ppermute | solution.py:21
  255.1 26.2 %collective-permute-start = (bf16[1024,192]{1,0:T(8,128)(2,1)S(1)}, bf16[1024,192]{1,0:T(8,128)(2,1)S(1)}, u32[]{:S(2)}, u32[]{:S(2)}) collective-permute-start(bf16[1024,192]{1,0:T(8,128)(2,1)S(1)} %copy.95), channel_id=1, source_target_pairs={{0,32},{32,64},{64,96},{96,128},{128,160},{160,192},{192,224},{224... | collective-permute-start | bytes 1179656 | tf_op jit(solution)/shard_map/while/body/eval_jaxpr/ppermute | solution.py:21
  257.0 24.3 %collective-permute-start.1 = (bf16[8,128]{1,0:T(8,128)(2,1)S(1)}, bf16[8,128]{1,0:T(8,128)(2,1)S(1)}, u32[]{:S(2)}, u32[]{:S(2)}) collective-permute-start(bf16[8,128]{1,0:T(8,128)(2,1)S(1)} %copy.96), channel_id=1, source_target_pairs={{0,32},{32,64},{64,96},{96,128},{128,160},{160,192},{192,224},{224... | collective-permute-start | bytes 6152 | tf_op jit(solution)/shard_map/while/body/eval_jaxpr/ppermute | solution.py:21
  281.3 16.2 %collective-permute-start = (bf16[1024,192]{1,0:T(8,128)(2,1)S(1)}, bf16[1024,192]{1,0:T(8,128)(2,1)S(1)}, u32[]{:S(2)}, u32[]{:S(2)}) collective-permute-start(bf16[1024,192]{1,0:T(8,128)(2,1)S(1)} %copy.95), channel_id=1, source_target_pairs={{0,32},{32,64},{64,96},{96,128},{128,160},{160,192},{192,224},{224... | collective-permute-start | bytes 1179656 | tf_op jit(solution)/shard_map/while/body/eval_jaxpr/ppermute | solution.py:21
  283.3 14.3 %collective-permute-start.1 = (bf16[8,128]{1,0:T(8,128)(2,1)S(1)}, bf16[8,128]{1,0:T(8,128)(2,1)S(1)}, u32[]{:S(2)}, u32[]{:S(2)}) collective-permute-start(bf16[8,128]{1,0:T(8,128)(2,1)S(1)} %copy.96), channel_id=1, source_target_pairs={{0,32},{32,64},{64,96},{96,128},{128,160},{160,192},{192,224},{224... | collective-permute-start | bytes 6152 | tf_op jit(solution)/shard_map/while/body/eval_jaxpr/ppermute | solution.py:21
  312.3 27.7 %copy-start.9 = (bf16[256,384]{1,0:T(8,128)(2,1)S(1)}, bf16[256,384]{1,0:T(8,128)(2,1)}, u32[]{:S(2)}) copy-start(bf16[256,384]{1,0:T(8,128)(2,1)} %param.14) | copy-start | bytes 589828
  312.3 26.0 %all-to-all-start.2 = ((bf16[8,256,384]{2,1,0:T(8,128)(2,1)}), bf16[8,256,384]{2,1,0:T(8,128)(2,1)}, u32[]{:S(2)}, u32[]{:S(2)}) async-start(bf16[8,256,384]{2,1,0:T(8,128)(2,1)} %bitcast.57), calls=%async_computation.2 | async-start | bytes 3145728 | tf_op jit(solution)/shard_map/all_to_all | solution.py:168
  340.8 9.5 %all-to-all-start.3 = ((f32[8,1,256]{2,1,0:T(1,128)}), f32[8,1,256]{2,1,0:T(1,128)S(1)}, u32[]{:S(2)}, u32[]{:S(2)}) async-start(f32[8,1,256]{2,1,0:T(1,128)} %broadcast_in_dim.168), calls=%async_computation.3 | async-start | bytes 16384 | tf_op jit(solution)/shard_map/all_to_all | solution.py:174
  (31 other events, 249.8 us)

commit v6 on v5

--- a/solution.py
+++ b/solution.py
@@ -43,11 +43,13 @@
     return rotated.reshape(count_rows, head_count * head_dim).astype(jnp.bfloat16)
 
 
-def attend(softmax_state, query_heads, key_heads, val_heads, visible):
+def attend(softmax_state, query_heads, key_heads, val_heads, visible, key_form="kd"):
     row_peak, row_total, weighted = softmax_state
     factor = 1.0 / math.sqrt(HEAD_DIM)
     logits = (
-        jnp.einsum("qd,kd->qk", query_heads, key_heads, preferred_element_type=jnp.float32)
+        jnp.einsum(
+            "qd," + key_form + "->qk", query_heads, key_heads, preferred_element_type=jnp.float32
+        )
         * factor
     )
     logits = jnp.where(visible, logits, masked_score)
@@ -56,7 +58,10 @@
     unnormed = jnp.where(visible, jnp.exp(logits - new_peak[..., None]), 0.0)
     row_total = row_total * rescale + jnp.sum(unnormed, axis=-1)
     weighted = weighted * rescale[..., None] + jnp.einsum(
-        "qk,kd->qd", unnormed.astype(jnp.bfloat16), val_heads, preferred_element_type=jnp.float32
+        "qk," + key_form + "->qd",
+        unnormed.astype(jnp.bfloat16),
+        val_heads,
+        preferred_element_type=jnp.float32,
     )
     return (new_peak, row_total, weighted)
 
@@ -109,7 +114,7 @@
     chunk_ktag = chunk[:, 3 * HEAD_DIM]
     chunk_qtag = chunk[:, 3 * HEAD_DIM + 1]
     signed_tag = jnp.where(chunk_ktag > 0, chunk_qtag, -chunk_qtag)
-    ring_own = (chunk[:, HEAD_DIM : 3 * HEAD_DIM], signed_tag.reshape(-1, 128))
+    ring_own = (chunk[:, HEAD_DIM : 3 * HEAD_DIM].T, signed_tag.reshape(-1, 128))
     chunk_row = lax.axis_index("seq_hi")
     chunk_offsets = jnp.arange(chunk_count, dtype=jnp.int32)
 
@@ -130,7 +135,7 @@
         moved_tags = moved_tags.reshape(-1)
         visible = moved_tags[None, :] == chunk_qtag[:, None]
         state = attend(
-            state, chunk_q, moved_kv[:, :HEAD_DIM], moved_kv[:, HEAD_DIM:], visible
+            state, chunk_q, moved_kv[:HEAD_DIM], moved_kv[HEAD_DIM:], visible, "dk"
         )
         moved_index = (chunk_row - distance) * chunk_count + chunk_offsets
         seen_first = jnp.minimum(seen_first, first_of(jnp.abs(moved_tags), moved_index))

time: 352 us -> 304 us (0.86)
  the two profiles are of different devices: /device:TPU:256 before, /device:TPU:160 now
where the time goes in v6:
time: 304 us; the launch traced here: 303 us
  starting transfers between devices  167 us (55%)
  waiting for transfers between devices  48.3 us (16%)
  matrix products  29.1 us (10%)
  other arithmetic  28 us (9%)
  local copies, waits for them, and re-layouts  19.5 us (6%)
  blocking collectives  7.67 us (3%)
    ppermute x16, starting transfers between devices, passed_along(): return lax.ppermute(block, axis, route)  156 us
    all_to_all x1, waiting for transfers between devices, per_device(): gathered = lax.all_to_all(pieces, 'tp', 0, 0, tiled=True)  19.8 us
    dot_general x9, matrix products, attend(): jnp.einsum('qd,' + key_form + '->qk', query_heads, key_heads, preferred_e...  15.7 us
    ppermute x16, waiting for transfers between devices, passed_along(): return lax.ppermute(block, axis, route)  14.6 us
    reduce_sum x9, other arithmetic, attend(): row_total = row_total * rescale + jnp.sum(unnormed, axis=-1)  12.6 us
    dot_general x9, matrix products, attend(): jnp.einsum('qk,' + key_form + '->qd', unnormed.astype(jnp.bfloat16), val_...  12.4 us
    all_to_all x1, waiting for transfers between devices, per_device(): chunk = lax.all_to_all(payload, 'seq_lo', 0, 0, tiled=True)  9.62 us
    while x105, local copies, waits for them, and re-layouts  8.33 us
  transfers between devices with their start and end apart: 19, of which 5 were waited for; matrix products, arithmetic and copies ran while one was open for 17% of the time, Pallas kernels for 0%

profile of v6, /device:TPU:160, one launch (start us, length us, event | category | flops | bytes accessed | tf_op | source)
XLA Modules:
  0.0 302.5 jit_solution(8415477155417361503)
XLA Ops:
  8.3 3.5 %all-to-all-start = ((bf16[4,256,290]{1,2,0:T(8,128)(2,1)}), bf16[4,256,290]{1,2,0:T(8,128)(2,1)S(1)}, u32[]{:S(2)}, u32[]{:S(2)}) async-start(bf16[4,256,290]{1,2,0:T(8,128)(2,1)} %bitcast.70), calls=%async_computation | async-start | bytes 1212416 | tf_op jit(solution)/shard_map/all_to_all | solution.py:108
  11.8 9.6 %all-to-all-done = bf16[4,256,290]{1,2,0:T(8,128)(2,1)S(1)} async-done(((bf16[4,256,290]{1,2,0:T(8,128)(2,1)}), bf16[4,256,290]{1,2,0:T(8,128)(2,1)S(1)}, u32[]{:S(2)}, u32[]{:S(2)}) %all-to-all-start) | async-done | bytes 593952 | tf_op jit(solution)/shard_map/all_to_all | solution.py:108
  30.5 6.8 %collective-permute-start.2 = (bf16[192,1024]{1,0:T(8,128)(2,1)}, bf16[192,1024]{1,0:T(8,128)(2,1)S(1)}, u32[]{:S(2)}, u32[]{:S(2)}) collective-permute-start(bf16[192,1024]{1,0:T(8,128)(2,1)} %slice_bitcast_fusion), channel_id=1, source_target_pairs={{0,32},{32,64},{64,96},{96,128},{128,160},{160,192},{192,224},{224... | collective-permute-start | bytes 1179656 | tf_op jit(solution)/shard_map/ppermute | solution.py:21
  40.8 12.0 %collective-permute-done.2 = bf16[192,1024]{1,0:T(8,128)(2,1)S(1)} collective-permute-done((bf16[192,1024]{1,0:T(8,128)(2,1)}, bf16[192,1024]{1,0:T(8,128)(2,1)S(1)}, u32[]{:S(2)}, u32[]{:S(2)}) %collective-permute-start.2) | collective-permute-done | bytes 393248 | tf_op jit(solution)/shard_map/ppermute | solution.py:21
  52.8 195.2 %while.26 = (s32[]{:T(128)}, f32[1024]{0:T(1024)S(1)}, f32[1024]{0:T(1024)}, f32[1024,96]{0,1:T(8,128)}, s32[32]{0:T(128)}, /*index=5*/bf16[192,1024]{1,0:T(8,12...) while((s32[]{:T(128)}, f32[1024]{0:T(1024)S(1)}, ...), condition=%wide.region_7.8_spmd.clone, body=%wide.region_3.7_spmd.clone.sunk | while | flops 419729472 | bytes 19607572 | solution.py:152
  52.8 5.2 %collective-permute-start = (bf16[192,1024]{1,0:T(8,128)(2,1)S(1)}, bf16[192,1024]{1,0:T(8,128)(2,1)S(1)}, u32[]{:S(2)}, u32[]{:S(2)}) collective-permute-start(bf16[192,1024]{1,0:T(8,128)(2,1)S(1)} %copy.93), channel_id=1, source_target_pairs={{0,32},{32,64},{64,96},{96,128},{128,160},{160,192},{192,224},{224... | collective-permute-start | bytes 1179656 | tf_op jit(solution)/shard_map/while/body/eval_jaxpr/ppermute | solution.py:21
  58.8 10.0 %collective-permute-start.1 = (bf16[8,128]{1,0:T(8,128)(2,1)S(1)}, bf16[8,128]{1,0:T(8,128)(2,1)}, u32[]{:S(2)}, u32[]{:S(2)}) collective-permute-start(bf16[8,128]{1,0:T(8,128)(2,1)S(1)} %copy.94), channel_id=1, source_target_pairs={{0,32},{32,64},{64,96},{96,128},{128,160},{160,192},{192,224},{224... | collective-permute-start | bytes 6152 | tf_op jit(solution)/shard_map/while/body/eval_jaxpr/ppermute | solution.py:21
  74.7 8.9 %collective-permute-start = (bf16[192,1024]{1,0:T(8,128)(2,1)S(1)}, bf16[192,1024]{1,0:T(8,128)(2,1)S(1)}, u32[]{:S(2)}, u32[]{:S(2)}) collective-permute-start(bf16[192,1024]{1,0:T(8,128)(2,1)S(1)} %copy.93), channel_id=1, source_target_pairs={{0,32},{32,64},{64,96},{96,128},{128,160},{160,192},{192,224},{224... | collective-permute-start | bytes 1179656 | tf_op jit(solution)/shard_map/while/body/eval_jaxpr/ppermute | solution.py:21
  84.3 11.9 %collective-permute-start.1 = (bf16[8,128]{1,0:T(8,128)(2,1)S(1)}, bf16[8,128]{1,0:T(8,128)(2,1)}, u32[]{:S(2)}, u32[]{:S(2)}) collective-permute-start(bf16[8,128]{1,0:T(8,128)(2,1)S(1)} %copy.94), channel_id=1, source_target_pairs={{0,32},{32,64},{64,96},{96,128},{128,160},{160,192},{192,224},{224... | collective-permute-start | bytes 6152 | tf_op jit(solution)/shard_map/while/body/eval_jaxpr/ppermute | solution.py:21
  102.1 15.0 %collective-permute-start = (bf16[192,1024]{1,0:T(8,128)(2,1)S(1)}, bf16[192,1024]{1,0:T(8,128)(2,1)S(1)}, u32[]{:S(2)}, u32[]{:S(2)}) collective-permute-start(bf16[192,1024]{1,0:T(8,128)(2,1)S(1)} %copy.93), channel_id=1, source_target_pairs={{0,32},{32,64},{64,96},{96,128},{128,160},{160,192},{192,224},{224... | collective-permute-start | bytes 1179656 | tf_op jit(solution)/shard_map/while/body/eval_jaxpr/ppermute | solution.py:21
  117.9 10.3 %collective-permute-start.1 = (bf16[8,128]{1,0:T(8,128)(2,1)S(1)}, bf16[8,128]{1,0:T(8,128)(2,1)}, u32[]{:S(2)}, u32[]{:S(2)}) collective-permute-start(bf16[8,128]{1,0:T(8,128)(2,1)S(1)} %copy.94), channel_id=1, source_target_pairs={{0,32},{32,64},{64,96},{96,128},{128,160},{160,192},{192,224},{224... | collective-permute-start | bytes 6152 | tf_op jit(solution)/shard_map/while/body/eval_jaxpr/ppermute | solution.py:21
  134.2 13.7 %collective-permute-start = (bf16[192,1024]{1,0:T(8,128)(2,1)S(1)}, bf16[192,1024]{1,0:T(8,128)(2,1)S(1)}, u32[]{:S(2)}, u32[]{:S(2)}) collective-permute-start(bf16[192,1024]{1,0:T(8,128)(2,1)S(1)} %copy.93), channel_id=1, source_target_pairs={{0,32},{32,64},{64,96},{96,128},{128,160},{160,192},{192,224},{224... | collective-permute-start | bytes 1179656 | tf_op jit(solution)/shard_map/while/body/eval_jaxpr/ppermute | solution.py:21
  148.5 10.9 %collective-permute-start.1 = (bf16[8,128]{1,0:T(8,128)(2,1)S(1)}, bf16[8,128]{1,0:T(8,128)(2,1)}, u32[]{:S(2)}, u32[]{:S(2)}) collective-permute-start(bf16[8,128]{1,0:T(8,128)(2,1)S(1)} %copy.94), channel_id=1, source_target_pairs={{0,32},{32,64},{64,96},{96,128},{128,160},{160,192},{192,224},{224... | collective-permute-start | bytes 6152 | tf_op jit(solution)/shard_map/while/body/eval_jaxpr/ppermute | solution.py:21
  167.3 5.8 %collective-permute-start = (bf16[192,1024]{1,0:T(8,128)(2,1)S(1)}, bf16[192,1024]{1,0:T(8,128)(2,1)S(1)}, u32[]{:S(2)}, u32[]{:S(2)}) collective-permute-start(bf16[192,1024]{1,0:T(8,128)(2,1)S(1)} %copy.93), channel_id=1, source_target_pairs={{0,32},{32,64},{64,96},{96,128},{128,160},{160,192},{192,224},{224... | collective-permute-start | bytes 1179656 | tf_op jit(solution)/shard_map/while/body/eval_jaxpr/ppermute | solution.py:21
  173.8 13.2 %collective-permute-start.1 = (bf16[8,128]{1,0:T(8,128)(2,1)S(1)}, bf16[8,128]{1,0:T(8,128)(2,1)}, u32[]{:S(2)}, u32[]{:S(2)}) collective-permute-start(bf16[8,128]{1,0:T(8,128)(2,1)S(1)} %copy.94), channel_id=1, source_target_pairs={{0,32},{32,64},{64,96},{96,128},{128,160},{160,192},{192,224},{224... | collective-permute-start | bytes 6152 | tf_op jit(solution)/shard_map/while/body/eval_jaxpr/ppermute | solution.py:21
  193.0 11.0 %collective-permute-start = (bf16[192,1024]{1,0:T(8,128)(2,1)S(1)}, bf16[192,1024]{1,0:T(8,128)(2,1)S(1)}, u32[]{:S(2)}, u32[]{:S(2)}) collective-permute-start(bf16[192,1024]{1,0:T(8,128)(2,1)S(1)} %copy.93), channel_id=1, source_target_pairs={{0,32},{32,64},{64,96},{96,128},{128,160},{160,192},{192,224},{224... | collective-permute-start | bytes 1179656 | tf_op jit(solution)/shard_map/while/body/eval_jaxpr/ppermute | solution.py:21
  204.7 12.0 %collective-permute-start.1 = (bf16[8,128]{1,0:T(8,128)(2,1)S(1)}, bf16[8,128]{1,0:T(8,128)(2,1)}, u32[]{:S(2)}, u32[]{:S(2)}) collective-permute-start(bf16[8,128]{1,0:T(8,128)(2,1)S(1)} %copy.94), channel_id=1, source_target_pairs={{0,32},{32,64},{64,96},{96,128},{128,160},{160,192},{192,224},{224... | collective-permute-start | bytes 6152 | tf_op jit(solution)/shard_map/while/body/eval_jaxpr/ppermute | solution.py:21
  222.8 4.7 %collective-permute-start = (bf16[192,1024]{1,0:T(8,128)(2,1)S(1)}, bf16[192,1024]{1,0:T(8,128)(2,1)S(1)}, u32[]{:S(2)}, u32[]{:S(2)}) collective-permute-start(bf16[192,1024]{1,0:T(8,128)(2,1)S(1)} %copy.93), channel_id=1, source_target_pairs={{0,32},{32,64},{64,96},{96,128},{128,160},{160,192},{192,224},{224... | collective-permute-start | bytes 1179656 | tf_op jit(solution)/shard_map/while/body/eval_jaxpr/ppermute | solution.py:21
  228.2 13.9 %collective-permute-start.1 = (bf16[8,128]{1,0:T(8,128)(2,1)S(1)}, bf16[8,128]{1,0:T(8,128)(2,1)}, u32[]{:S(2)}, u32[]{:S(2)}) collective-permute-start(bf16[8,128]{1,0:T(8,128)(2,1)S(1)} %copy.94), channel_id=1, source_target_pairs={{0,32},{32,64},{64,96},{96,128},{128,160},{160,192},{192,224},{224... | collective-permute-start | bytes 6152 | tf_op jit(solution)/shard_map/while/body/eval_jaxpr/ppermute | solution.py:21
  253.7 7.7 %all_to_all.21 = bf16[4,256,96]{1,2,0:T(8,128)(2,1)S(1)} all-to-all(bf16[4,256,96]{1,2,0:T(8,128)(2,1)S(1)} %bitcast.74), channel_id=1, replica_groups=mesh['seq_hi'=16,'seq_lo'=4,'tp'=8] {'seq_lo'}, dimensions={0} | all-to-all | bytes 393216 | tf_op jit(solution)/shard_map/all_to_all | solution.py:161
  263.7 4.4 %all-to-all-start.2 = ((bf16[8,256,384]{2,1,0:T(8,128)(2,1)}), bf16[8,256,384]{2,1,0:T(8,128)(2,1)}, u32[]{:S(2)}, u32[]{:S(2)}) async-start(bf16[8,256,384]{2,1,0:T(8,128)(2,1)} %bitcast.59), calls=%async_computation.2 | async-start | bytes 3145728 | tf_op jit(solution)/shard_map/all_to_all | solution.py:173
  270.0 19.8 %all-to-all-done.2 = bf16[8,256,384]{2,1,0:T(8,128)(2,1)} async-done(((bf16[8,256,384]{2,1,0:T(8,128)(2,1)}), bf16[8,256,384]{2,1,0:T(8,128)(2,1)}, u32[]{:S(2)}, u32[]{:S(2)}) %all-to-all-start.2) | async-done | bytes 1572896 | tf_op jit(solution)/shard_map/all_to_all | solution.py:173
  292.2 3.3 %all-to-all-start.3 = ((f32[8,1,256]{2,1,0:T(1,128)}), f32[8,1,256]{2,1,0:T(1,128)S(1)}, u32[]{:S(2)}, u32[]{:S(2)}) async-start(f32[8,1,256]{2,1,0:T(1,128)} %broadcast_in_dim.168), calls=%async_computation.3 | async-start | bytes 16384 | tf_op jit(solution)/shard_map/all_to_all | solution.py:179
  297.3 4.4 %all-to-all-done.3 = f32[8,1,256]{2,1,0:T(1,128)S(1)} async-done(((f32[8,1,256]{2,1,0:T(1,128)}), f32[8,1,256]{2,1,0:T(1,128)S(1)}, u32[]{:S(2)}, u32[]{:S(2)}) %all-to-all-start.3) | async-done | bytes 8224 | tf_op jit(solution)/shard_map/all_to_all | solution.py:179
  (307 shorter events, 81.8 us)
Async XLA Ops:
  0.6 260.7 %copy-start = (bf16[384,3072]{1,0:T(8,128)(2,1)S(1)}, bf16[384,3072]{1,0:T(8,128)(2,1)}, u32[]{:S(2)}) copy-start(bf16[384,3072]{1,0:T(8,128)(2,1)} %param.15) | copy-start | bytes 7077892
  8.3 13.1 %all-to-all-start = ((bf16[4,256,290]{1,2,0:T(8,128)(2,1)}), bf16[4,256,290]{1,2,0:T(8,128)(2,1)S(1)}, u32[]{:S(2)}, u32[]{:S(2)}) async-start(bf16[4,256,290]{1,2,0:T(8,128)(2,1)} %bitcast.70), calls=%async_computation | async-start | bytes 1212416 | tf_op jit(solution)/shard_map/all_to_all | solution.py:108
  11.8 27.3 %copy-start.16 = (bf16[32]{0:T(256)(128)(2,1)}, bf16[32]{0:T(256)(128)(2,1)S(1)}, u32[]{:S(2)}) copy-start(bf16[32]{0:T(256)(128)(2,1)S(1)} %add_convert_fusion.5) | copy-start | bytes 196
  22.1 17.9 %copy-start.1 = (bf16[37,8,4,256]{3,1,2,0:T(8,128)(2,1)}, bf16[37,8,4,256]{3,1,2,0:T(8,128)(2,1)S(1)}, u32[]{:S(2)}) copy-start(bf16[37,8,4,256]{3,1,2,0:T(8,128)(2,1)S(1)} %copy.69) | copy-start | bytes 1818628
  22.7 16.4 %copy-start.10 = (bf16[1024]{0:T(1024)(128)(2,1)}, bf16[1024]{0:T(1024)(128)(2,1)S(1)}, u32[]{:S(2)}) copy-start(bf16[1024]{0:T(1024)(128)(2,1)S(1)} %get-tuple-element.373) | copy-start | bytes 6148
  23.5 17.2 %collective-permute-start.3 = (bf16[8,128]{1,0:T(8,128)(2,1)S(1)}, bf16[8,128]{1,0:T(8,128)(2,1)}, u32[]{:S(2)}, u32[]{:S(2)}) collective-permute-start(bf16[8,128]{1,0:T(8,128)(2,1)S(1)} %bitcast_select_fusion), channel_id=1, source_target_pairs={{0,32},{32,64},{64,96},{96,128},{128,160},{160,192},{192,224},{224... | collective-permute-start | bytes 6152 | tf_op jit(solution)/shard_map/ppermute | solution.py:21
  30.5 22.3 %collective-permute-start.2 = (bf16[192,1024]{1,0:T(8,128)(2,1)}, bf16[192,1024]{1,0:T(8,128)(2,1)S(1)}, u32[]{:S(2)}, u32[]{:S(2)}) collective-permute-start(bf16[192,1024]{1,0:T(8,128)(2,1)} %slice_bitcast_fusion), channel_id=1, source_target_pairs={{0,32},{32,64},{64,96},{96,128},{128,160},{160,192},{192,224},{224... | collective-permute-start | bytes 1179656 | tf_op jit(solution)/shard_map/ppermute | solution.py:21
  52.8 21.3 %collective-permute-start = (bf16[192,1024]{1,0:T(8,128)(2,1)S(1)}, bf16[192,1024]{1,0:T(8,128)(2,1)S(1)}, u32[]{:S(2)}, u32[]{:S(2)}) collective-permute-start(bf16[192,1024]{1,0:T(8,128)(2,1)S(1)} %copy.93), channel_id=1, source_target_pairs={{0,32},{32,64},{64,96},{96,128},{128,160},{160,192},{192,224},{224... | collective-permute-start | bytes 1179656 | tf_op jit(solution)/shard_map/while/body/eval_jaxpr/ppermute | solution.py:21
  58.8 15.4 %collective-permute-start.1 = (bf16[8,128]{1,0:T(8,128)(2,1)S(1)}, bf16[8,128]{1,0:T(8,128)(2,1)}, u32[]{:S(2)}, u32[]{:S(2)}) collective-permute-start(bf16[8,128]{1,0:T(8,128)(2,1)S(1)} %copy.94), channel_id=1, source_target_pairs={{0,32},{32,64},{64,96},{96,128},{128,160},{160,192},{192,224},{224... | collective-permute-start | bytes 6152 | tf_op jit(solution)/shard_map/while/body/eval_jaxpr/ppermute | solution.py:21
  74.7 26.8 %collective-permute-start = (bf16[192,1024]{1,0:T(8,128)(2,1)S(1)}, bf16[192,1024]{1,0:T(8,128)(2,1)S(1)}, u32[]{:S(2)}, u32[]{:S(2)}) collective-permute-start(bf16[192,1024]{1,0:T(8,128)(2,1)S(1)} %copy.93), channel_id=1, source_target_pairs={{0,32},{32,64},{64,96},{96,128},{128,160},{160,192},{192,224},{224... | collective-permute-start | bytes 1179656 | tf_op jit(solution)/shard_map/while/body/eval_jaxpr/ppermute | solution.py:21
  84.3 17.3 %collective-permute-start.1 = (bf16[8,128]{1,0:T(8,128)(2,1)S(1)}, bf16[8,128]{1,0:T(8,128)(2,1)}, u32[]{:S(2)}, u32[]{:S(2)}) collective-permute-start(bf16[8,128]{1,0:T(8,128)(2,1)S(1)} %copy.94), channel_id=1, source_target_pairs={{0,32},{32,64},{64,96},{96,128},{128,160},{160,192},{192,224},{224... | collective-permute-start | bytes 6152 | tf_op jit(solution)/shard_map/while/body/eval_jaxpr/ppermute | solution.py:21
  102.1 31.4 %collective-permute-start = (bf16[192,1024]{1,0:T(8,128)(2,1)S(1)}, bf16[192,1024]{1,0:T(8,128)(2,1)S(1)}, u32[]{:S(2)}, u32[]{:S(2)}) collective-permute-start(bf16[192,1024]{1,0:T(8,128)(2,1)S(1)} %copy.93), channel_id=1, source_target_pairs={{0,32},{32,64},{64,96},{96,128},{128,160},{160,192},{192,224},{224... | collective-permute-start | bytes 1179656 | tf_op jit(solution)/shard_map/while/body/eval_jaxpr/ppermute | solution.py:21
  117.9 15.7 %collective-permute-start.1 = (bf16[8,128]{1,0:T(8,128)(2,1)S(1)}, bf16[8,128]{1,0:T(8,128)(2,1)}, u32[]{:S(2)}, u32[]{:S(2)}) collective-permute-start(bf16[8,128]{1,0:T(8,128)(2,1)S(1)} %copy.94), channel_id=1, source_target_pairs={{0,32},{32,64},{64,96},{96,128},{128,160},{160,192},{192,224},{224... | collective-permute-start | bytes 6152 | tf_op jit(solution)/shard_map/while/body/eval_jaxpr/ppermute | solution.py:21
  134.2 33.1 %collective-permute-start = (bf16[192,1024]{1,0:T(8,128)(2,1)S(1)}, bf16[192,1024]{1,0:T(8,128)(2,1)S(1)}, u32[]{:S(2)}, u32[]{:S(2)}) collective-permute-start(bf16[192,1024]{1,0:T(8,128)(2,1)S(1)} %copy.93), channel_id=1, source_target_pairs={{0,32},{32,64},{64,96},{96,128},{128,160},{160,192},{192,224},{224... | collective-permute-start | bytes 1179656 | tf_op jit(solution)/shard_map/while/body/eval_jaxpr/ppermute | solution.py:21
  148.5 18.7 %collective-permute-start.1 = (bf16[8,128]{1,0:T(8,128)(2,1)S(1)}, bf16[8,128]{1,0:T(8,128)(2,1)}, u32[]{:S(2)}, u32[]{:S(2)}) collective-permute-start(bf16[8,128]{1,0:T(8,128)(2,1)S(1)} %copy.94), channel_id=1, source_target_pairs={{0,32},{32,64},{64,96},{96,128},{128,160},{160,192},{192,224},{224... | collective-permute-start | bytes 6152 | tf_op jit(solution)/shard_map/while/body/eval_jaxpr/ppermute | solution.py:21
  167.3 25.2 %collective-permute-start = (bf16[192,1024]{1,0:T(8,128)(2,1)S(1)}, bf16[192,1024]{1,0:T(8,128)(2,1)S(1)}, u32[]{:S(2)}, u32[]{:S(2)}) collective-permute-start(bf16[192,1024]{1,0:T(8,128)(2,1)S(1)} %copy.93), channel_id=1, source_target_pairs={{0,32},{32,64},{64,96},{96,128},{128,160},{160,192},{192,224},{224... | collective-permute-start | bytes 1179656 | tf_op jit(solution)/shard_map/while/body/eval_jaxpr/ppermute | solution.py:21
  173.8 18.6 %collective-permute-start.1 = (bf16[8,128]{1,0:T(8,128)(2,1)S(1)}, bf16[8,128]{1,0:T(8,128)(2,1)}, u32[]{:S(2)}, u32[]{:S(2)}) collective-permute-start(bf16[8,128]{1,0:T(8,128)(2,1)S(1)} %copy.94), channel_id=1, source_target_pairs={{0,32},{32,64},{64,96},{96,128},{128,160},{160,192},{192,224},{224... | collective-permute-start | bytes 6152 | tf_op jit(solution)/shard_map/while/body/eval_jaxpr/ppermute | solution.py:21
  193.0 29.2 %collective-permute-start = (bf16[192,1024]{1,0:T(8,128)(2,1)S(1)}, bf16[192,1024]{1,0:T(8,128)(2,1)S(1)}, u32[]{:S(2)}, u32[]{:S(2)}) collective-permute-start(bf16[192,1024]{1,0:T(8,128)(2,1)S(1)} %copy.93), channel_id=1, source_target_pairs={{0,32},{32,64},{64,96},{96,128},{128,160},{160,192},{192,224},{224... | collective-permute-start | bytes 1179656 | tf_op jit(solution)/shard_map/while/body/eval_jaxpr/ppermute | solution.py:21
  204.7 17.4 %collective-permute-start.1 = (bf16[8,128]{1,0:T(8,128)(2,1)S(1)}, bf16[8,128]{1,0:T(8,128)(2,1)}, u32[]{:S(2)}, u32[]{:S(2)}) collective-permute-start(bf16[8,128]{1,0:T(8,128)(2,1)S(1)} %copy.94), channel_id=1, source_target_pairs={{0,32},{32,64},{64,96},{96,128},{128,160},{160,192},{192,224},{224... | collective-permute-start | bytes 6152 | tf_op jit(solution)/shard_map/while/body/eval_jaxpr/ppermute | solution.py:21
  222.8 24.7 %collective-permute-start = (bf16[192,1024]{1,0:T(8,128)(2,1)S(1)}, bf16[192,1024]{1,0:T(8,128)(2,1)S(1)}, u32[]{:S(2)}, u32[]{:S(2)}) collective-permute-start(bf16[192,1024]{1,0:T(8,128)(2,1)S(1)} %copy.93), channel_id=1, source_target_pairs={{0,32},{32,64},{64,96},{96,128},{128,160},{160,192},{192,224},{224... | collective-permute-start | bytes 1179656 | tf_op jit(solution)/shard_map/while/body/eval_jaxpr/ppermute | solution.py:21
  228.2 19.3 %collective-permute-start.1 = (bf16[8,128]{1,0:T(8,128)(2,1)S(1)}, bf16[8,128]{1,0:T(8,128)(2,1)}, u32[]{:S(2)}, u32[]{:S(2)}) collective-permute-start(bf16[8,128]{1,0:T(8,128)(2,1)S(1)} %copy.94), channel_id=1, source_target_pairs={{0,32},{32,64},{64,96},{96,128},{128,160},{160,192},{192,224},{224... | collective-permute-start | bytes 6152 | tf_op jit(solution)/shard_map/while/body/eval_jaxpr/ppermute | solution.py:21
  263.7 27.7 %copy-start.9 = (bf16[256,384]{1,0:T(8,128)(2,1)S(1)}, bf16[256,384]{1,0:T(8,128)(2,1)}, u32[]{:S(2)}) copy-start(bf16[256,384]{1,0:T(8,128)(2,1)} %param.14) | copy-start | bytes 589828
  263.7 26.0 %all-to-all-start.2 = ((bf16[8,256,384]{2,1,0:T(8,128)(2,1)}), bf16[8,256,384]{2,1,0:T(8,128)(2,1)}, u32[]{:S(2)}, u32[]{:S(2)}) async-start(bf16[8,256,384]{2,1,0:T(8,128)(2,1)} %bitcast.59), calls=%async_computation.2 | async-start | bytes 3145728 | tf_op jit(solution)/shard_map/all_to_all | solution.py:173
  292.2 9.5 %all-to-all-start.3 = ((f32[8,1,256]{2,1,0:T(1,128)}), f32[8,1,256]{2,1,0:T(1,128)S(1)}, u32[]{:S(2)}, u32[]{:S(2)}) async-start(f32[8,1,256]{2,1,0:T(1,128)} %broadcast_in_dim.168), calls=%async_computation.3 | async-start | bytes 16384 | tf_op jit(solution)/shard_map/all_to_all | solution.py:179
  (57 other events, 159.4 us)

commit v7 on v3

--- a/solution.py
+++ b/solution.py
@@ -141,9 +141,10 @@
     reach_count = lo_count * hi_count // 2 * tok_count // chunk_count
     seen_first = first_of(chunk_qtag, chunk_row * chunk_count + chunk_offsets)
     moved = passed_along(ring_own, "seq_hi", 1)
-    (softmax_state, seen_first), moved = lax.fori_loop(
-        0, reach_count - 1, cycle_turn, ((softmax_state, seen_first), moved)
-    )
+    loop_state = ((softmax_state, seen_first), moved)
+    for turn_index in range(reach_count - 1):
+        loop_state = cycle_turn(turn_index, loop_state)
+    (softmax_state, seen_first), moved = loop_state
     softmax_state, first_tok = visit_block((softmax_state, seen_first), moved, reach_count)
     member = segment_ids[:, None] == jnp.arange(seg_count, dtype=jnp.int32)[None, :]
     position = tok_index - jnp.sum(jnp.where(member, first_tok[None, :], 0), axis=1)

time: 294 us -> 313 us (1.065)
  blocking collectives: 7.67 us -> 27.7 us
  starting transfers between devices: 94.8 us -> 110 us
  local copies, waits for them, and re-layouts: 25.2 us -> 17.5 us
  other arithmetic: 18.9 us -> 12.8 us
    dot_general x9, matrix products: 34.5 us -> 11.6 us  [attend(): jnp.einsum('qk,kd->qd', unnormed.astype(jnp.bfloat16), val_heads, preferr...]
    dot_general x9, matrix products: 15.3 us -> 35.1 us  [attend(): jnp.einsum('qd,kd->qk', query_heads, key_heads, preferred_element_type=jn...]
    all_to_all x1, starting transfers between devices: 4.42 us -> 19.3 us  [per_device(): gathered = lax.all_to_all(pieces, 'tp', 0, 0, tiled=True)]
    while x28 -> x0, local copies, waits for them, and re-layouts: 13.6 us -> none
    all_to_all x0 -> x1, blocking collectives: none -> 13.1 us  [per_device(): chunk = lax.all_to_all(payload, 'seq_lo', 0, 0, tiled=True)]
    ppermute x8, waiting for transfers between devices: 59.9 us -> 70.4 us  [passed_along(): return lax.ppermute(block, axis, route)]
    all_to_all x1 -> x0, waiting for transfers between devices: 9.62 us -> none  [per_device(): chunk = lax.all_to_all(payload, 'seq_lo', 0, 0, tiled=True)]
    reduce_sum x9 -> x1, other arithmetic: 12 us -> 4.09 us  [attend(): row_total = row_total * rescale + jnp.sum(unnormed, axis=-1)]
  transfers between devices with their start and end apart: 11 -> 10, of which waited for: 9 -> 9; matrix products, arithmetic and copies ran while one was open for 21% -> 10% of each run, Pallas kernels for 0% -> 0%
where the time goes in v7:
time: 313 us; the launch traced here: 312 us
  starting transfers between devices  110 us (35%)
  waiting for transfers between devices  94.7 us (30%)
  matrix products  47.7 us (15%)
  blocking collectives  27.7 us (9%)
  local copies, waits for them, and re-layouts  17.5 us (6%)
  other arithmetic  12.8 us (4%)
    ppermute x8, starting transfers between devices, passed_along(): return lax.ppermute(block, axis, route)  87.5 us
    ppermute x8, waiting for transfers between devices, passed_along(): return lax.ppermute(block, axis, route)  70.4 us
    dot_general x9, matrix products, attend(): jnp.einsum('qd,kd->qk', query_heads, key_heads, preferred_element_type=jn...  35.1 us
    all_to_all x1, waiting for transfers between devices, per_device(): gathered = lax.all_to_all(pieces, 'tp', 0, 0, tiled=True)  19.9 us
    all_to_all x1, starting transfers between devices, per_device(): gathered = lax.all_to_all(pieces, 'tp', 0, 0, tiled=True)  19.3 us
    all_to_all x1, blocking collectives, per_device(): lax.all_to_all(chunk_attn.reshape(lo_count, tok_count, HEAD_DIM), 'seq_lo...  14.6 us
    all_to_all x1, blocking collectives, per_device(): chunk = lax.all_to_all(payload, 'seq_lo', 0, 0, tiled=True)  13.1 us
    dot_general x9, matrix products, attend(): jnp.einsum('qk,kd->qd', unnormed.astype(jnp.bfloat16), val_heads, preferr...  11.6 us
  transfers between devices with their start and end apart: 10, of which 9 were waited for; matrix products, arithmetic and copies ran while one was open for 10% of the time, Pallas kernels for 0%

profile of v7, /device:TPU:176, one launch (start us, length us, event | category | flops | bytes accessed | tf_op | source)
XLA Modules:
  0.0 311.9 jit_solution(8910766082632031916)
XLA Ops:
  8.1 13.1 %all_to_all.21 = bf16[4,256,290]{1,2,0:T(8,128)(2,1)S(1)} all-to-all(bf16[4,256,290]{1,2,0:T(8,128)(2,1)} %bitcast.5), channel_id=1, replica_groups=mesh['seq_hi'=16,'seq_lo'=4,'tp'=8] {'seq_lo'}, dimensions={0} | all-to-all | bytes 1187840 | tf_op jit(solution)/shard_map/all_to_all | solution.py:103
  21.9 6.6 %collective-permute-start = (bf16[1024,194]{0,1:T(8,128)(2,1)S(1)}, bf16[1024,194]{0,1:T(8,128)(2,1)S(1)}, u32[]{:S(2)}, u32[]{:S(2)}) collective-permute-start(bf16[1024,194]{0,1:T(8,128)(2,1)S(1)} %slice.179), channel_id=1, source_target_pairs={{0,32},{32,64},{64,96},{96,128},{128,160},{160,192},{192,224},{224... | collective-permute-start | bytes 1191944 | tf_op jit(solution)/shard_map/ppermute | solution.py:21
  28.5 15.6 %collective-permute-done = bf16[1024,194]{0,1:T(8,128)(2,1)S(1)} collective-permute-done((bf16[1024,194]{0,1:T(8,128)(2,1)S(1)}, bf16[1024,194]{0,1:T(8,128)(2,1)S(1)}, u32[]{:S(2)}, u32[]{:S(2)}) %collective-permute-start) | collective-permute-done | bytes 397344 | tf_op jit(solution)/shard_map/ppermute | solution.py:21
  44.2 12.0 %collective-permute-start.1 = (bf16[1024,194]{0,1:T(8,128)(2,1)S(1)}, bf16[1024,194]{0,1:T(8,128)(2,1)S(1)}, u32[]{:S(2)}, u32[]{:S(2)}) collective-permute-start(bf16[1024,194]{0,1:T(8,128)(2,1)S(1)} %collective-permute-done), channel_id=1, source_target_pairs={{0,32},{32,64},{64,96},{96,128},{128,160},{160,192},{192,224},{224... | collective-permute-start | bytes 1191944 | tf_op jit(solution)/shard_map/ppermute | solution.py:21
  59.6 13.1 %collective-permute-done.1 = bf16[1024,194]{0,1:T(8,128)(2,1)S(1)} collective-permute-done((bf16[1024,194]{0,1:T(8,128)(2,1)S(1)}, bf16[1024,194]{0,1:T(8,128)(2,1)S(1)}, u32[]{:S(2)}, u32[]{:S(2)}) %collective-permute-start.1) | collective-permute-done | bytes 397344 | tf_op jit(solution)/shard_map/ppermute | solution.py:21
  72.7 10.2 %collective-permute-start.2 = (bf16[1024,194]{0,1:T(8,128)(2,1)S(1)}, bf16[1024,194]{0,1:T(8,128)(2,1)S(1)}, u32[]{:S(2)}, u32[]{:S(2)}) collective-permute-start(bf16[1024,194]{0,1:T(8,128)(2,1)S(1)} %collective-permute-done.1), channel_id=1, source_target_pairs={{0,32},{32,64},{64,96},{96,128},{128,160},{160,192},{192,224},{224... | collective-permute-start | bytes 1191944 | tf_op jit(solution)/shard_map/ppermute | solution.py:21
  84.3 13.0 %collective-permute-done.2 = bf16[1024,194]{0,1:T(8,128)(2,1)S(1)} collective-permute-done((bf16[1024,194]{0,1:T(8,128)(2,1)S(1)}, bf16[1024,194]{0,1:T(8,128)(2,1)S(1)}, u32[]{:S(2)}, u32[]{:S(2)}) %collective-permute-start.2) | collective-permute-done | bytes 397344 | tf_op jit(solution)/shard_map/ppermute | solution.py:21
  97.3 10.7 %collective-permute-start.3 = (bf16[1024,194]{0,1:T(8,128)(2,1)S(1)}, bf16[1024,194]{0,1:T(8,128)(2,1)S(1)}, u32[]{:S(2)}, u32[]{:S(2)}) collective-permute-start(bf16[1024,194]{0,1:T(8,128)(2,1)S(1)} %collective-permute-done.2), channel_id=1, source_target_pairs={{0,32},{32,64},{64,96},{96,128},{128,160},{160,192},{192,224},{224... | collective-permute-start | bytes 1191944 | tf_op jit(solution)/shard_map/ppermute | solution.py:21
  111.3 5.8 %collective-permute-done.3 = bf16[1024,194]{0,1:T(8,128)(2,1)S(1)} collective-permute-done((bf16[1024,194]{0,1:T(8,128)(2,1)S(1)}, bf16[1024,194]{0,1:T(8,128)(2,1)S(1)}, u32[]{:S(2)}, u32[]{:S(2)}) %collective-permute-start.3) | collective-permute-done | bytes 397344 | tf_op jit(solution)/shard_map/ppermute | solution.py:21
  117.1 12.3 %collective-permute-start.4 = (bf16[1024,194]{0,1:T(8,128)(2,1)S(1)}, bf16[1024,194]{0,1:T(8,128)(2,1)S(1)}, u32[]{:S(2)}, u32[]{:S(2)}) collective-permute-start(bf16[1024,194]{0,1:T(8,128)(2,1)S(1)} %collective-permute-done.3), channel_id=1, source_target_pairs={{0,32},{32,64},{64,96},{96,128},{128,160},{160,192},{192,224},{224... | collective-permute-start | bytes 1191944 | tf_op jit(solution)/shard_map/ppermute | solution.py:21
  132.7 6.0 %collective-permute-done.4 = bf16[1024,194]{0,1:T(8,128)(2,1)S(1)} collective-permute-done((bf16[1024,194]{0,1:T(8,128)(2,1)S(1)}, bf16[1024,194]{0,1:T(8,128)(2,1)S(1)}, u32[]{:S(2)}, u32[]{:S(2)}) %collective-permute-start.4) | collective-permute-done | bytes 397344 | tf_op jit(solution)/shard_map/ppermute | solution.py:21
  138.6 12.0 %collective-permute-start.5 = (bf16[1024,194]{0,1:T(8,128)(2,1)S(1)}, bf16[1024,194]{0,1:T(8,128)(2,1)S(1)}, u32[]{:S(2)}, u32[]{:S(2)}) collective-permute-start(bf16[1024,194]{0,1:T(8,128)(2,1)S(1)} %collective-permute-done.4), channel_id=1, source_target_pairs={{0,32},{32,64},{64,96},{96,128},{128,160},{160,192},{192,224},{224... | collective-permute-start | bytes 1191944 | tf_op jit(solution)/shard_map/ppermute | solution.py:21
  154.0 5.0 %collective-permute-done.5 = bf16[1024,194]{0,1:T(8,128)(2,1)S(1)} collective-permute-done((bf16[1024,194]{0,1:T(8,128)(2,1)S(1)}, bf16[1024,194]{0,1:T(8,128)(2,1)S(1)}, u32[]{:S(2)}, u32[]{:S(2)}) %collective-permute-start.5) | collective-permute-done | bytes 397344 | tf_op jit(solution)/shard_map/ppermute | solution.py:21
  159.0 11.4 %collective-permute-start.6 = (bf16[1024,194]{0,1:T(8,128)(2,1)S(1)}, bf16[1024,194]{0,1:T(8,128)(2,1)S(1)}, u32[]{:S(2)}, u32[]{:S(2)}) collective-permute-start(bf16[1024,194]{0,1:T(8,128)(2,1)S(1)} %collective-permute-done.5), channel_id=1, source_target_pairs={{0,32},{32,64},{64,96},{96,128},{128,160},{160,192},{192,224},{224... | collective-permute-start | bytes 1191944 | tf_op jit(solution)/shard_map/ppermute | solution.py:21
  171.7 11.9 %collective-permute-done.6 = bf16[1024,194]{0,1:T(8,128)(2,1)S(1)} collective-permute-done((bf16[1024,194]{0,1:T(8,128)(2,1)S(1)}, bf16[1024,194]{0,1:T(8,128)(2,1)S(1)}, u32[]{:S(2)}, u32[]{:S(2)}) %collective-permute-start.6) | collective-permute-done | bytes 397344 | tf_op jit(solution)/shard_map/ppermute | solution.py:21
  183.6 12.3 %collective-permute-start.7 = (bf16[1024,194]{0,1:T(8,128)(2,1)S(1)}, bf16[1024,194]{0,1:T(8,128)(2,1)}, u32[]{:S(2)}, u32[]{:S(2)}) collective-permute-start(bf16[1024,194]{0,1:T(8,128)(2,1)S(1)} %collective-permute-done.6), channel_id=1, source_target_pairs={{0,32},{32,64},{64,96},{96,128},{128,160},{160,192},{192,224},{224... | collective-permute-start | bytes 1191944 | tf_op jit(solution)/shard_map/ppermute | solution.py:21
  197.3 11.2 %fusion.27 = (f32[1024]{0:T(1024)S(1)}, f32[1024]{0:T(1024)S(1)}, f32[1024]{0:T(1024)S(1)}, f32[1024]{0:T(1024)S(1)}, f32[1024]{0:T(1024)S(1)}, /*index=5*/f32[1...) fusion(f32[1024,1024]{0,1:T(8,128)} %get-tuple-element.77, ...), kind=kOutput, calls=%fused_computation.50 | convolution fusion | flops 250601472 | bytes 34002944 | tf_op jit(solution)/shard_map/qd,kd->qk/dot_general | solution.py:50
  210.0 10.6 %fusion.11 = (f32[1024]{0:T(1024)S(1)}, f32[1024]{0:T(1024)S(1)}, f32[1024]{0:T(1024)S(1)}, f32[1024]{0:T(1024)S(1)}, f32[1024]{0:T(1024)S(1)}, /*index=5*/f32[1024]{0:T(1024)S(1)}, f32[1024,1024]{0,1:T(8,128)S(1)}) fusion(f32[1024,1024]{0,1:T(8,128)} %get-tuple-element.78, f32[1024]{0:T(1024)S(1)} %get-tuple-element.65, ...), kind=kOutput, calls=%fused_computation.34 | convolution fusion | flops 236972032 | bytes 25618432 | tf_op jit(solution)/shard_map/qd,kd->qk/dot_general | solution.py:50
  220.6 4.1 %fusion.21 = (f32[1024]{0:T(1024)S(1)}, f32[1024]{0:T(1024)S(1)}, f32[1024]{0:T(1024)S(1)}) fusion(f32[1024,1024]{0,1:T(8,128)S(1)} %fusion.131, f32[1024]{0:T(1024)S(1)} %get-tuple-element.60, bf16[1024]{0:T(1024)(128)(2,1)S(1)} %get-tuple-element.4, bf16[1024]{0:T(1024)(128)(2,1)S(1)} %get-tuple-element.16, f32[1024]{0:T(1024)S(1)} %get-tuple-element.59, ...), kind=kLoop, calls=%fused_computation.44 | loop fusion | flops 18871296 | bytes 12615680 | tf_op jit(solution)/shard_map/reduce_sum | solution.py:57
  240.5 14.6 %all_to_all.22 = bf16[4,256,96]{1,2,0:T(8,128)(2,1)S(1)} all-to-all(bf16[4,256,96]{1,2,0:T(8,128)(2,1)S(1)} %bitcast.57), channel_id=1, replica_groups=mesh['seq_hi'=16,'seq_lo'=4,'tp'=8] {'seq_lo'}, dimensions={0} | all-to-all | bytes 393216 | tf_op jit(solution)/shard_map/all_to_all | solution.py:154
  257.5 19.3 %all-to-all-start.2 = ((bf16[8,256,384]{2,1,0:T(8,128)(2,1)}), bf16[8,256,384]{2,1,0:T(8,128)(2,1)}, u32[]{:S(2)}, u32[]{:S(2)}) async-start(bf16[8,256,384]{2,1,0:T(8,128)(2,1)} %bitcast.50), calls=%async_computation.2 | async-start | bytes 3145728 | tf_op jit(solution)/shard_map/all_to_all | solution.py:166
  278.3 19.9 %all-to-all-done.2 = bf16[8,256,384]{2,1,0:T(8,128)(2,1)} async-done(((bf16[8,256,384]{2,1,0:T(8,128)(2,1)}), bf16[8,256,384]{2,1,0:T(8,128)(2,1)}, u32[]{:S(2)}, u32[]{:S(2)}) %all-to-all-start.2) | async-done | bytes 1572896 | tf_op jit(solution)/shard_map/all_to_all | solution.py:166
  301.6 3.3 %all-to-all-start.3 = ((f32[8,1,256]{2,1,0:T(1,128)}), f32[8,1,256]{2,1,0:T(1,128)S(1)}, u32[]{:S(2)}, u32[]{:S(2)}) async-start(f32[8,1,256]{2,1,0:T(1,128)} %broadcast_in_dim.189), calls=%async_computation.3 | async-start | bytes 16384 | tf_op jit(solution)/shard_map/all_to_all | solution.py:172
  306.7 4.4 %all-to-all-done.3 = f32[8,1,256]{2,1,0:T(1,128)S(1)} async-done(((f32[8,1,256]{2,1,0:T(1,128)}), f32[8,1,256]{2,1,0:T(1,128)S(1)}, u32[]{:S(2)}, u32[]{:S(2)}) %all-to-all-start.3) | async-done | bytes 8224 | tf_op jit(solution)/shard_map/all_to_all | solution.py:172
  (139 shorter events, 52.1 us)
Async XLA Ops:
  0.6 254.4 %copy-start = (bf16[384,3072]{1,0:T(8,128)(2,1)S(1)}, bf16[384,3072]{1,0:T(8,128)(2,1)}, u32[]{:S(2)}) copy-start(bf16[384,3072]{1,0:T(8,128)(2,1)} %param.13) | copy-start | bytes 7077892
  21.9 22.3 %collective-permute-start = (bf16[1024,194]{0,1:T(8,128)(2,1)S(1)}, bf16[1024,194]{0,1:T(8,128)(2,1)S(1)}, u32[]{:S(2)}, u32[]{:S(2)}) collective-permute-start(bf16[1024,194]{0,1:T(8,128)(2,1)S(1)} %slice.179), channel_id=1, source_target_pairs={{0,32},{32,64},{64,96},{96,128},{128,160},{160,192},{192,224},{224... | collective-permute-start | bytes 1191944 | tf_op jit(solution)/shard_map/ppermute | solution.py:21
  28.5 209.8 %copy-start.7 = (bf16[1024]{0:T(1024)(128)(2,1)}, bf16[1024]{0:T(1024)(128)(2,1)S(1)}, u32[]{:S(2)}) copy-start(bf16[1024]{0:T(1024)(128)(2,1)S(1)} %get-tuple-element.4) | copy-start | bytes 6148
  44.2 28.6 %collective-permute-start.1 = (bf16[1024,194]{0,1:T(8,128)(2,1)S(1)}, bf16[1024,194]{0,1:T(8,128)(2,1)S(1)}, u32[]{:S(2)}, u32[]{:S(2)}) collective-permute-start(bf16[1024,194]{0,1:T(8,128)(2,1)S(1)} %collective-permute-done), channel_id=1, source_target_pairs={{0,32},{32,64},{64,96},{96,128},{128,160},{160,192},{192,224},{224... | collective-permute-start | bytes 1191944 | tf_op jit(solution)/shard_map/ppermute | solution.py:21
  72.7 24.5 %collective-permute-start.2 = (bf16[1024,194]{0,1:T(8,128)(2,1)S(1)}, bf16[1024,194]{0,1:T(8,128)(2,1)S(1)}, u32[]{:S(2)}, u32[]{:S(2)}) collective-permute-start(bf16[1024,194]{0,1:T(8,128)(2,1)S(1)} %collective-permute-done.1), channel_id=1, source_target_pairs={{0,32},{32,64},{64,96},{96,128},{128,160},{160,192},{192,224},{224... | collective-permute-start | bytes 1191944 | tf_op jit(solution)/shard_map/ppermute | solution.py:21
  97.3 19.8 %collective-permute-start.3 = (bf16[1024,194]{0,1:T(8,128)(2,1)S(1)}, bf16[1024,194]{0,1:T(8,128)(2,1)S(1)}, u32[]{:S(2)}, u32[]{:S(2)}) collective-permute-start(bf16[1024,194]{0,1:T(8,128)(2,1)S(1)} %collective-permute-done.2), channel_id=1, source_target_pairs={{0,32},{32,64},{64,96},{96,128},{128,160},{160,192},{192,224},{224... | collective-permute-start | bytes 1191944 | tf_op jit(solution)/shard_map/ppermute | solution.py:21
  117.1 21.6 %collective-permute-start.4 = (bf16[1024,194]{0,1:T(8,128)(2,1)S(1)}, bf16[1024,194]{0,1:T(8,128)(2,1)S(1)}, u32[]{:S(2)}, u32[]{:S(2)}) collective-permute-start(bf16[1024,194]{0,1:T(8,128)(2,1)S(1)} %collective-permute-done.3), channel_id=1, source_target_pairs={{0,32},{32,64},{64,96},{96,128},{128,160},{160,192},{192,224},{224... | collective-permute-start | bytes 1191944 | tf_op jit(solution)/shard_map/ppermute | solution.py:21
  138.6 20.4 %collective-permute-start.5 = (bf16[1024,194]{0,1:T(8,128)(2,1)S(1)}, bf16[1024,194]{0,1:T(8,128)(2,1)S(1)}, u32[]{:S(2)}, u32[]{:S(2)}) collective-permute-start(bf16[1024,194]{0,1:T(8,128)(2,1)S(1)} %collective-permute-done.4), channel_id=1, source_target_pairs={{0,32},{32,64},{64,96},{96,128},{128,160},{160,192},{192,224},{224... | collective-permute-start | bytes 1191944 | tf_op jit(solution)/shard_map/ppermute | solution.py:21
  159.0 24.6 %collective-permute-start.6 = (bf16[1024,194]{0,1:T(8,128)(2,1)S(1)}, bf16[1024,194]{0,1:T(8,128)(2,1)S(1)}, u32[]{:S(2)}, u32[]{:S(2)}) collective-permute-start(bf16[1024,194]{0,1:T(8,128)(2,1)S(1)} %collective-permute-done.5), channel_id=1, source_target_pairs={{0,32},{32,64},{64,96},{96,128},{128,160},{160,192},{192,224},{224... | collective-permute-start | bytes 1191944 | tf_op jit(solution)/shard_map/ppermute | solution.py:21
  183.6 24.9 %collective-permute-start.7 = (bf16[1024,194]{0,1:T(8,128)(2,1)S(1)}, bf16[1024,194]{0,1:T(8,128)(2,1)}, u32[]{:S(2)}, u32[]{:S(2)}) collective-permute-start(bf16[1024,194]{0,1:T(8,128)(2,1)S(1)} %collective-permute-done.6), channel_id=1, source_target_pairs={{0,32},{32,64},{64,96},{96,128},{128,160},{160,192},{192,224},{224... | collective-permute-start | bytes 1191944 | tf_op jit(solution)/shard_map/ppermute | solution.py:21
  256.1 21.2 %copy-start.24 = (s32[2]{0:T(128)S(1)}, s32[2]{0:T(128)}, u32[]{:S(2)}) copy-start(s32[2]{0:T(128)} %param.17) | copy-start | bytes 28
  256.1 21.2 %copy-start.8 = (bf16[1024]{0:T(1024)(128)(2,1)S(1)}, bf16[1024]{0:T(1024)(128)(2,1)}, u32[]{:S(2)}) copy-start(bf16[1024]{0:T(1024)(128)(2,1)} %copy-done.7) | copy-start | bytes 6148
  256.1 21.2 %copy-start.9 = (bf16[1024]{0:T(1024)(128)(2,1)S(1)}, bf16[1024]{0:T(1024)(128)(2,1)}, u32[]{:S(2)}) copy-start(bf16[1024]{0:T(1024)(128)(2,1)} %get-tuple-element.5) | copy-start | bytes 6148
  256.1 21.2 %copy-start.10 = (bf16[1024]{0:T(1024)(128)(2,1)S(1)}, bf16[1024]{0:T(1024)(128)(2,1)}, u32[]{:S(2)}) copy-start(bf16[1024]{0:T(1024)(128)(2,1)} %get-tuple-element.7) | copy-start | bytes 6148
  256.1 21.2 %copy-start.11 = (bf16[1024]{0:T(1024)(128)(2,1)S(1)}, bf16[1024]{0:T(1024)(128)(2,1)}, u32[]{:S(2)}) copy-start(bf16[1024]{0:T(1024)(128)(2,1)} %get-tuple-element.9) | copy-start | bytes 6148
  256.2 21.2 %copy-start.12 = (bf16[1024]{0:T(1024)(128)(2,1)S(1)}, bf16[1024]{0:T(1024)(128)(2,1)}, u32[]{:S(2)}) copy-start(bf16[1024]{0:T(1024)(128)(2,1)} %get-tuple-element.11) | copy-start | bytes 6148
  256.2 21.2 %copy-start.13 = (bf16[1024]{0:T(1024)(128)(2,1)S(1)}, bf16[1024]{0:T(1024)(128)(2,1)}, u32[]{:S(2)}) copy-start(bf16[1024]{0:T(1024)(128)(2,1)} %get-tuple-element.13) | copy-start | bytes 6148
  256.2 21.2 %copy-start.14 = (bf16[1024]{0:T(1024)(128)(2,1)S(1)}, bf16[1024]{0:T(1024)(128)(2,1)}, u32[]{:S(2)}) copy-start(bf16[1024]{0:T(1024)(128)(2,1)} %get-tuple-element.15) | copy-start | bytes 6148
  256.2 21.2 %copy-start.15 = (bf16[1024]{0:T(1024)(128)(2,1)S(1)}, bf16[1024]{0:T(1024)(128)(2,1)}, u32[]{:S(2)}) copy-start(bf16[1024]{0:T(1024)(128)(2,1)} %get-tuple-element.17) | copy-start | bytes 6148
  256.2 21.2 %copy-start.16 = (bf16[1024]{0:T(1024)(128)(2,1)S(1)}, bf16[1024]{0:T(1024)(128)(2,1)}, u32[]{:S(2)}) copy-start(bf16[1024]{0:T(1024)(128)(2,1)} %get-tuple-element.19) | copy-start | bytes 6148
  256.2 21.6 %copy-start.19 = (s32[256]{0:T(256)S(1)}, s32[256]{0:T(256)}, u32[]{:S(2)}) copy-start(s32[256]{0:T(256)} %param.15) | copy-start | bytes 3076
  256.2 21.7 %copy-start.21 = (f32[48]{0:T(128)S(1)}, f32[48]{0:T(128)}, u32[]{:S(2)}) copy-start(f32[48]{0:T(128)} %copy-done.20) | copy-start | bytes 580
  257.5 40.7 %all-to-all-start.2 = ((bf16[8,256,384]{2,1,0:T(8,128)(2,1)}), bf16[8,256,384]{2,1,0:T(8,128)(2,1)}, u32[]{:S(2)}, u32[]{:S(2)}) async-start(bf16[8,256,384]{2,1,0:T(8,128)(2,1)} %bitcast.50), calls=%async_computation.2 | async-start | bytes 3145728 | tf_op jit(solution)/shard_map/all_to_all | solution.py:166
  301.6 9.5 %all-to-all-start.3 = ((f32[8,1,256]{2,1,0:T(1,128)}), f32[8,1,256]{2,1,0:T(1,128)S(1)}, u32[]{:S(2)}, u32[]{:S(2)}) async-start(f32[8,1,256]{2,1,0:T(1,128)} %broadcast_in_dim.189), calls=%async_computation.3 | async-start | bytes 16384 | tf_op jit(solution)/shard_map/all_to_all | solution.py:172
  (13 other events, 89.6 us)

commit v8 on v3

--- a/solution.py
+++ b/solution.py
@@ -156,20 +156,28 @@
     attn = back.transpose(1, 0, 2).reshape(tok_count, feat_count)
     partial_value = jnp.dot(attn, out_weight, preferred_element_type=jnp.float32)
     feature_width = hidden.shape[1]
-    tp_count = lax.axis_size("tp")
+    tp_hi_count = lax.axis_size("tp_hi")
+    tp_lo_count = lax.axis_size("tp_lo")
+    tp_count = tp_hi_count * tp_lo_count
     pieces = (
         partial_value.astype(jnp.bfloat16)
-        .reshape(tok_count, tp_count, feature_width)
-        .transpose(1, 0, 2)
-    )
-    gathered = lax.all_to_all(pieces, "tp", 0, 0, tiled=True)
-    own_sum = jnp.sum(gathered.astype(jnp.float32), axis=0)
+        .reshape(tok_count, tp_hi_count, tp_lo_count, feature_width)
+        .transpose(2, 1, 0, 3)
+    )
+    near = lax.all_to_all(pieces, "tp_lo", 0, 0, tiled=True)
+    near_sum = jnp.sum(near.astype(jnp.float32), axis=0).astype(jnp.bfloat16)
+    far = lax.all_to_all(near_sum, "tp_hi", 0, 0, tiled=True)
+    own_sum = jnp.sum(far.astype(jnp.float32), axis=0)
     hidden_out = (hidden.astype(jnp.float32) + own_sum).astype(jnp.bfloat16)
     stream_wide = hidden_out.astype(jnp.float32)
     square_part = jnp.sum(stream_wide * stream_wide, axis=1)
     square_total = jnp.sum(
         lax.all_to_all(
-            jnp.broadcast_to(square_part[None, :], (tp_count, tok_count)), "tp", 0, 0, tiled=True
+            jnp.broadcast_to(square_part[None, :], (tp_count, tok_count)),
+            ("tp_hi", "tp_lo"),
+            0,
+            0,
+            tiled=True,
         ),
         axis=0,
     )
@@ -188,19 +196,21 @@
 
 def solution(mesh):
     seq_count = mesh.shape["seq"]
-    head_count = D // mesh.shape["tp"] // HEAD_DIM
+    tp_count = mesh.shape["tp"]
+    head_count = D // tp_count // HEAD_DIM
     grouped = Mesh(
-        mesh.devices.reshape(seq_count // head_count, head_count, mesh.shape["tp"]),
-        ("seq_hi", "seq_lo", "tp"),
+        mesh.devices.reshape(seq_count // head_count, head_count, tp_count // 2, 2),
+        ("seq_hi", "seq_lo", "tp_hi", "tp_lo"),
     )
     rows = ("seq_hi", "seq_lo")
+    cols = ("tp_hi", "tp_lo")
     placed = (
-        P(rows, "tp"),
-        P(rows, "tp"),
-        P(rows, "tp"),
-        P(rows, "tp"),
-        P("tp", None),
-        P("tp"),
+        P(rows, cols),
+        P(rows, cols),
+        P(rows, cols),
+        P(rows, cols),
+        P(cols, None),
+        P(cols),
         P(rows),
         P(rows),
         P(rows),
@@ -209,6 +219,6 @@
         per_device,
         mesh=grouped,
         in_specs=placed,
-        out_specs=(P(rows, "tp"), P(rows, "tp"), P(rows, None, None, "tp")),
+        out_specs=(P(rows, cols), P(rows, cols), P(rows, None, None, cols)),
         check_vma=False,
     )

time: 294 us -> 319 us (1.085)
  local copies, waits for them, and re-layouts: 25.2 us -> 33.9 us
  waiting for transfers between devices: 93.8 us -> 101 us
  starting transfers between devices: 94.8 us -> 98.8 us
  other arithmetic: 18.9 us -> 22.7 us
    all_to_all x1 -> x2, waiting for transfers between devices: 20 us -> 28 us  [the longest x1 17.5 us: per_device(): near = lax.all_to_all(pieces, 'tp_lo', 0, 0, tiled=True)]
    reshape x1 -> x2, local copies, waits for them, and re-layouts: 1.32 us -> 8.25 us  [per_device(): pieces = partial_value.astype(jnp.bfloat16).reshape(tok_count, tp_hi_coun...]
    all_to_all x1 -> x2, starting transfers between devices: 4.42 us -> 8.46 us  [the longest x1 4.96 us: per_device(): near = lax.all_to_all(pieces, 'tp_lo', 0, 0, tiled=True)]
  transfers between devices with their start and end apart: 11 -> 12, of which waited for: 9 -> 10; matrix products, arithmetic and copies ran while one was open for 21% -> 20% of each run, Pallas kernels for 0% -> 0%
where the time goes in v8:
time: 319 us; the launch traced here: 317 us
  waiting for transfers between devices  101 us (32%)
  starting transfers between devices  98.8 us (31%)
  matrix products  52 us (16%)
  local copies, waits for them, and re-layouts  33.9 us (11%)
  other arithmetic  22.7 us (7%)
  blocking collectives  7.67 us (2%)
    ppermute x8, starting transfers between devices, passed_along(): return lax.ppermute(block, axis, route)  83.6 us
    ppermute x8, waiting for transfers between devices, passed_along(): return lax.ppermute(block, axis, route)  59.9 us
    dot_general x9, matrix products, attend(): jnp.einsum('qk,kd->qd', unnormed.astype(jnp.bfloat16), val_heads, preferr...  34.5 us
    all_to_all x1, waiting for transfers between devices, per_device(): near = lax.all_to_all(pieces, 'tp_lo', 0, 0, tiled=True)  17.5 us
    dot_general x9, matrix products, attend(): jnp.einsum('qd,kd->qk', query_heads, key_heads, preferred_element_type=jn...  15.3 us
    while x28, local copies, waits for them, and re-layouts  13.6 us
    reduce_sum x9, other arithmetic, attend(): row_total = row_total * rescale + jnp.sum(unnormed, axis=-1)  12 us
    all_to_all x1, waiting for transfers between devices, per_device(): far = lax.all_to_all(near_sum, 'tp_hi', 0, 0, tiled=True)  10.5 us
  transfers between devices with their start and end apart: 12, of which 10 were waited for; matrix products, arithmetic and copies ran while one was open for 20% of the time, Pallas kernels for 0%

profile of v8, /device:TPU:176, one launch (start us, length us, event | category | flops | bytes accessed | tf_op | source)
XLA Modules:
  0.0 317.5 jit_solution(3044769590388668041)
XLA Ops:
  8.8 9.6 %all-to-all-done = bf16[4,256,290]{1,2,0:T(8,128)(2,1)S(1)} async-done(((bf16[4,256,290]{1,2,0:T(8,128)(2,1)}), bf16[4,256,290]{1,2,0:T(8,128)(2,1)S(1)}, u32[]{:S(2)}, u32[]{:S(2)}) %all-to-all-start) | async-done | bytes 593952 | tf_op jit(solution)/shard_map/all_to_all | solution.py:103
  24.3 6.8 %collective-permute-start.1 = (bf16[1024,194]{0,1:T(8,128)(2,1)}, bf16[1024,194]{0,1:T(8,128)(2,1)S(1)}, u32[]{:S(2)}, u32[]{:S(2)}) collective-permute-start(bf16[1024,194]{0,1:T(8,128)(2,1)} %slice.107), channel_id=1, source_target_pairs={{0,32},{32,64},{64,96},{96,128},{128,160},{160,192},{192,224},{224... | collective-permute-start | bytes 1191944 | tf_op jit(solution)/shard_map/ppermute | solution.py:21
  37.1 11.0 %collective-permute-done.1 = bf16[1024,194]{0,1:T(8,128)(2,1)S(1)} collective-permute-done((bf16[1024,194]{0,1:T(8,128)(2,1)}, bf16[1024,194]{0,1:T(8,128)(2,1)S(1)}, u32[]{:S(2)}, u32[]{:S(2)}) %collective-permute-start.1) | collective-permute-done | bytes 397344 | tf_op jit(solution)/shard_map/ppermute | solution.py:21
  48.1 191.8 %while.24 = (s32[]{:T(128)}, f32[1024]{0:T(1024)S(1)}, f32[1024]{0:T(1024)S(1)}, f32[1024,96]{0,1:T(8,128)}, s32[32]{0:T(128)S(1)}, /*index=5*/bf16[1024,194]{0,...) while((s32[]{:T(128)}, f32[1024]{0:T(1024)S(1)}, ...), condition=%wide.region_7.8_spmd.clone, body=%wide.region_3.7_spmd.clone.sunk | while | flops 419728448 | bytes 33221464 | solution.py:144
  48.1 11.6 %collective-permute-start = (bf16[1024,194]{0,1:T(8,128)(2,1)S(1)}, bf16[1024,194]{0,1:T(8,128)(2,1)S(1)}, u32[]{:S(2)}, u32[]{:S(2)}) collective-permute-start(bf16[1024,194]{0,1:T(8,128)(2,1)S(1)} %copy.107), channel_id=1, source_target_pairs={{0,32},{32,64},{64,96},{96,128},{128,160},{160,192},{192,224},{224... | collective-permute-start | bytes 1191944 | tf_op jit(solution)/shard_map/while/body/eval_jaxpr/ppermute | solution.py:21
  69.1 7.8 %collective-permute-done = bf16[1024,194]{0,1:T(8,128)(2,1)S(1)} collective-permute-done((bf16[1024,194]{0,1:T(8,128)(2,1)S(1)}, bf16[1024,194]{0,1:T(8,128)(2,1)S(1)}, u32[]{:S(2)}, u32[]{:S(2)}) %collective-permute-start) | collective-permute-done | bytes 397344 | tf_op jit(solution)/shard_map/while/body/eval_jaxpr/ppermute | solution.py:21
  77.0 10.2 %collective-permute-start = (bf16[1024,194]{0,1:T(8,128)(2,1)S(1)}, bf16[1024,194]{0,1:T(8,128)(2,1)S(1)}, u32[]{:S(2)}, u32[]{:S(2)}) collective-permute-start(bf16[1024,194]{0,1:T(8,128)(2,1)S(1)} %copy.107), channel_id=1, source_target_pairs={{0,32},{32,64},{64,96},{96,128},{128,160},{160,192},{192,224},{224... | collective-permute-start | bytes 1191944 | tf_op jit(solution)/shard_map/while/body/eval_jaxpr/ppermute | solution.py:21
  96.6 9.9 %collective-permute-done = bf16[1024,194]{0,1:T(8,128)(2,1)S(1)} collective-permute-done((bf16[1024,194]{0,1:T(8,128)(2,1)S(1)}, bf16[1024,194]{0,1:T(8,128)(2,1)S(1)}, u32[]{:S(2)}, u32[]{:S(2)}) %collective-permute-start) | collective-permute-done | bytes 397344 | tf_op jit(solution)/shard_map/while/body/eval_jaxpr/ppermute | solution.py:21
  106.6 9.5 %collective-permute-start = (bf16[1024,194]{0,1:T(8,128)(2,1)S(1)}, bf16[1024,194]{0,1:T(8,128)(2,1)S(1)}, u32[]{:S(2)}, u32[]{:S(2)}) collective-permute-start(bf16[1024,194]{0,1:T(8,128)(2,1)S(1)} %copy.107), channel_id=1, source_target_pairs={{0,32},{32,64},{64,96},{96,128},{128,160},{160,192},{192,224},{224... | collective-permute-start | bytes 1191944 | tf_op jit(solution)/shard_map/while/body/eval_jaxpr/ppermute | solution.py:21
  125.5 9.4 %collective-permute-done = bf16[1024,194]{0,1:T(8,128)(2,1)S(1)} collective-permute-done((bf16[1024,194]{0,1:T(8,128)(2,1)S(1)}, bf16[1024,194]{0,1:T(8,128)(2,1)S(1)}, u32[]{:S(2)}, u32[]{:S(2)}) %collective-permute-start) | collective-permute-done | bytes 397344 | tf_op jit(solution)/shard_map/while/body/eval_jaxpr/ppermute | solution.py:21
  135.0 12.4 %collective-permute-start = (bf16[1024,194]{0,1:T(8,128)(2,1)S(1)}, bf16[1024,194]{0,1:T(8,128)(2,1)S(1)}, u32[]{:S(2)}, u32[]{:S(2)}) collective-permute-start(bf16[1024,194]{0,1:T(8,128)(2,1)S(1)} %copy.107), channel_id=1, source_target_pairs={{0,32},{32,64},{64,96},{96,128},{128,160},{160,192},{192,224},{224... | collective-permute-start | bytes 1191944 | tf_op jit(solution)/shard_map/while/body/eval_jaxpr/ppermute | solution.py:21
  152.5 4.2 %fusion.81 = f32[1024,96]{0,1:T(8,128)} fusion(f32[1024,1024]{0,1:T(8,128)} %copy-done.1, f32[1024]{0:T(1024)S(1)} %max.15, bf16[1024]{0:T(1024)(128)(2,1)S(1)} %reduce.18, bf16[1024]{0:T(1024)(128)(2,1)S(1)} %get-tuple-element.459, f32[1024,96]{0,1:T(8,128)} %get-tuple-element.480, bf16[1024,194]{0,1:T(8,128)(2,1)S(1)} %copy.107, ...), kind=kOutput, calls=%fused_computation.9.clone.1 | convolution fusion | flops 207814656 | bytes 5189632 | tf_op jit(solution)/shard_map/while/body/eval_jaxpr/qk,kd->qd/dot_general | solution.py:58
  156.7 13.7 %collective-permute-done = bf16[1024,194]{0,1:T(8,128)(2,1)S(1)} collective-permute-done((bf16[1024,194]{0,1:T(8,128)(2,1)S(1)}, bf16[1024,194]{0,1:T(8,128)(2,1)S(1)}, u32[]{:S(2)}, u32[]{:S(2)}) %collective-permute-start) | collective-permute-done | bytes 397344 | tf_op jit(solution)/shard_map/while/body/eval_jaxpr/ppermute | solution.py:21
  170.5 9.7 %collective-permute-start = (bf16[1024,194]{0,1:T(8,128)(2,1)S(1)}, bf16[1024,194]{0,1:T(8,128)(2,1)S(1)}, u32[]{:S(2)}, u32[]{:S(2)}) collective-permute-start(bf16[1024,194]{0,1:T(8,128)(2,1)S(1)} %copy.107), channel_id=1, source_target_pairs={{0,32},{32,64},{64,96},{96,128},{128,160},{160,192},{192,224},{224... | collective-permute-start | bytes 1191944 | tf_op jit(solution)/shard_map/while/body/eval_jaxpr/ppermute | solution.py:21
  189.6 8.0 %collective-permute-done = bf16[1024,194]{0,1:T(8,128)(2,1)S(1)} collective-permute-done((bf16[1024,194]{0,1:T(8,128)(2,1)S(1)}, bf16[1024,194]{0,1:T(8,128)(2,1)S(1)}, u32[]{:S(2)}, u32[]{:S(2)}) %collective-permute-start) | collective-permute-done | bytes 397344 | tf_op jit(solution)/shard_map/while/body/eval_jaxpr/ppermute | solution.py:21
  197.7 11.1 %collective-permute-start = (bf16[1024,194]{0,1:T(8,128)(2,1)S(1)}, bf16[1024,194]{0,1:T(8,128)(2,1)S(1)}, u32[]{:S(2)}, u32[]{:S(2)}) collective-permute-start(bf16[1024,194]{0,1:T(8,128)(2,1)S(1)} %copy.107), channel_id=1, source_target_pairs={{0,32},{32,64},{64,96},{96,128},{128,160},{160,192},{192,224},{224... | collective-permute-start | bytes 1191944 | tf_op jit(solution)/shard_map/while/body/eval_jaxpr/ppermute | solution.py:21
  214.1 4.2 %fusion.81 = f32[1024,96]{0,1:T(8,128)} fusion(f32[1024,1024]{0,1:T(8,128)} %copy-done.1, f32[1024]{0:T(1024)S(1)} %max.15, bf16[1024]{0:T(1024)(128)(2,1)S(1)} %reduce.18, bf16[1024]{0:T(1024)(128)(2,1)S(1)} %get-tuple-element.459, f32[1024,96]{0,1:T(8,128)} %get-tuple-element.480, bf16[1024,194]{0,1:T(8,128)(2,1)S(1)} %copy.107, ...), kind=kOutput, calls=%fused_computation.9.clone.1 | convolution fusion | flops 207814656 | bytes 5189632 | tf_op jit(solution)/shard_map/while/body/eval_jaxpr/qk,kd->qd/dot_general | solution.py:58
  218.3 12.2 %collective-permute-start = (bf16[1024,194]{0,1:T(8,128)(2,1)S(1)}, bf16[1024,194]{0,1:T(8,128)(2,1)S(1)}, u32[]{:S(2)}, u32[]{:S(2)}) collective-permute-start(bf16[1024,194]{0,1:T(8,128)(2,1)S(1)} %copy.107), channel_id=1, source_target_pairs={{0,32},{32,64},{64,96},{96,128},{128,160},{160,192},{192,224},{224... | collective-permute-start | bytes 1191944 | tf_op jit(solution)/shard_map/while/body/eval_jaxpr/ppermute | solution.py:21
  235.7 4.2 %fusion.81 = f32[1024,96]{0,1:T(8,128)} fusion(f32[1024,1024]{0,1:T(8,128)} %copy-done.1, f32[1024]{0:T(1024)S(1)} %max.15, bf16[1024]{0:T(1024)(128)(2,1)S(1)} %reduce.18, bf16[1024]{0:T(1024)(128)(2,1)S(1)} %get-tuple-element.459, f32[1024,96]{0,1:T(8,128)} %get-tuple-element.480, bf16[1024,194]{0,1:T(8,128)(2,1)S(1)} %copy.107, ...), kind=kOutput, calls=%fused_computation.9.clone.1 | convolution fusion | flops 207814656 | bytes 5189632 | tf_op jit(solution)/shard_map/while/body/eval_jaxpr/qk,kd->qd/dot_general | solution.py:58
  244.2 7.7 %all_to_all.26 = bf16[4,256,96]{1,2,0:T(8,128)(2,1)S(1)} all-to-all(bf16[4,256,96]{1,2,0:T(8,128)(2,1)S(1)} %bitcast.54), channel_id=1, replica_groups=mesh['seq_hi'=16,'seq_lo'=4,'tp_hi'=4,'tp_lo'=2] {'seq_lo'}, dimensions={0} | all-to-all | bytes 393216 | tf_op jit(solution)/shard_map/all_to_all | solution.py:153
  254.0 5.1 %reshape.267 = bf16[256,4,2,384]{3,2,1,0:T(2,128)(2,1)} reshape(bf16[256,3072]{1,0:T(8,128)(2,1)} %convolution_convert_fusion) | data formatting | bytes 3145728 | tf_op jit(solution)/shard_map/reshape | solution.py:164
  262.3 5.0 %all-to-all-start.2 = ((bf16[2,4,256,384]{3,1,2,0:T(4,128)(2,1)}), bf16[2,4,256,384]{3,1,2,0:T(4,128)(2,1)}, u32[]{:S(2)}, u32[]{:S(2)}) async-start(bf16[2,4,256,384]{3,1,2,0:T(4,128)(2,1)} %bitcast.41), calls=%async_computation.2 | async-start | bytes 3145728 | tf_op jit(solution)/shard_map/all_to_all | solution.py:167
  269.1 17.5 %all-to-all-done.2 = bf16[2,4,256,384]{3,1,2,0:T(4,128)(2,1)} async-done(((bf16[2,4,256,384]{3,1,2,0:T(4,128)(2,1)}), bf16[2,4,256,384]{3,1,2,0:T(4,128)(2,1)}, u32[]{:S(2)}, u32[]{:S(2)}) %all-to-all-start.2) | async-done | bytes 1572896 | tf_op jit(solution)/shard_map/all_to_all | solution.py:167
  294.8 10.5 %all-to-all-done.3 = bf16[4,256,384]{2,1,0:T(8,128)(2,1)S(1)} async-done(((bf16[4,256,384]{2,1,0:T(8,128)(2,1)}), bf16[4,256,384]{2,1,0:T(8,128)(2,1)S(1)}, u32[]{:S(2)}, u32[]{:S(2)}) %all-to-all-start.3) | async-done | bytes 786464 | tf_op jit(solution)/shard_map/all_to_all | solution.py:169
  (207 shorter events, 104.5 us)
Async XLA Ops:
  0.6 251.2 %copy-start = (bf16[384,3072]{1,0:T(8,128)(2,1)S(1)}, bf16[384,3072]{1,0:T(8,128)(2,1)}, u32[]{:S(2)}) copy-start(bf16[384,3072]{1,0:T(8,128)(2,1)} %param.15) | copy-start | bytes 7077892
  0.6 3.6 %copy-start.8 = (bf16[256,384]{1,0:T(8,128)(2,1)S(1)}, bf16[256,384]{1,0:T(8,128)(2,1)}, u32[]{:S(2)}) copy-start(bf16[256,384]{1,0:T(8,128)(2,1)} %param.13) | copy-start | bytes 589828
  0.7 3.7 %copy-start.11 = (s32[256]{0:T(256)S(1)}, s32[256]{0:T(256)}, u32[]{:S(2)}) copy-start(s32[256]{0:T(256)} %param.17) | copy-start | bytes 3076
  0.7 3.7 %copy-start.12 = (s32[256]{0:T(256)S(1)}, s32[256]{0:T(256)}, u32[]{:S(2)}) copy-start(s32[256]{0:T(256)} %param.18) | copy-start | bytes 3076
  5.3 13.1 %all-to-all-start = ((bf16[4,256,290]{1,2,0:T(8,128)(2,1)}), bf16[4,256,290]{1,2,0:T(8,128)(2,1)S(1)}, u32[]{:S(2)}, u32[]{:S(2)}) async-start(bf16[4,256,290]{1,2,0:T(8,128)(2,1)} %bitcast.50), calls=%async_computation | async-start | bytes 1212416 | tf_op jit(solution)/shard_map/all_to_all | solution.py:103
  19.0 14.0 %copy-start.5 = (bf16[37,8,4,256]{3,1,2,0:T(8,128)(2,1)}, bf16[37,8,4,256]{3,1,2,0:T(8,128)(2,1)S(1)}, u32[]{:S(2)}) copy-start(bf16[37,8,4,256]{3,1,2,0:T(8,128)(2,1)S(1)} %copy.84) | copy-start | bytes 1818628
  24.3 23.8 %collective-permute-start.1 = (bf16[1024,194]{0,1:T(8,128)(2,1)}, bf16[1024,194]{0,1:T(8,128)(2,1)S(1)}, u32[]{:S(2)}, u32[]{:S(2)}) collective-permute-start(bf16[1024,194]{0,1:T(8,128)(2,1)} %slice.107), channel_id=1, source_target_pairs={{0,32},{32,64},{64,96},{96,128},{128,160},{160,192},{192,224},{224... | collective-permute-start | bytes 1191944 | tf_op jit(solution)/shard_map/ppermute | solution.py:21
  48.1 28.8 %collective-permute-start = (bf16[1024,194]{0,1:T(8,128)(2,1)S(1)}, bf16[1024,194]{0,1:T(8,128)(2,1)S(1)}, u32[]{:S(2)}, u32[]{:S(2)}) collective-permute-start(bf16[1024,194]{0,1:T(8,128)(2,1)S(1)} %copy.107), channel_id=1, source_target_pairs={{0,32},{32,64},{64,96},{96,128},{128,160},{160,192},{192,224},{224... | collective-permute-start | bytes 1191944 | tf_op jit(solution)/shard_map/while/body/eval_jaxpr/ppermute | solution.py:21
  77.0 29.6 %collective-permute-start = (bf16[1024,194]{0,1:T(8,128)(2,1)S(1)}, bf16[1024,194]{0,1:T(8,128)(2,1)S(1)}, u32[]{:S(2)}, u32[]{:S(2)}) collective-permute-start(bf16[1024,194]{0,1:T(8,128)(2,1)S(1)} %copy.107), channel_id=1, source_target_pairs={{0,32},{32,64},{64,96},{96,128},{128,160},{160,192},{192,224},{224... | collective-permute-start | bytes 1191944 | tf_op jit(solution)/shard_map/while/body/eval_jaxpr/ppermute | solution.py:21
  106.6 28.4 %collective-permute-start = (bf16[1024,194]{0,1:T(8,128)(2,1)S(1)}, bf16[1024,194]{0,1:T(8,128)(2,1)S(1)}, u32[]{:S(2)}, u32[]{:S(2)}) collective-permute-start(bf16[1024,194]{0,1:T(8,128)(2,1)S(1)} %copy.107), channel_id=1, source_target_pairs={{0,32},{32,64},{64,96},{96,128},{128,160},{160,192},{192,224},{224... | collective-permute-start | bytes 1191944 | tf_op jit(solution)/shard_map/while/body/eval_jaxpr/ppermute | solution.py:21
  135.0 35.5 %collective-permute-start = (bf16[1024,194]{0,1:T(8,128)(2,1)S(1)}, bf16[1024,194]{0,1:T(8,128)(2,1)S(1)}, u32[]{:S(2)}, u32[]{:S(2)}) collective-permute-start(bf16[1024,194]{0,1:T(8,128)(2,1)S(1)} %copy.107), channel_id=1, source_target_pairs={{0,32},{32,64},{64,96},{96,128},{128,160},{160,192},{192,224},{224... | collective-permute-start | bytes 1191944 | tf_op jit(solution)/shard_map/while/body/eval_jaxpr/ppermute | solution.py:21
  170.5 27.2 %collective-permute-start = (bf16[1024,194]{0,1:T(8,128)(2,1)S(1)}, bf16[1024,194]{0,1:T(8,128)(2,1)S(1)}, u32[]{:S(2)}, u32[]{:S(2)}) collective-permute-start(bf16[1024,194]{0,1:T(8,128)(2,1)S(1)} %copy.107), channel_id=1, source_target_pairs={{0,32},{32,64},{64,96},{96,128},{128,160},{160,192},{192,224},{224... | collective-permute-start | bytes 1191944 | tf_op jit(solution)/shard_map/while/body/eval_jaxpr/ppermute | solution.py:21
  197.7 20.5 %collective-permute-start = (bf16[1024,194]{0,1:T(8,128)(2,1)S(1)}, bf16[1024,194]{0,1:T(8,128)(2,1)S(1)}, u32[]{:S(2)}, u32[]{:S(2)}) collective-permute-start(bf16[1024,194]{0,1:T(8,128)(2,1)S(1)} %copy.107), channel_id=1, source_target_pairs={{0,32},{32,64},{64,96},{96,128},{128,160},{160,192},{192,224},{224... | collective-permute-start | bytes 1191944 | tf_op jit(solution)/shard_map/while/body/eval_jaxpr/ppermute | solution.py:21
  218.3 21.6 %collective-permute-start = (bf16[1024,194]{0,1:T(8,128)(2,1)S(1)}, bf16[1024,194]{0,1:T(8,128)(2,1)S(1)}, u32[]{:S(2)}, u32[]{:S(2)}) collective-permute-start(bf16[1024,194]{0,1:T(8,128)(2,1)S(1)} %copy.107), channel_id=1, source_target_pairs={{0,32},{32,64},{64,96},{96,128},{128,160},{160,192},{192,224},{224... | collective-permute-start | bytes 1191944 | tf_op jit(solution)/shard_map/while/body/eval_jaxpr/ppermute | solution.py:21
  239.9 3.0 copy-start.15
  254.0 13.2 %copy-start.9 = (bf16[256,384]{1,0:T(8,128)(2,1)S(1)}, bf16[256,384]{1,0:T(8,128)(2,1)}, u32[]{:S(2)}) copy-start(bf16[256,384]{1,0:T(8,128)(2,1)} %param.13) | copy-start | bytes 589828
  259.1 9.2 %copy-start.13 = (bf16[384]{0:T(512)(128)(2,1)S(1)}, bf16[384]{0:T(512)(128)(2,1)}, u32[]{:S(2)}) copy-start(bf16[384]{0:T(512)(128)(2,1)} %param.16) | copy-start | bytes 2308
  259.1 9.2 %copy-start.14 = (s32[2]{0:T(128)S(1)}, s32[2]{0:T(128)}, u32[]{:S(2)}) copy-start(s32[2]{0:T(128)} %param.19) | copy-start | bytes 28
  262.3 31.7 %copy-start.3 = (f32[256,4,96]{0,2,1:T(8,128)S(1)}, f32[256,4,96]{0,2,1:T(8,128)}, u32[]{:S(2)}) copy-start(f32[256,4,96]{0,2,1:T(8,128)} %copy-done.2) | copy-start | bytes 1179652
  262.3 24.3 %all-to-all-start.2 = ((bf16[2,4,256,384]{3,1,2,0:T(4,128)(2,1)}), bf16[2,4,256,384]{3,1,2,0:T(4,128)(2,1)}, u32[]{:S(2)}, u32[]{:S(2)}) async-start(bf16[2,4,256,384]{3,1,2,0:T(4,128)(2,1)} %bitcast.41), calls=%async_computation.2 | async-start | bytes 3145728 | tf_op jit(solution)/shard_map/all_to_all | solution.py:167
  290.2 15.1 %all-to-all-start.3 = ((bf16[4,256,384]{2,1,0:T(8,128)(2,1)}), bf16[4,256,384]{2,1,0:T(8,128)(2,1)S(1)}, u32[]{:S(2)}, u32[]{:S(2)}) async-start(bf16[4,256,384]{2,1,0:T(8,128)(2,1)} %copy.76), calls=%async_computation.3 | async-start | bytes 1572864 | tf_op jit(solution)/shard_map/all_to_all | solution.py:169
  306.5 11.0 %copy-start.10 = (bf16[256,384]{1,0:T(8,128)(2,1)}, bf16[256,384]{1,0:T(8,128)(2,1)S(1)}, u32[]{:S(2)}) copy-start(bf16[256,384]{1,0:T(8,128)(2,1)S(1)} %get-tuple-element.377) | copy-start | bytes 589828
  307.2 9.5 %all-to-all-start.4 = ((f32[8,1,256]{2,1,0:T(1,128)}), f32[8,1,256]{2,1,0:T(1,128)S(1)}, u32[]{:S(2)}, u32[]{:S(2)}) async-start(f32[8,1,256]{2,1,0:T(1,128)} %broadcast_in_dim.164), calls=%async_computation.4 | async-start | bytes 16384 | tf_op jit(solution)/shard_map/all_to_all | solution.py:175
  313.4 4.0 %copy-start.6 = (bf16[2,2,128,384]{3,2,1,0:T(8,128)(2,1)}, bf16[2,2,128,384]{3,2,1,0:T(8,128)(2,1)S(1)}, u32[]{:S(2)}) copy-start(bf16[2,2,128,384]{3,2,1,0:T(8,128)(2,1)S(1)} %scatter_fusion) | copy-start | bytes 1179652
  (10 other events, 17.7 us)

commit v9 on v3

--- a/solution.py
+++ b/solution.py
@@ -144,7 +144,25 @@
     (softmax_state, seen_first), moved = lax.fori_loop(
         0, reach_count - 1, cycle_turn, ((softmax_state, seen_first), moved)
     )
-    softmax_state, first_tok = visit_block((softmax_state, seen_first), moved, reach_count)
+    last_tags = moved[:, 2 * HEAD_DIM]
+    row_parts = []
+    part_rows = chunk_count // lo_count
+    for part in range(lo_count):
+        rows = slice(part * part_rows, (part + 1) * part_rows)
+        keys = slice(part * part_rows, chunk_count)
+        visible = last_tags[keys][None, :] == chunk_qtag[rows][:, None]
+        row_parts.append(
+            attend(
+                tuple(s[rows] for s in softmax_state),
+                chunk_q[rows],
+                moved[keys, :HEAD_DIM],
+                moved[keys, HEAD_DIM : 2 * HEAD_DIM],
+                visible,
+            )
+        )
+    softmax_state = tuple(jnp.concatenate(parts, axis=0) for parts in zip(*row_parts))
+    last_index = (chunk_row - reach_count) * chunk_count + chunk_offsets
+    first_tok = jnp.minimum(seen_first, first_of(moved[:, 2 * HEAD_DIM + 1], last_index))
     member = segment_ids[:, None] == jnp.arange(seg_count, dtype=jnp.int32)[None, :]
     position = tok_index - jnp.sum(jnp.where(member, first_tok[None, :], 0), axis=1)
     k_rot = rotate(key_proj, position, head_count, HEAD_DIM)

time: 294 us -> 317 us (1.078)
  matrix products: 50.8 us -> 57.9 us
  waiting for transfers between devices: 93.8 us -> 100 us
  starting transfers between devices: 94.8 us -> 100 us
    ppermute x8, waiting for transfers between devices: 59.9 us -> 65.8 us  [passed_along(): return lax.ppermute(block, axis, route)]
    dot_general x9 -> x12, matrix products: 34.5 us -> 38.8 us  [attend(): jnp.einsum('qk,kd->qd', unnormed.astype(jnp.bfloat16), val_heads, preferr...]
    all_to_all x1, starting transfers between devices: 4.42 us -> 7.7 us  [per_device(): gathered = lax.all_to_all(pieces, 'tp', 0, 0, tiled=True)]
    dot_general x9 -> x12, matrix products: 15.3 us -> 18.1 us  [attend(): jnp.einsum('qd,kd->qk', query_heads, key_heads, preferred_element_type=jn...]
    unnamed x50 -> x98, local copies, waits for them, and re-layouts: 6.14 us -> 6.42 us
    reduce_sum x9 -> x12, other arithmetic: 12 us -> 11.8 us  [attend(): row_total = row_total * rescale + jnp.sum(unnormed, axis=-1)]
  transfers between devices with their start and end apart: 11 -> 11, of which waited for: 9 -> 10; matrix products, arithmetic and copies ran while one was open for 21% -> 19% of each run, Pallas kernels for 0% -> 0%
where the time goes in v9:
time: 317 us; the launch traced here: 315 us
  starting transfers between devices  100 us (32%)
  waiting for transfers between devices  100 us (32%)
  matrix products  57.9 us (18%)
  local copies, waits for them, and re-layouts  27.4 us (9%)
  other arithmetic  20.2 us (6%)
  blocking collectives  7.67 us (2%)
    ppermute x8, starting transfers between devices, passed_along(): return lax.ppermute(block, axis, route)  85.6 us
    ppermute x8, waiting for transfers between devices, passed_along(): return lax.ppermute(block, axis, route)  65.8 us
    dot_general x12, matrix products, attend(): jnp.einsum('qk,kd->qd', unnormed.astype(jnp.bfloat16), val_heads, preferr...  38.8 us
    all_to_all x1, waiting for transfers between devices, per_device(): gathered = lax.all_to_all(pieces, 'tp', 0, 0, tiled=True)  20.2 us
    dot_general x12, matrix products, attend(): jnp.einsum('qd,kd->qk', query_heads, key_heads, preferred_element_type=jn...  18.1 us
    while x28, local copies, waits for them, and re-layouts  13.6 us
    reduce_sum x12, other arithmetic, attend(): row_total = row_total * rescale + jnp.sum(unnormed, axis=-1)  11.8 us
    all_to_all x1, waiting for transfers between devices, per_device(): chunk = lax.all_to_all(payload, 'seq_lo', 0, 0, tiled=True)  9.62 us
  transfers between devices with their start and end apart: 11, of which 10 were waited for; matrix products, arithmetic and copies ran while one was open for 19% of the time, Pallas kernels for 0%

profile of v9, /device:TPU:176, one launch (start us, length us, event | category | flops | bytes accessed | tf_op | source)
XLA Modules:
  0.0 315.4 jit_solution(13442348743513595283)
XLA Ops:
  9.4 9.6 %all-to-all-done = bf16[4,256,290]{1,2,0:T(8,128)(2,1)S(1)} async-done(((bf16[4,256,290]{1,2,0:T(8,128)(2,1)}), bf16[4,256,290]{1,2,0:T(8,128)(2,1)S(1)}, u32[]{:S(2)}, u32[]{:S(2)}) %all-to-all-start) | async-done | bytes 593952 | tf_op jit(solution)/shard_map/all_to_all | solution.py:103
  24.9 6.6 %collective-permute-start.1 = (bf16[1024,194]{0,1:T(8,128)(2,1)}, bf16[1024,194]{0,1:T(8,128)(2,1)S(1)}, u32[]{:S(2)}, u32[]{:S(2)}) collective-permute-start(bf16[1024,194]{0,1:T(8,128)(2,1)} %slice.241), channel_id=1, source_target_pairs={{0,32},{32,64},{64,96},{96,128},{128,160},{160,192},{192,224},{224... | collective-permute-start | bytes 1191944 | tf_op jit(solution)/shard_map/ppermute | solution.py:21
  37.6 11.1 %collective-permute-done.1 = bf16[1024,194]{0,1:T(8,128)(2,1)S(1)} collective-permute-done((bf16[1024,194]{0,1:T(8,128)(2,1)}, bf16[1024,194]{0,1:T(8,128)(2,1)S(1)}, u32[]{:S(2)}, u32[]{:S(2)}) %collective-permute-start.1) | collective-permute-done | bytes 397344 | tf_op jit(solution)/shard_map/ppermute | solution.py:21
  48.7 199.8 %while.24 = (s32[]{:T(128)}, f32[1024]{0:T(1024)S(1)}, f32[1024]{0:T(1024)S(1)}, f32[1024,96]{0,1:T(8,128)}, s32[32]{0:T(128)S(1)}, /*index=5*/bf16[1024,194]{0,...) while((s32[]{:T(128)}, f32[1024]{0:T(1024)S(1)}, ...), condition=%wide.region_7.8_spmd.clone, body=%wide.region_3.7_spmd.clone.sunk | while | flops 419728448 | bytes 33221464 | solution.py:144
  48.7 11.6 %collective-permute-start = (bf16[1024,194]{0,1:T(8,128)(2,1)S(1)}, bf16[1024,194]{0,1:T(8,128)(2,1)S(1)}, u32[]{:S(2)}, u32[]{:S(2)}) collective-permute-start(bf16[1024,194]{0,1:T(8,128)(2,1)S(1)} %copy.90), channel_id=1, source_target_pairs={{0,32},{32,64},{64,96},{96,128},{128,160},{160,192},{192,224},{224... | collective-permute-start | bytes 1191944 | tf_op jit(solution)/shard_map/while/body/eval_jaxpr/ppermute | solution.py:21
  69.7 5.5 %collective-permute-done = bf16[1024,194]{0,1:T(8,128)(2,1)S(1)} collective-permute-done((bf16[1024,194]{0,1:T(8,128)(2,1)S(1)}, bf16[1024,194]{0,1:T(8,128)(2,1)S(1)}, u32[]{:S(2)}, u32[]{:S(2)}) %collective-permute-start) | collective-permute-done | bytes 397344 | tf_op jit(solution)/shard_map/while/body/eval_jaxpr/ppermute | solution.py:21
  75.3 12.5 %collective-permute-start = (bf16[1024,194]{0,1:T(8,128)(2,1)S(1)}, bf16[1024,194]{0,1:T(8,128)(2,1)S(1)}, u32[]{:S(2)}, u32[]{:S(2)}) collective-permute-start(bf16[1024,194]{0,1:T(8,128)(2,1)S(1)} %copy.90), channel_id=1, source_target_pairs={{0,32},{32,64},{64,96},{96,128},{128,160},{160,192},{192,224},{224... | collective-permute-start | bytes 1191944 | tf_op jit(solution)/shard_map/while/body/eval_jaxpr/ppermute | solution.py:21
  93.0 4.2 %fusion.130 = f32[1024,96]{0,1:T(8,128)} fusion(f32[1024,1024]{0,1:T(8,128)} %copy-done.1, f32[1024]{0:T(1024)S(1)} %max.31, bf16[1024]{0:T(1024)(128)(2,1)S(1)} %reduce.31, bf16[1024]{0:T(1024)(128)(2,1)S(1)} %get-tuple-element.476, f32[1024,96]{0,1:T(8,128)} %get-tuple-element.497, bf16[1024,194]{0,1:T(8,128)(2,1)S(1)} %copy.90, ...), kind=kOutput, calls=%fused_computation.9.clone.1 | convolution fusion | flops 207814656 | bytes 5189632 | tf_op jit(solution)/shard_map/while/body/eval_jaxpr/qk,kd->qd/dot_general | solution.py:58
  97.1 11.5 %collective-permute-done = bf16[1024,194]{0,1:T(8,128)(2,1)S(1)} collective-permute-done((bf16[1024,194]{0,1:T(8,128)(2,1)S(1)}, bf16[1024,194]{0,1:T(8,128)(2,1)S(1)}, u32[]{:S(2)}, u32[]{:S(2)}) %collective-permute-start) | collective-permute-done | bytes 397344 | tf_op jit(solution)/shard_map/while/body/eval_jaxpr/ppermute | solution.py:21
  108.7 9.6 %collective-permute-start = (bf16[1024,194]{0,1:T(8,128)(2,1)S(1)}, bf16[1024,194]{0,1:T(8,128)(2,1)S(1)}, u32[]{:S(2)}, u32[]{:S(2)}) collective-permute-start(bf16[1024,194]{0,1:T(8,128)(2,1)S(1)} %copy.90), channel_id=1, source_target_pairs={{0,32},{32,64},{64,96},{96,128},{128,160},{160,192},{192,224},{224... | collective-permute-start | bytes 1191944 | tf_op jit(solution)/shard_map/while/body/eval_jaxpr/ppermute | solution.py:21
  123.5 4.2 %fusion.130 = f32[1024,96]{0,1:T(8,128)} fusion(f32[1024,1024]{0,1:T(8,128)} %copy-done.1, f32[1024]{0:T(1024)S(1)} %max.31, bf16[1024]{0:T(1024)(128)(2,1)S(1)} %reduce.31, bf16[1024]{0:T(1024)(128)(2,1)S(1)} %get-tuple-element.476, f32[1024,96]{0,1:T(8,128)} %get-tuple-element.497, bf16[1024,194]{0,1:T(8,128)(2,1)S(1)} %copy.90, ...), kind=kOutput, calls=%fused_computation.9.clone.1 | convolution fusion | flops 207814656 | bytes 5189632 | tf_op jit(solution)/shard_map/while/body/eval_jaxpr/qk,kd->qd/dot_general | solution.py:58
  127.7 9.6 %collective-permute-done = bf16[1024,194]{0,1:T(8,128)(2,1)S(1)} collective-permute-done((bf16[1024,194]{0,1:T(8,128)(2,1)S(1)}, bf16[1024,194]{0,1:T(8,128)(2,1)S(1)}, u32[]{:S(2)}, u32[]{:S(2)}) %collective-permute-start) | collective-permute-done | bytes 397344 | tf_op jit(solution)/shard_map/while/body/eval_jaxpr/ppermute | solution.py:21
  137.3 9.7 %collective-permute-start = (bf16[1024,194]{0,1:T(8,128)(2,1)S(1)}, bf16[1024,194]{0,1:T(8,128)(2,1)S(1)}, u32[]{:S(2)}, u32[]{:S(2)}) collective-permute-start(bf16[1024,194]{0,1:T(8,128)(2,1)S(1)} %copy.90), channel_id=1, source_target_pairs={{0,32},{32,64},{64,96},{96,128},{128,160},{160,192},{192,224},{224... | collective-permute-start | bytes 1191944 | tf_op jit(solution)/shard_map/while/body/eval_jaxpr/ppermute | solution.py:21
  156.5 10.4 %collective-permute-done = bf16[1024,194]{0,1:T(8,128)(2,1)S(1)} collective-permute-done((bf16[1024,194]{0,1:T(8,128)(2,1)S(1)}, bf16[1024,194]{0,1:T(8,128)(2,1)S(1)}, u32[]{:S(2)}, u32[]{:S(2)}) %collective-permute-start) | collective-permute-done | bytes 397344 | tf_op jit(solution)/shard_map/while/body/eval_jaxpr/ppermute | solution.py:21
  166.9 11.8 %collective-permute-start = (bf16[1024,194]{0,1:T(8,128)(2,1)S(1)}, bf16[1024,194]{0,1:T(8,128)(2,1)S(1)}, u32[]{:S(2)}, u32[]{:S(2)}) collective-permute-start(bf16[1024,194]{0,1:T(8,128)(2,1)S(1)} %copy.90), channel_id=1, source_target_pairs={{0,32},{32,64},{64,96},{96,128},{128,160},{160,192},{192,224},{224... | collective-permute-start | bytes 1191944 | tf_op jit(solution)/shard_map/while/body/eval_jaxpr/ppermute | solution.py:21
  183.9 4.2 %fusion.130 = f32[1024,96]{0,1:T(8,128)} fusion(f32[1024,1024]{0,1:T(8,128)} %copy-done.1, f32[1024]{0:T(1024)S(1)} %max.31, bf16[1024]{0:T(1024)(128)(2,1)S(1)} %reduce.31, bf16[1024]{0:T(1024)(128)(2,1)S(1)} %get-tuple-element.476, f32[1024,96]{0,1:T(8,128)} %get-tuple-element.497, bf16[1024,194]{0,1:T(8,128)(2,1)S(1)} %copy.90, ...), kind=kOutput, calls=%fused_computation.9.clone.1 | convolution fusion | flops 207814656 | bytes 5189632 | tf_op jit(solution)/shard_map/while/body/eval_jaxpr/qk,kd->qd/dot_general | solution.py:58
  188.1 14.1 %collective-permute-done = bf16[1024,194]{0,1:T(8,128)(2,1)S(1)} collective-permute-done((bf16[1024,194]{0,1:T(8,128)(2,1)S(1)}, bf16[1024,194]{0,1:T(8,128)(2,1)S(1)}, u32[]{:S(2)}, u32[]{:S(2)}) %collective-permute-start) | collective-permute-done | bytes 397344 | tf_op jit(solution)/shard_map/while/body/eval_jaxpr/ppermute | solution.py:21
  202.1 10.4 %collective-permute-start = (bf16[1024,194]{0,1:T(8,128)(2,1)S(1)}, bf16[1024,194]{0,1:T(8,128)(2,1)S(1)}, u32[]{:S(2)}, u32[]{:S(2)}) collective-permute-start(bf16[1024,194]{0,1:T(8,128)(2,1)S(1)} %copy.90), channel_id=1, source_target_pairs={{0,32},{32,64},{64,96},{96,128},{128,160},{160,192},{192,224},{224... | collective-permute-start | bytes 1191944 | tf_op jit(solution)/shard_map/while/body/eval_jaxpr/ppermute | solution.py:21
  217.8 4.2 %fusion.130 = f32[1024,96]{0,1:T(8,128)} fusion(f32[1024,1024]{0,1:T(8,128)} %copy-done.1, f32[1024]{0:T(1024)S(1)} %max.31, bf16[1024]{0:T(1024)(128)(2,1)S(1)} %reduce.31, bf16[1024]{0:T(1024)(128)(2,1)S(1)} %get-tuple-element.476, f32[1024,96]{0,1:T(8,128)} %get-tuple-element.497, bf16[1024,194]{0,1:T(8,128)(2,1)S(1)} %copy.90, ...), kind=kOutput, calls=%fused_computation.9.clone.1 | convolution fusion | flops 207814656 | bytes 5189632 | tf_op jit(solution)/shard_map/while/body/eval_jaxpr/qk,kd->qd/dot_general | solution.py:58
  225.6 13.5 %collective-permute-start = (bf16[1024,194]{0,1:T(8,128)(2,1)S(1)}, bf16[1024,194]{0,1:T(8,128)(2,1)S(1)}, u32[]{:S(2)}, u32[]{:S(2)}) collective-permute-start(bf16[1024,194]{0,1:T(8,128)(2,1)S(1)} %copy.90), channel_id=1, source_target_pairs={{0,32},{32,64},{64,96},{96,128},{128,160},{160,192},{192,224},{224... | collective-permute-start | bytes 1191944 | tf_op jit(solution)/shard_map/while/body/eval_jaxpr/ppermute | solution.py:21
  263.4 7.7 %all_to_all.21 = bf16[4,256,96]{1,2,0:T(8,128)(2,1)S(1)} all-to-all(bf16[4,256,96]{1,2,0:T(8,128)(2,1)S(1)} %fusion.46), channel_id=1, replica_groups=mesh['seq_hi'=16,'seq_lo'=4,'tp'=8] {'seq_lo'}, dimensions={0} | all-to-all | bytes 393216 | tf_op jit(solution)/shard_map/all_to_all | solution.py:171
  273.5 7.7 %all-to-all-start.2 = ((bf16[8,256,384]{2,1,0:T(8,128)(2,1)}), bf16[8,256,384]{2,1,0:T(8,128)(2,1)}, u32[]{:S(2)}, u32[]{:S(2)}) async-start(bf16[8,256,384]{2,1,0:T(8,128)(2,1)} %bitcast.46), calls=%async_computation.2 | async-start | bytes 3145728 | tf_op jit(solution)/shard_map/all_to_all | solution.py:183
  282.3 20.2 %all-to-all-done.2 = bf16[8,256,384]{2,1,0:T(8,128)(2,1)} async-done(((bf16[8,256,384]{2,1,0:T(8,128)(2,1)}), bf16[8,256,384]{2,1,0:T(8,128)(2,1)}, u32[]{:S(2)}, u32[]{:S(2)}) %all-to-all-start.2) | async-done | bytes 1572896 | tf_op jit(solution)/shard_map/all_to_all | solution.py:183
  310.2 4.4 %all-to-all-done.3 = f32[8,1,256]{2,1,0:T(1,128)S(1)} async-done(((f32[8,1,256]{2,1,0:T(1,128)}), f32[8,1,256]{2,1,0:T(1,128)S(1)}, u32[]{:S(2)}, u32[]{:S(2)}) %all-to-all-start.3) | async-done | bytes 8224 | tf_op jit(solution)/shard_map/all_to_all | solution.py:189
  (278 shorter events, 99.1 us)
Async XLA Ops:
  0.6 270.4 %copy-start = (bf16[384,3072]{1,0:T(8,128)(2,1)S(1)}, bf16[384,3072]{1,0:T(8,128)(2,1)}, u32[]{:S(2)}) copy-start(bf16[384,3072]{1,0:T(8,128)(2,1)} %param.15) | copy-start | bytes 7077892
  5.9 13.1 %all-to-all-start = ((bf16[4,256,290]{1,2,0:T(8,128)(2,1)}), bf16[4,256,290]{1,2,0:T(8,128)(2,1)S(1)}, u32[]{:S(2)}, u32[]{:S(2)}) async-start(bf16[4,256,290]{1,2,0:T(8,128)(2,1)} %bitcast.61), calls=%async_computation | async-start | bytes 1212416 | tf_op jit(solution)/shard_map/all_to_all | solution.py:103
  9.4 24.0 %copy-start.35 = (bf16[32]{0:T(256)(128)(2,1)}, bf16[32]{0:T(256)(128)(2,1)S(1)}, u32[]{:S(2)}) copy-start(bf16[32]{0:T(256)(128)(2,1)S(1)} %add_convert_fusion.5) | copy-start | bytes 196
  19.6 13.9 %copy-start.5 = (bf16[37,8,4,256]{3,1,2,0:T(8,128)(2,1)}, bf16[37,8,4,256]{3,1,2,0:T(8,128)(2,1)S(1)}, u32[]{:S(2)}) copy-start(bf16[37,8,4,256]{3,1,2,0:T(8,128)(2,1)S(1)} %copy.68) | copy-start | bytes 1818628
  21.2 232.6 %copy-start.31 = (bf16[256]{0:T(256)(128)(2,1)}, bf16[256]{0:T(256)(128)(2,1)S(1)}, u32[]{:S(2)}) copy-start(bf16[256]{0:T(256)(128)(2,1)S(1)} %get-tuple-element.344) | copy-start | bytes 1540
  21.2 232.7 %copy-start.37 = (bf16[256]{0:T(256)(128)(2,1)}, bf16[256]{0:T(256)(128)(2,1)S(1)}, u32[]{:S(2)}) copy-start(bf16[256]{0:T(256)(128)(2,1)S(1)} %get-tuple-element.346) | copy-start | bytes 1540
  21.2 233.2 %copy-start.33 = (bf16[256]{0:T(256)(128)(2,1)}, bf16[256]{0:T(256)(128)(2,1)S(1)}, u32[]{:S(2)}) copy-start(bf16[256]{0:T(256)(128)(2,1)S(1)} %get-tuple-element.345) | copy-start | bytes 1540
  21.3 233.5 %copy-start.34 = (bf16[256]{0:T(256)(128)(2,1)}, bf16[256]{0:T(256)(128)(2,1)S(1)}, u32[]{:S(2)}) copy-start(bf16[256]{0:T(256)(128)(2,1)S(1)} %get-tuple-element.343) | copy-start | bytes 1540
  24.9 23.7 %collective-permute-start.1 = (bf16[1024,194]{0,1:T(8,128)(2,1)}, bf16[1024,194]{0,1:T(8,128)(2,1)S(1)}, u32[]{:S(2)}, u32[]{:S(2)}) collective-permute-start(bf16[1024,194]{0,1:T(8,128)(2,1)} %slice.241), channel_id=1, source_target_pairs={{0,32},{32,64},{64,96},{96,128},{128,160},{160,192},{192,224},{224... | collective-permute-start | bytes 1191944 | tf_op jit(solution)/shard_map/ppermute | solution.py:21
  48.7 26.5 %collective-permute-start = (bf16[1024,194]{0,1:T(8,128)(2,1)S(1)}, bf16[1024,194]{0,1:T(8,128)(2,1)S(1)}, u32[]{:S(2)}, u32[]{:S(2)}) collective-permute-start(bf16[1024,194]{0,1:T(8,128)(2,1)S(1)} %copy.90), channel_id=1, source_target_pairs={{0,32},{32,64},{64,96},{96,128},{128,160},{160,192},{192,224},{224... | collective-permute-start | bytes 1191944 | tf_op jit(solution)/shard_map/while/body/eval_jaxpr/ppermute | solution.py:21
  75.3 33.4 %collective-permute-start = (bf16[1024,194]{0,1:T(8,128)(2,1)S(1)}, bf16[1024,194]{0,1:T(8,128)(2,1)S(1)}, u32[]{:S(2)}, u32[]{:S(2)}) collective-permute-start(bf16[1024,194]{0,1:T(8,128)(2,1)S(1)} %copy.90), channel_id=1, source_target_pairs={{0,32},{32,64},{64,96},{96,128},{128,160},{160,192},{192,224},{224... | collective-permute-start | bytes 1191944 | tf_op jit(solution)/shard_map/while/body/eval_jaxpr/ppermute | solution.py:21
  108.7 28.6 %collective-permute-start = (bf16[1024,194]{0,1:T(8,128)(2,1)S(1)}, bf16[1024,194]{0,1:T(8,128)(2,1)S(1)}, u32[]{:S(2)}, u32[]{:S(2)}) collective-permute-start(bf16[1024,194]{0,1:T(8,128)(2,1)S(1)} %copy.90), channel_id=1, source_target_pairs={{0,32},{32,64},{64,96},{96,128},{128,160},{160,192},{192,224},{224... | collective-permute-start | bytes 1191944 | tf_op jit(solution)/shard_map/while/body/eval_jaxpr/ppermute | solution.py:21
  137.3 29.5 %collective-permute-start = (bf16[1024,194]{0,1:T(8,128)(2,1)S(1)}, bf16[1024,194]{0,1:T(8,128)(2,1)S(1)}, u32[]{:S(2)}, u32[]{:S(2)}) collective-permute-start(bf16[1024,194]{0,1:T(8,128)(2,1)S(1)} %copy.90), channel_id=1, source_target_pairs={{0,32},{32,64},{64,96},{96,128},{128,160},{160,192},{192,224},{224... | collective-permute-start | bytes 1191944 | tf_op jit(solution)/shard_map/while/body/eval_jaxpr/ppermute | solution.py:21
  166.9 35.2 %collective-permute-start = (bf16[1024,194]{0,1:T(8,128)(2,1)S(1)}, bf16[1024,194]{0,1:T(8,128)(2,1)S(1)}, u32[]{:S(2)}, u32[]{:S(2)}) collective-permute-start(bf16[1024,194]{0,1:T(8,128)(2,1)S(1)} %copy.90), channel_id=1, source_target_pairs={{0,32},{32,64},{64,96},{96,128},{128,160},{160,192},{192,224},{224... | collective-permute-start | bytes 1191944 | tf_op jit(solution)/shard_map/while/body/eval_jaxpr/ppermute | solution.py:21
  202.1 23.4 %collective-permute-start = (bf16[1024,194]{0,1:T(8,128)(2,1)S(1)}, bf16[1024,194]{0,1:T(8,128)(2,1)S(1)}, u32[]{:S(2)}, u32[]{:S(2)}) collective-permute-start(bf16[1024,194]{0,1:T(8,128)(2,1)S(1)} %copy.90), channel_id=1, source_target_pairs={{0,32},{32,64},{64,96},{96,128},{128,160},{160,192},{192,224},{224... | collective-permute-start | bytes 1191944 | tf_op jit(solution)/shard_map/while/body/eval_jaxpr/ppermute | solution.py:21
  225.6 22.9 %collective-permute-start = (bf16[1024,194]{0,1:T(8,128)(2,1)S(1)}, bf16[1024,194]{0,1:T(8,128)(2,1)S(1)}, u32[]{:S(2)}, u32[]{:S(2)}) collective-permute-start(bf16[1024,194]{0,1:T(8,128)(2,1)S(1)} %copy.90), channel_id=1, source_target_pairs={{0,32},{32,64},{64,96},{96,128},{128,160},{160,192},{192,224},{224... | collective-permute-start | bytes 1191944 | tf_op jit(solution)/shard_map/while/body/eval_jaxpr/ppermute | solution.py:21
  271.1 10.1 %copy-start.10 = (bf16[256,384]{1,0:T(8,128)(2,1)S(1)}, bf16[256,384]{1,0:T(8,128)(2,1)}, u32[]{:S(2)}) copy-start(bf16[256,384]{1,0:T(8,128)(2,1)} %param.13) | copy-start | bytes 589828
  271.1 10.1 %copy-start.25 = (bf16[256]{0:T(256)(128)(2,1)S(1)}, bf16[256]{0:T(256)(128)(2,1)}, u32[]{:S(2)}) copy-start(bf16[256]{0:T(256)(128)(2,1)} %get-tuple-element.402) | copy-start | bytes 1540
  272.1 9.8 %copy-start.30 = (f32[48]{0:T(128)S(1)}, f32[48]{0:T(128)}, u32[]{:S(2)}) copy-start(f32[48]{0:T(128)} %copy-done.29) | copy-start | bytes 580
  272.2 10.0 %copy-start.3 = (f32[256,4,96]{0,2,1:T(8,128)S(1)}, f32[256,4,96]{0,2,1:T(8,128)}, u32[]{:S(2)}) copy-start(f32[256,4,96]{0,2,1:T(8,128)} %copy-done.2) | copy-start | bytes 1179652
  273.5 30.8 %copy-start.15 = (bf16[256,384]{1,0:T(8,128)(2,1)S(1)}, bf16[256,384]{1,0:T(8,128)(2,1)}, u32[]{:S(2)}) copy-start(bf16[256,384]{1,0:T(8,128)(2,1)} %param.14) | copy-start | bytes 589828
  273.5 29.1 %all-to-all-start.2 = ((bf16[8,256,384]{2,1,0:T(8,128)(2,1)}), bf16[8,256,384]{2,1,0:T(8,128)(2,1)}, u32[]{:S(2)}, u32[]{:S(2)}) async-start(bf16[8,256,384]{2,1,0:T(8,128)(2,1)} %bitcast.46), calls=%async_computation.2 | async-start | bytes 3145728 | tf_op jit(solution)/shard_map/all_to_all | solution.py:183
  304.4 11.0 %copy-start.12 = (bf16[256,384]{1,0:T(8,128)(2,1)}, bf16[256,384]{1,0:T(8,128)(2,1)S(1)}, u32[]{:S(2)}) copy-start(bf16[256,384]{1,0:T(8,128)(2,1)S(1)} %get-tuple-element.372) | copy-start | bytes 589828
  305.1 9.5 %all-to-all-start.3 = ((f32[8,1,256]{2,1,0:T(1,128)}), f32[8,1,256]{2,1,0:T(1,128)S(1)}, u32[]{:S(2)}, u32[]{:S(2)}) async-start(f32[8,1,256]{2,1,0:T(1,128)} %broadcast_in_dim.211), calls=%async_computation.3 | async-start | bytes 16384 | tf_op jit(solution)/shard_map/all_to_all | solution.py:189
  (39 other events, 165.2 us)

commit v10 on v3

--- a/solution.py
+++ b/solution.py
@@ -80,7 +80,6 @@
     seg_count = lo_count * hi_count // 2
     device_row = lax.axis_index("seq_hi") * lo_count + lax.axis_index("seq_lo")
     tok_index = device_row * tok_count + jnp.arange(tok_count, dtype=jnp.int32)
-    q_rot = rotate(query_proj, tok_index, head_count, HEAD_DIM)
     k_abs = rotate(key_proj, tok_index, head_count, HEAD_DIM)
     query_tag = segment_ids + 1
     key_tag = jnp.where(pad_mask == 1, segment_ids + 1, 0)
@@ -93,7 +92,7 @@
     tags = jnp.stack([key_tag, query_tag], axis=-1).astype(jnp.bfloat16)
     payload = jnp.concatenate(
         [
-            q_rot.reshape(tok_count, head_count, HEAD_DIM),
+            query_proj.reshape(tok_count, head_count, HEAD_DIM),
             k_abs.reshape(tok_count, head_count, HEAD_DIM),
             value_proj.reshape(tok_count, head_count, HEAD_DIM),
             jnp.broadcast_to(tags[:, None, :], (tok_count, head_count, 2)),
@@ -103,7 +102,12 @@
     chunk = lax.all_to_all(payload, "seq_lo", 0, 0, tiled=True)
     chunk_count = lo_count * tok_count
     chunk = chunk.reshape(chunk_count, 3 * HEAD_DIM + 2)
-    chunk_q = chunk[:, :HEAD_DIM]
+    chunk_q = rotate(
+        chunk[:, :HEAD_DIM],
+        lax.axis_index("seq_hi") * chunk_count + jnp.arange(chunk_count, dtype=jnp.int32),
+        1,
+        HEAD_DIM,
+    )
     chunk_k = chunk[:, HEAD_DIM : 2 * HEAD_DIM]
     chunk_v = chunk[:, 2 * HEAD_DIM : 3 * HEAD_DIM]
     chunk_ktag = chunk[:, 3 * HEAD_DIM]

time: 294 us -> 301 us (1.024)
  other arithmetic: 18.9 us -> 22.3 us
    unnamed x50 -> x47, local copies, waits for them, and re-layouts: 6.14 us -> 7.36 us
  transfers between devices with their start and end apart: 11 -> 11, of which waited for: 9 -> 9; matrix products, arithmetic and copies ran while one was open for 21% -> 20% of each run, Pallas kernels for 0% -> 0%
where the time goes in v10:
time: 301 us
  starting transfers between devices  97 us (32%)
  waiting for transfers between devices  96.4 us (32%)
  matrix products  49.9 us (17%)
  local copies, waits for them, and re-layouts  25.6 us (9%)
  other arithmetic  22.3 us (7%)
  blocking collectives  7.67 us (3%)
    ppermute x8, starting transfers between devices, passed_along(): return lax.ppermute(block, axis, route)  85.8 us
    ppermute x8, waiting for transfers between devices, passed_along(): return lax.ppermute(block, axis, route)  62 us
    dot_general x9, matrix products, attend(): jnp.einsum('qk,kd->qd', unnormed.astype(jnp.bfloat16), val_heads, preferr...  34.5 us
    all_to_all x1, waiting for transfers between devices, per_device(): gathered = lax.all_to_all(pieces, 'tp', 0, 0, tiled=True)  20.4 us
    dot_general x9, matrix products, attend(): jnp.einsum('qd,kd->qk', query_heads, key_heads, preferred_element_type=jn...  14.4 us
    while x28, local copies, waits for them, and re-layouts  13.6 us
    reduce_sum x9, other arithmetic, attend(): row_total = row_total * rescale + jnp.sum(unnormed, axis=-1)  11.9 us
    all_to_all x1, waiting for transfers between devices, per_device(): chunk = lax.all_to_all(payload, 'seq_lo', 0, 0, tiled=True)  9.62 us
  transfers between devices with their start and end apart: 11, of which 9 were waited for; matrix products, arithmetic and copies ran while one was open for 20% of the time, Pallas kernels for 0%

profile of v10, /device:TPU:176, one launch (start us, length us, event | category | flops | bytes accessed | tf_op | source)
XLA Modules:
  0.0 300.6 jit_solution(15832171121520053519)
XLA Ops:
  12.0 9.6 %all-to-all-done = bf16[4,256,290]{1,2,0:T(8,128)(2,1)S(1)} async-done(((bf16[4,256,290]{1,2,0:T(8,128)(2,1)}), bf16[4,256,290]{1,2,0:T(8,128)(2,1)S(1)}, u32[]{:S(2)}, u32[]{:S(2)}) %all-to-all-start) | async-done | bytes 593952 | tf_op jit(solution)/shard_map/all_to_all | solution.py:102
  30.3 6.8 %collective-permute-start.1 = (bf16[1024,194]{0,1:T(8,128)(2,1)}, bf16[1024,194]{0,1:T(8,128)(2,1)S(1)}, u32[]{:S(2)}, u32[]{:S(2)}) collective-permute-start(bf16[1024,194]{0,1:T(8,128)(2,1)} %slice.107), channel_id=1, source_target_pairs={{0,32},{32,64},{64,96},{96,128},{128,160},{160,192},{192,224},{224... | collective-permute-start | bytes 1191944 | tf_op jit(solution)/shard_map/ppermute | solution.py:21
  41.3 12.7 %collective-permute-done.1 = bf16[1024,194]{0,1:T(8,128)(2,1)S(1)} collective-permute-done((bf16[1024,194]{0,1:T(8,128)(2,1)}, bf16[1024,194]{0,1:T(8,128)(2,1)S(1)}, u32[]{:S(2)}, u32[]{:S(2)}) %collective-permute-start.1) | collective-permute-done | bytes 397344 | tf_op jit(solution)/shard_map/ppermute | solution.py:21
  54.0 194.3 %while.24 = (s32[]{:T(128)}, f32[1024]{0:T(1024)S(1)}, f32[1024]{0:T(1024)S(1)}, f32[1024,96]{0,1:T(8,128)}, s32[32]{0:T(128)S(1)}, /*index=5*/bf16[1024,194]{0,...) while((s32[]{:T(128)}, f32[1024]{0:T(1024)S(1)}, ...), condition=%wide.region_7.8_spmd.clone, body=%wide.region_3.7_spmd.clone.sunk | while | flops 419728448 | bytes 33221464 | solution.py:148
  54.1 11.7 %collective-permute-start = (bf16[1024,194]{0,1:T(8,128)(2,1)S(1)}, bf16[1024,194]{0,1:T(8,128)(2,1)S(1)}, u32[]{:S(2)}, u32[]{:S(2)}) collective-permute-start(bf16[1024,194]{0,1:T(8,128)(2,1)S(1)} %copy.89), channel_id=1, source_target_pairs={{0,32},{32,64},{64,96},{96,128},{128,160},{160,192},{192,224},{224... | collective-permute-start | bytes 1191944 | tf_op jit(solution)/shard_map/while/body/eval_jaxpr/ppermute | solution.py:21
  79.1 13.3 %collective-permute-start = (bf16[1024,194]{0,1:T(8,128)(2,1)S(1)}, bf16[1024,194]{0,1:T(8,128)(2,1)S(1)}, u32[]{:S(2)}, u32[]{:S(2)}) collective-permute-start(bf16[1024,194]{0,1:T(8,128)(2,1)S(1)} %copy.89), channel_id=1, source_target_pairs={{0,32},{32,64},{64,96},{96,128},{128,160},{160,192},{192,224},{224... | collective-permute-start | bytes 1191944 | tf_op jit(solution)/shard_map/while/body/eval_jaxpr/ppermute | solution.py:21
  97.7 4.2 %fusion.87 = f32[1024,96]{0,1:T(8,128)} fusion(f32[1024,1024]{0,1:T(8,128)} %copy-done.1, f32[1024]{0:T(1024)S(1)} %max.15, bf16[1024]{0:T(1024)(128)(2,1)S(1)} %reduce.17, bf16[1024]{0:T(1024)(128)(2,1)S(1)} %get-tuple-element.452, f32[1024,96]{0,1:T(8,128)} %get-tuple-element.473, bf16[1024,194]{0,1:T(8,128)(2,1)S(1)} %copy.89, ...), kind=kOutput, calls=%fused_computation.9.clone.1 | convolution fusion | flops 207814656 | bytes 5189632 | tf_op jit(solution)/shard_map/while/body/eval_jaxpr/qk,kd->qd/dot_general | solution.py:58
  101.8 14.6 %collective-permute-done = bf16[1024,194]{0,1:T(8,128)(2,1)S(1)} collective-permute-done((bf16[1024,194]{0,1:T(8,128)(2,1)S(1)}, bf16[1024,194]{0,1:T(8,128)(2,1)S(1)}, u32[]{:S(2)}, u32[]{:S(2)}) %collective-permute-start) | collective-permute-done | bytes 397344 | tf_op jit(solution)/shard_map/while/body/eval_jaxpr/ppermute | solution.py:21
  116.4 10.3 %collective-permute-start = (bf16[1024,194]{0,1:T(8,128)(2,1)S(1)}, bf16[1024,194]{0,1:T(8,128)(2,1)S(1)}, u32[]{:S(2)}, u32[]{:S(2)}) collective-permute-start(bf16[1024,194]{0,1:T(8,128)(2,1)S(1)} %copy.89), channel_id=1, source_target_pairs={{0,32},{32,64},{64,96},{96,128},{128,160},{160,192},{192,224},{224... | collective-permute-start | bytes 1191944 | tf_op jit(solution)/shard_map/while/body/eval_jaxpr/ppermute | solution.py:21
  131.9 4.2 %fusion.87 = f32[1024,96]{0,1:T(8,128)} fusion(f32[1024,1024]{0,1:T(8,128)} %copy-done.1, f32[1024]{0:T(1024)S(1)} %max.15, bf16[1024]{0:T(1024)(128)(2,1)S(1)} %reduce.17, bf16[1024]{0:T(1024)(128)(2,1)S(1)} %get-tuple-element.452, f32[1024,96]{0,1:T(8,128)} %get-tuple-element.473, bf16[1024,194]{0,1:T(8,128)(2,1)S(1)} %copy.89, ...), kind=kOutput, calls=%fused_computation.9.clone.1 | convolution fusion | flops 207814656 | bytes 5189632 | tf_op jit(solution)/shard_map/while/body/eval_jaxpr/qk,kd->qd/dot_general | solution.py:58
  136.1 8.1 %collective-permute-done = bf16[1024,194]{0,1:T(8,128)(2,1)S(1)} collective-permute-done((bf16[1024,194]{0,1:T(8,128)(2,1)S(1)}, bf16[1024,194]{0,1:T(8,128)(2,1)S(1)}, u32[]{:S(2)}, u32[]{:S(2)}) %collective-permute-start) | collective-permute-done | bytes 397344 | tf_op jit(solution)/shard_map/while/body/eval_jaxpr/ppermute | solution.py:21
  144.3 11.0 %collective-permute-start = (bf16[1024,194]{0,1:T(8,128)(2,1)S(1)}, bf16[1024,194]{0,1:T(8,128)(2,1)S(1)}, u32[]{:S(2)}, u32[]{:S(2)}) collective-permute-start(bf16[1024,194]{0,1:T(8,128)(2,1)S(1)} %copy.89), channel_id=1, source_target_pairs={{0,32},{32,64},{64,96},{96,128},{128,160},{160,192},{192,224},{224... | collective-permute-start | bytes 1191944 | tf_op jit(solution)/shard_map/while/body/eval_jaxpr/ppermute | solution.py:21
  164.7 13.5 %collective-permute-done = bf16[1024,194]{0,1:T(8,128)(2,1)S(1)} collective-permute-done((bf16[1024,194]{0,1:T(8,128)(2,1)S(1)}, bf16[1024,194]{0,1:T(8,128)(2,1)S(1)}, u32[]{:S(2)}, u32[]{:S(2)}) %collective-permute-start) | collective-permute-done | bytes 397344 | tf_op jit(solution)/shard_map/while/body/eval_jaxpr/ppermute | solution.py:21
  178.3 11.5 %collective-permute-start = (bf16[1024,194]{0,1:T(8,128)(2,1)S(1)}, bf16[1024,194]{0,1:T(8,128)(2,1)S(1)}, u32[]{:S(2)}, u32[]{:S(2)}) collective-permute-start(bf16[1024,194]{0,1:T(8,128)(2,1)S(1)} %copy.89), channel_id=1, source_target_pairs={{0,32},{32,64},{64,96},{96,128},{128,160},{160,192},{192,224},{224... | collective-permute-start | bytes 1191944 | tf_op jit(solution)/shard_map/while/body/eval_jaxpr/ppermute | solution.py:21
  195.0 4.2 %fusion.87 = f32[1024,96]{0,1:T(8,128)} fusion(f32[1024,1024]{0,1:T(8,128)} %copy-done.1, f32[1024]{0:T(1024)S(1)} %max.15, bf16[1024]{0:T(1024)(128)(2,1)S(1)} %reduce.17, bf16[1024]{0:T(1024)(128)(2,1)S(1)} %get-tuple-element.452, f32[1024,96]{0,1:T(8,128)} %get-tuple-element.473, bf16[1024,194]{0,1:T(8,128)(2,1)S(1)} %copy.89, ...), kind=kOutput, calls=%fused_computation.9.clone.1 | convolution fusion | flops 207814656 | bytes 5189632 | tf_op jit(solution)/shard_map/while/body/eval_jaxpr/qk,kd->qd/dot_general | solution.py:58
  199.1 9.1 %collective-permute-done = bf16[1024,194]{0,1:T(8,128)(2,1)S(1)} collective-permute-done((bf16[1024,194]{0,1:T(8,128)(2,1)S(1)}, bf16[1024,194]{0,1:T(8,128)(2,1)S(1)}, u32[]{:S(2)}, u32[]{:S(2)}) %collective-permute-start) | collective-permute-done | bytes 397344 | tf_op jit(solution)/shard_map/while/body/eval_jaxpr/ppermute | solution.py:21
  208.3 11.9 %collective-permute-start = (bf16[1024,194]{0,1:T(8,128)(2,1)S(1)}, bf16[1024,194]{0,1:T(8,128)(2,1)S(1)}, u32[]{:S(2)}, u32[]{:S(2)}) collective-permute-start(bf16[1024,194]{0,1:T(8,128)(2,1)S(1)} %copy.89), channel_id=1, source_target_pairs={{0,32},{32,64},{64,96},{96,128},{128,160},{160,192},{192,224},{224... | collective-permute-start | bytes 1191944 | tf_op jit(solution)/shard_map/while/body/eval_jaxpr/ppermute | solution.py:21
  225.4 4.2 %fusion.87 = f32[1024,96]{0,1:T(8,128)} fusion(f32[1024,1024]{0,1:T(8,128)} %copy-done.1, f32[1024]{0:T(1024)S(1)} %max.15, bf16[1024]{0:T(1024)(128)(2,1)S(1)} %reduce.17, bf16[1024]{0:T(1024)(128)(2,1)S(1)} %get-tuple-element.452, f32[1024,96]{0,1:T(8,128)} %get-tuple-element.473, bf16[1024,194]{0,1:T(8,128)(2,1)S(1)} %copy.89, ...), kind=kOutput, calls=%fused_computation.9.clone.1 | convolution fusion | flops 207814656 | bytes 5189632 | tf_op jit(solution)/shard_map/while/body/eval_jaxpr/qk,kd->qd/dot_general | solution.py:58
  229.6 9.3 %collective-permute-start = (bf16[1024,194]{0,1:T(8,128)(2,1)S(1)}, bf16[1024,194]{0,1:T(8,128)(2,1)S(1)}, u32[]{:S(2)}, u32[]{:S(2)}) collective-permute-start(bf16[1024,194]{0,1:T(8,128)(2,1)S(1)} %copy.89), channel_id=1, source_target_pairs={{0,32},{32,64},{64,96},{96,128},{128,160},{160,192},{192,224},{224... | collective-permute-start | bytes 1191944 | tf_op jit(solution)/shard_map/while/body/eval_jaxpr/ppermute | solution.py:21
  244.2 4.2 %fusion.87 = f32[1024,96]{0,1:T(8,128)} fusion(f32[1024,1024]{0,1:T(8,128)} %copy-done.1, f32[1024]{0:T(1024)S(1)} %max.15, bf16[1024]{0:T(1024)(128)(2,1)S(1)} %reduce.17, bf16[1024]{0:T(1024)(128)(2,1)S(1)} %get-tuple-element.452, f32[1024,96]{0,1:T(8,128)} %get-tuple-element.473, bf16[1024,194]{0,1:T(8,128)(2,1)S(1)} %copy.89, ...), kind=kOutput, calls=%fused_computation.9.clone.1 | convolution fusion | flops 207814656 | bytes 5189632 | tf_op jit(solution)/shard_map/while/body/eval_jaxpr/qk,kd->qd/dot_general | solution.py:58
  251.7 7.7 %all_to_all.21 = bf16[4,256,96]{1,2,0:T(8,128)(2,1)S(1)} all-to-all(bf16[4,256,96]{1,2,0:T(8,128)(2,1)S(1)} %bitcast.70), channel_id=1, replica_groups=mesh['seq_hi'=16,'seq_lo'=4,'tp'=8] {'seq_lo'}, dimensions={0} | all-to-all | bytes 393216 | tf_op jit(solution)/shard_map/all_to_all | solution.py:157
  261.8 4.4 %all-to-all-start.2 = ((bf16[8,256,384]{2,1,0:T(8,128)(2,1)}), bf16[8,256,384]{2,1,0:T(8,128)(2,1)}, u32[]{:S(2)}, u32[]{:S(2)}) async-start(bf16[8,256,384]{2,1,0:T(8,128)(2,1)} %bitcast.57), calls=%async_computation.2 | async-start | bytes 3145728 | tf_op jit(solution)/shard_map/all_to_all | solution.py:169
  267.3 20.4 %all-to-all-done.2 = bf16[8,256,384]{2,1,0:T(8,128)(2,1)} async-done(((bf16[8,256,384]{2,1,0:T(8,128)(2,1)}), bf16[8,256,384]{2,1,0:T(8,128)(2,1)}, u32[]{:S(2)}, u32[]{:S(2)}) %all-to-all-start.2) | async-done | bytes 1572896 | tf_op jit(solution)/shard_map/all_to_all | solution.py:169
  295.4 4.4 %all-to-all-done.3 = f32[8,1,256]{2,1,0:T(1,128)S(1)} async-done(((f32[8,1,256]{2,1,0:T(1,128)}), f32[8,1,256]{2,1,0:T(1,128)S(1)}, u32[]{:S(2)}, u32[]{:S(2)}) %all-to-all-start.3) | async-done | bytes 8224 | tf_op jit(solution)/shard_map/all_to_all | solution.py:175
  (211 shorter events, 87.6 us)
Async XLA Ops:
  0.6 258.8 %copy-start = (bf16[384,3072]{1,0:T(8,128)(2,1)S(1)}, bf16[384,3072]{1,0:T(8,128)(2,1)}, u32[]{:S(2)}) copy-start(bf16[384,3072]{1,0:T(8,128)(2,1)} %param.15) | copy-start | bytes 7077892
  2.8 20.2 %copy-start.2 = (f32[256,4,96]{0,2,1:T(8,128)}, f32[256,4,96]{0,2,1:T(8,128)S(1)}, u32[]{:S(2)}) copy-start(f32[256,4,96]{0,2,1:T(8,128)S(1)} %convert.36) | copy-start | bytes 1179652
  7.6 15.5 %copy-start.13 = (f32[48]{0:T(128)S(1)}, f32[48]{0:T(128)}, u32[]{:S(2)}) copy-start(f32[48]{0:T(128)} %multiply_exponential_fusion) | copy-start | bytes 580
  8.4 13.1 %all-to-all-start = ((bf16[4,256,290]{1,2,0:T(8,128)(2,1)}), bf16[4,256,290]{1,2,0:T(8,128)(2,1)S(1)}, u32[]{:S(2)}, u32[]{:S(2)}) async-start(bf16[4,256,290]{1,2,0:T(8,128)(2,1)} %bitcast.66), calls=%async_computation | async-start | bytes 1212416 | tf_op jit(solution)/shard_map/all_to_all | solution.py:102
  30.3 23.7 %collective-permute-start.1 = (bf16[1024,194]{0,1:T(8,128)(2,1)}, bf16[1024,194]{0,1:T(8,128)(2,1)S(1)}, u32[]{:S(2)}, u32[]{:S(2)}) collective-permute-start(bf16[1024,194]{0,1:T(8,128)(2,1)} %slice.107), channel_id=1, source_target_pairs={{0,32},{32,64},{64,96},{96,128},{128,160},{160,192},{192,224},{224... | collective-permute-start | bytes 1191944 | tf_op jit(solution)/shard_map/ppermute | solution.py:21
  54.0 194.4 %copy-start.10 = (bf16[1024,1,48]{0,2,1:T(8,128)(2,1)S(1)}, bf16[1024,1,48]{0,2,1:T(8,128)(2,1)}, u32[]{:S(2)}) copy-start(bf16[1024,1,48]{0,2,1:T(8,128)(2,1)} %copy-done.9) | copy-start | bytes 294916
  54.1 25.0 %collective-permute-start = (bf16[1024,194]{0,1:T(8,128)(2,1)S(1)}, bf16[1024,194]{0,1:T(8,128)(2,1)S(1)}, u32[]{:S(2)}, u32[]{:S(2)}) collective-permute-start(bf16[1024,194]{0,1:T(8,128)(2,1)S(1)} %copy.89), channel_id=1, source_target_pairs={{0,32},{32,64},{64,96},{96,128},{128,160},{160,192},{192,224},{224... | collective-permute-start | bytes 1191944 | tf_op jit(solution)/shard_map/while/body/eval_jaxpr/ppermute | solution.py:21
  79.1 37.3 %collective-permute-start = (bf16[1024,194]{0,1:T(8,128)(2,1)S(1)}, bf16[1024,194]{0,1:T(8,128)(2,1)S(1)}, u32[]{:S(2)}, u32[]{:S(2)}) collective-permute-start(bf16[1024,194]{0,1:T(8,128)(2,1)S(1)} %copy.89), channel_id=1, source_target_pairs={{0,32},{32,64},{64,96},{96,128},{128,160},{160,192},{192,224},{224... | collective-permute-start | bytes 1191944 | tf_op jit(solution)/shard_map/while/body/eval_jaxpr/ppermute | solution.py:21
  116.4 27.8 %collective-permute-start = (bf16[1024,194]{0,1:T(8,128)(2,1)S(1)}, bf16[1024,194]{0,1:T(8,128)(2,1)S(1)}, u32[]{:S(2)}, u32[]{:S(2)}) collective-permute-start(bf16[1024,194]{0,1:T(8,128)(2,1)S(1)} %copy.89), channel_id=1, source_target_pairs={{0,32},{32,64},{64,96},{96,128},{128,160},{160,192},{192,224},{224... | collective-permute-start | bytes 1191944 | tf_op jit(solution)/shard_map/while/body/eval_jaxpr/ppermute | solution.py:21
  144.3 34.0 %collective-permute-start = (bf16[1024,194]{0,1:T(8,128)(2,1)S(1)}, bf16[1024,194]{0,1:T(8,128)(2,1)S(1)}, u32[]{:S(2)}, u32[]{:S(2)}) collective-permute-start(bf16[1024,194]{0,1:T(8,128)(2,1)S(1)} %copy.89), channel_id=1, source_target_pairs={{0,32},{32,64},{64,96},{96,128},{128,160},{160,192},{192,224},{224... | collective-permute-start | bytes 1191944 | tf_op jit(solution)/shard_map/while/body/eval_jaxpr/ppermute | solution.py:21
  178.3 30.0 %collective-permute-start = (bf16[1024,194]{0,1:T(8,128)(2,1)S(1)}, bf16[1024,194]{0,1:T(8,128)(2,1)S(1)}, u32[]{:S(2)}, u32[]{:S(2)}) collective-permute-start(bf16[1024,194]{0,1:T(8,128)(2,1)S(1)} %copy.89), channel_id=1, source_target_pairs={{0,32},{32,64},{64,96},{96,128},{128,160},{160,192},{192,224},{224... | collective-permute-start | bytes 1191944 | tf_op jit(solution)/shard_map/while/body/eval_jaxpr/ppermute | solution.py:21
  208.3 21.3 %collective-permute-start = (bf16[1024,194]{0,1:T(8,128)(2,1)S(1)}, bf16[1024,194]{0,1:T(8,128)(2,1)S(1)}, u32[]{:S(2)}, u32[]{:S(2)}) collective-permute-start(bf16[1024,194]{0,1:T(8,128)(2,1)S(1)} %copy.89), channel_id=1, source_target_pairs={{0,32},{32,64},{64,96},{96,128},{128,160},{160,192},{192,224},{224... | collective-permute-start | bytes 1191944 | tf_op jit(solution)/shard_map/while/body/eval_jaxpr/ppermute | solution.py:21
  229.6 18.7 %collective-permute-start = (bf16[1024,194]{0,1:T(8,128)(2,1)S(1)}, bf16[1024,194]{0,1:T(8,128)(2,1)S(1)}, u32[]{:S(2)}, u32[]{:S(2)}) collective-permute-start(bf16[1024,194]{0,1:T(8,128)(2,1)S(1)} %copy.89), channel_id=1, source_target_pairs={{0,32},{32,64},{64,96},{96,128},{128,160},{160,192},{192,224},{224... | collective-permute-start | bytes 1191944 | tf_op jit(solution)/shard_map/while/body/eval_jaxpr/ppermute | solution.py:21
  259.4 6.8 %copy-start.7 = (bf16[256,384]{1,0:T(8,128)(2,1)S(1)}, bf16[256,384]{1,0:T(8,128)(2,1)}, u32[]{:S(2)}) copy-start(bf16[256,384]{1,0:T(8,128)(2,1)} %param.13) | copy-start | bytes 589828
  259.4 6.8 %copy-start.12 = (bf16[256]{0:T(256)(128)(2,1)S(1)}, bf16[256]{0:T(256)(128)(2,1)}, u32[]{:S(2)}) copy-start(bf16[256]{0:T(256)(128)(2,1)} %get-tuple-element.384) | copy-start | bytes 1540
  260.4 6.1 %copy-start.15 = (bf16[384]{0:T(512)(128)(2,1)S(1)}, bf16[384]{0:T(512)(128)(2,1)}, u32[]{:S(2)}) copy-start(bf16[384]{0:T(512)(128)(2,1)} %param.16) | copy-start | bytes 2308
  260.4 6.1 %copy-start.18 = (s32[2]{0:T(128)S(1)}, s32[2]{0:T(128)}, u32[]{:S(2)}) copy-start(s32[2]{0:T(128)} %param.19) | copy-start | bytes 28
  260.4 6.4 %copy-start.17 = (s32[32]{0:T(128)S(1)}, s32[32]{0:T(128)}, u32[]{:S(2)}) copy-start(s32[32]{0:T(128)} %copy-done.16) | copy-start | bytes 388
  260.4 6.4 %copy-start.14 = (s32[256]{0:T(256)S(1)}, s32[256]{0:T(256)}, u32[]{:S(2)}) copy-start(s32[256]{0:T(256)} %param.17) | copy-start | bytes 3076
  260.4 6.7 %copy-start.3 = (f32[256,4,96]{0,2,1:T(8,128)S(1)}, f32[256,4,96]{0,2,1:T(8,128)}, u32[]{:S(2)}) copy-start(f32[256,4,96]{0,2,1:T(8,128)} %copy-done.2) | copy-start | bytes 1179652
  261.8 27.7 %copy-start.11 = (bf16[256,384]{1,0:T(8,128)(2,1)S(1)}, bf16[256,384]{1,0:T(8,128)(2,1)}, u32[]{:S(2)}) copy-start(bf16[256,384]{1,0:T(8,128)(2,1)} %param.14) | copy-start | bytes 589828
  261.8 26.0 %all-to-all-start.2 = ((bf16[8,256,384]{2,1,0:T(8,128)(2,1)}), bf16[8,256,384]{2,1,0:T(8,128)(2,1)}, u32[]{:S(2)}, u32[]{:S(2)}) async-start(bf16[8,256,384]{2,1,0:T(8,128)(2,1)} %bitcast.57), calls=%async_computation.2 | async-start | bytes 3145728 | tf_op jit(solution)/shard_map/all_to_all | solution.py:169
  289.6 11.0 %copy-start.8 = (bf16[256,384]{1,0:T(8,128)(2,1)}, bf16[256,384]{1,0:T(8,128)(2,1)S(1)}, u32[]{:S(2)}) copy-start(bf16[256,384]{1,0:T(8,128)(2,1)S(1)} %get-tuple-element.368) | copy-start | bytes 589828
  290.3 9.5 %all-to-all-start.3 = ((f32[8,1,256]{2,1,0:T(1,128)}), f32[8,1,256]{2,1,0:T(1,128)S(1)}, u32[]{:S(2)}, u32[]{:S(2)}) async-start(f32[8,1,256]{2,1,0:T(1,128)} %broadcast_in_dim.164), calls=%async_computation.3 | async-start | bytes 16384 | tf_op jit(solution)/shard_map/all_to_all | solution.py:175
  (13 other events, 26.6 us)
